TPU v7x, 128 devices: a whole 4x4x4 slice. The times are simulated.
128 devices in a mesh: gx: 16 (over x, y), gy: 8 (over z, core).
Axes of the slice: x: 4, y: 4, z: 4, core: 2. Of those that a mesh axis runs over, the one named last changes fastest.
Arguments:
- start_block: float32 [8, 8, 1024, 1024], P(None, None, 'gx', 'gy'), may hold values from -120 to 120
- conductivity: float32 [8, 1024, 1024], P(None, 'gx', 'gy'), may hold values from 0.5 to 2
- reaction: float32 [8, 1024, 1024], P(None, 'gx', 'gy'), may hold values from 0.5 to 2
Outputs:
- basis: float32 [40, 8, 1024, 1024], P(None, None, 'gx', 'gy')
- r_factor: float32 [40, 40], replicated
- first_factor: float32 [40, 40], replicated
All inputs are finite; a program needn't handle non-finite values.
Results may differ from a plain program's by a relative error of at most 0.00045.
Values sent between devices are 32-bit elements; how exact they have to be, the bound alone decides.
No kernel may reach another device: no remote copies, remote signals or barrier semaphores. Data moves between devices by JAX's collectives and lax.ppermute only.
A program may use at most 128 MiB of HBM per device.

v0:
```python
import jax
import jax.numpy as jnp
from jax import lax
from jax.sharding import PartitionSpec as P
from jax.experimental import pallas as pl
from jax.experimental.pallas import tpu as pltpu

STEPS = 4
COLS = 40


center_shift = 7.0
step_scale = 1.0 / 3.0


HALO = 4
LANES = 256


def edge_rows(start_block, conductivity, reaction, lo, hi):
    rhs, depth, rows, cols = start_block.shape
    return jnp.concatenate(
        [
            start_block[:, :, lo:hi].reshape(rhs * depth, hi - lo, cols),
            conductivity[:, lo:hi],
            reaction[:, lo:hi],
        ],
        axis=0,
    )


def shift_pairs(axis):
    count = lax.axis_size(axis)
    to_next = [(i, (i + 1) % count) for i in range(count)]
    return (to_next, [(j, i) for i, j in to_next])


def tall_plane(core, from_next, from_prev):
    return jnp.concatenate([core, from_next, from_prev], axis=0)


def columns_kernel(block_ref, coef_ref, react_ref, xn_ref, xp_ref, first_ref, last_ref):
    rhs, depth, rows, cols = block_ref.shape
    width = xn_ref.shape[1]
    fill = jnp.zeros((cols - rows - 2 * width, cols), jnp.float32)

    def one(plane, core):
        tall = tall_plane(core, xn_ref[plane], xp_ref[plane])
        turned = jnp.concatenate([tall, fill], axis=0).T
        first_ref[plane] = turned[:width]
        last_ref[plane] = turned[cols - width :]

    def block_plane(p, carry):
        one(p, block_ref[p // depth, p % depth])
        return carry

    def coef_plane(z, carry):
        one(rhs * depth + z, coef_ref[z])
        one(rhs * depth + depth + z, react_ref[z])
        return carry

    lax.fori_loop(0, rhs * depth, block_plane, 0)
    lax.fori_loop(0, depth, coef_plane, 0)


def edge_columns(start_block, conductivity, reaction, x_next, x_prev):
    planes, width, cols = x_next.shape
    whole = lambda shape: pl.BlockSpec(shape, lambda: (0,) * len(shape))
    strip = jax.ShapeDtypeStruct((planes, width, cols), jnp.float32)
    return pl.pallas_call(
        columns_kernel,
        in_specs=[
            whole(start_block.shape),
            whole(conductivity.shape),
            whole(reaction.shape),
            whole(x_next.shape),
            whole(x_prev.shape),
        ],
        out_specs=[whole(strip.shape), whole(strip.shape)],
        out_shape=[strip, strip],
    )(start_block, conductivity, reaction, x_next, x_prev)


def halo_strips(start_block, conductivity, reaction):
    rows = start_block.shape[2]
    x_next_pairs, x_prev_pairs = shift_pairs("gx")
    first = edge_rows(start_block, conductivity, reaction, 0, HALO)
    last = edge_rows(start_block, conductivity, reaction, rows - HALO, rows)
    x_next = lax.ppermute(first, "gx", x_prev_pairs)
    x_prev = lax.ppermute(last, "gx", x_next_pairs)
    first, last = edge_columns(start_block, conductivity, reaction, x_next, x_prev)
    y_next_pairs, y_prev_pairs = shift_pairs("gy")
    y_next = lax.ppermute(first, "gy", y_prev_pairs)
    y_prev = lax.ppermute(last, "gy", y_next_pairs)
    return (x_next, x_prev, y_next, y_prev)


def padded_plane(core, xn, xp, yn, yp):
    cols = core.shape[-1]
    width = yn.shape[0]
    tall = tall_plane(core, xn, xp)
    gap = jnp.zeros((cols - 2 * width, cols), jnp.float32)
    side = jnp.concatenate([yn, gap, yp], axis=0).T[: tall.shape[0]]
    return jnp.concatenate([tall, side], axis=1)


def tree_sum(value, axes):
    for axis in axes:
        count = lax.axis_size(axis)
        stride = 1
        while stride < count:
            pairs = [(i, i ^ stride) for i in range(count)]
            value = value + lax.ppermute(value, axis, pairs)
            stride *= 2
    return value


def neighbour(value, direction):
    axis, offset = direction
    if axis == 0:
        count = value.shape[0]
        cut = offset % count
        return jnp.concatenate([value[cut:], value[:cut]], axis=0)
    return pltpu.roll(value, (-offset) % value.shape[axis], axis)


DIRECTIONS = ((1, 1), (1, -1), (2, 1), (2, -1), (0, 1), (0, -1))


def powers_kernel(*refs):
    block_ref, coef_ref, react_ref = refs[:3]
    strips = refs[3:15]
    out_ref, weight_ref, react_pad_ref = refs[15:]
    depth, rows, cols = (out_ref.shape[2], out_ref.shape[3], out_ref.shape[4])

    def planes(core_of, group):
        sides = [strips[4 * group + k] for k in range(4)]
        return jnp.stack(
            [padded_plane(core_of(z), *(side[z] for side in sides)) for z in range(depth)], axis=0
        )

    @pl.when(pl.program_id(0) == 0)
    def _():
        coef = planes(lambda z: coef_ref[z], 1)
        for d, direction in enumerate(DIRECTIONS):
            weight_ref[d] = 0.5 * (coef + neighbour(coef, direction))
        react_pad_ref[...] = planes(lambda z: react_ref[z], 2)

    out_ref[0, 0] = block_ref[0]
    current = planes(lambda z: block_ref[0, z], 0)
    react = react_pad_ref[...]
    for power in range(1, STEPS + 1):
        running = jnp.zeros_like(current)
        for d, direction in enumerate(DIRECTIONS):
            beside = neighbour(current, direction)
            running = running + weight_ref[d] * (current - beside)
        current = (react * current + running - center_shift * current) * step_scale
        out_ref[power, 0] = current[:, :rows, :cols]


def krylov_powers(start_block, conductivity, reaction, strips):
    rhs, depth, rows, cols = start_block.shape
    width = strips[0].shape[1]
    strip_specs = []
    for group in (lambda r: r, lambda r: rhs, lambda r: rhs + 1):
        for _ in strips:
            strip_specs.append(pl.BlockSpec((depth, width, cols), lambda r, g=group: (g(r), 0, 0)))
    return pl.pallas_call(
        powers_kernel,
        grid=(rhs,),
        in_specs=[
            pl.BlockSpec((1, depth, rows, cols), lambda r: (r, 0, 0, 0)),
            pl.BlockSpec((depth, rows, cols), lambda r: (0, 0, 0)),
            pl.BlockSpec((depth, rows, cols), lambda r: (0, 0, 0)),
        ]
        + strip_specs,
        out_specs=pl.BlockSpec((STEPS + 1, 1, depth, rows, cols), lambda r: (0, r, 0, 0, 0)),
        out_shape=jax.ShapeDtypeStruct((STEPS + 1, rhs, depth, rows, cols), jnp.float32),
        scratch_shapes=[
            pltpu.VMEM((len(DIRECTIONS), depth, rows + 2 * width, LANES), jnp.float32),
            pltpu.VMEM((depth, rows + 2 * width, LANES), jnp.float32),
        ],
        compiler_params=pltpu.CompilerParams(dimension_semantics=("arbitrary",)),
    )(start_block, conductivity, reaction, *(strips * 3))


def body(start_block, conductivity, reaction):
    cells_total = (
        start_block.shape[1]
        * start_block.shape[2]
        * start_block.shape[3]
        * lax.axis_size("gx")
        * lax.axis_size("gy")
    )
    rhs, depth, rows, cols = start_block.shape
    strips = halo_strips(start_block, conductivity, reaction)
    krylov = krylov_powers(start_block, conductivity, reaction, strips).reshape(COLS, -1)
    local_gram = jnp.dot(
        krylov, krylov.T, precision=lax.Precision.HIGHEST, preferred_element_type=jnp.float32
    )
    gram_first = tree_sum(local_gram, ("gx", "gy"))
    gram_first = gram_first / cells_total
    lower_first = jnp.linalg.cholesky(gram_first)
    first_q = jax.scipy.linalg.solve_triangular(lower_first, krylov, lower=True)
    local_again = jnp.dot(
        first_q, first_q.T, precision=lax.Precision.HIGHEST, preferred_element_type=jnp.float32
    )
    gram_second = tree_sum(local_again, ("gx", "gy")) / cells_total
    lower_second = jnp.linalg.cholesky(gram_second)
    basis = jax.scipy.linalg.solve_triangular(lower_second, first_q, lower=True)
    r_factor = jnp.dot(
        lower_second.T,
        lower_first.T,
        precision=lax.Precision.HIGHEST,
        preferred_element_type=jnp.float32,
    )
    return (
        basis.reshape(COLS, start_block.shape[1], start_block.shape[2], start_block.shape[3]),
        r_factor,
        lower_first.T,
    )


def solution(mesh):
    return jax.shard_map(
        body,
        mesh=mesh,
        in_specs=(P(None, None, "gx", "gy"), P(None, "gx", "gy"), P(None, "gx", "gy")),
        out_specs=(P(None, None, "gx", "gy"), P(), P()),
        check_vma=False,
    )
```

profile of v0, /device:TPU:0, one launch (start us, length us, event | category | flops | bytes accessed | tf_op | source)
XLA Modules:
  0.0 193.7 jit_solution(6837071247779822769)
XLA Ops:
  2.6 5.4 %collective-permute-start = (f32[80,4,128]{2,1,0:T(4,128)S(1)}, f32[80,4,128]{2,1,0:T(4,128)S(1)}, u32[]{:S(2)}, u32[]{:S(2)}) collective-permute-start(f32[80,4,128]{2,1,0:T(4,128)S(1)} %pad_maximum_fusion), channel_id=1, source_target_pairs={{8,0},{16,8},{24,16},{32,24},{40,32},{48,40},{56,48},{64,56},{72,6... | collective-permute-start | bytes 491528 | tf_op jit(solution)/shard_map/ppermute | solution.py:89
  8.1 3.3 %collective-permute-done.xn_ref.refs_3_.refs_7_.refs_11_ = f32[80,4,128]{2,1,0:T(4,128)S(1)} collective-permute-done((f32[80,4,128]{2,1,0:T(4,128)S(1)}, f32[80,4,128]{2,1,0:T(4,128)S(1)}, u32[]{:S(2)}, u32[]{:S(2)}) %collective-permute-start) | collective-permute-done | bytes 163872 | tf_op jit(solution)/shard_map/ppermute | solution.py:89
  11.4 5.6 %collective-permute-done.1.xp_ref.refs_4_.refs_8_.refs_12_ = f32[80,4,128]{2,1,0:T(4,128)S(1)} collective-permute-done((f32[80,4,128]{2,1,0:T(4,128)S(1)}, f32[80,4,128]{2,1,0:T(4,128)S(1)}, u32[]{:S(2)}, u32[]{:S(2)}) %collective-permute-start.1) | collective-permute-done | bytes 163872 | tf_op jit(solution)/shard_map/ppermute | solution.py:90
  17.7 9.8 %shard_map.58 = (f32[80,4,128]{2,1,0:T(4,128)}, f32[80,4,128]{2,1,0:T(4,128)}) custom-call(f32[8,8,64,128]{3,2,1,0:T(8,128)} %refs_0_.1, f32[8,64,128]{2,1,0:T(8,128)} %refs_1_.1, f32[8,64,128]{2,1,0:T(8,128)} %refs_2_.1, f32[80,4,128]{2,1,0:T(4,128)} %copy-done.1, f32[80,4,128]{2,1,0:T(4,128)} %copy-done.2), custom_call_target="tpu_custom_call" | custom-call | tf_op jit(solution)/shard_map/pallas_call | solution.py:70
  27.6 2.3 %collective-permute-start.2 = (f32[80,4,128]{2,1,0:T(4,128)}, f32[80,4,128]{2,1,0:T(4,128)S(1)}, u32[]{:S(2)}, u32[]{:S(2)}) collective-permute-start(f32[80,4,128]{2,1,0:T(4,128)} %get-tuple-element.7), channel_id=1, source_target_pairs={{1,0},{2,1},{3,2},{4,3},{5,4},{6,5},{7,6},{0,7},{9,8},{10,9},{11,1... | collective-permute-start | bytes 491528 | tf_op jit(solution)/shard_map/ppermute | solution.py:93
  29.8 3.1 %collective-permute-done.2.refs_5_.refs_9_.refs_13_ = f32[80,4,128]{2,1,0:T(4,128)S(1)} collective-permute-done((f32[80,4,128]{2,1,0:T(4,128)}, f32[80,4,128]{2,1,0:T(4,128)S(1)}, u32[]{:S(2)}, u32[]{:S(2)}) %collective-permute-start.2) | collective-permute-done | bytes 163872 | tf_op jit(solution)/shard_map/ppermute | solution.py:93
  33.0 3.0 %collective-permute-done.3.refs_6_.refs_10_.refs_14_ = f32[80,4,128]{2,1,0:T(4,128)S(1)} collective-permute-done((f32[80,4,128]{2,1,0:T(4,128)}, f32[80,4,128]{2,1,0:T(4,128)S(1)}, u32[]{:S(2)}, u32[]{:S(2)}) %collective-permute-start.3) | collective-permute-done | bytes 163872 | tf_op jit(solution)/shard_map/ppermute | solution.py:94
  36.7 21.2 %shard_map.59 = f32[5,8,8,64,128]{4,3,2,1,0:T(8,128)} custom-call(f32[8,8,64,128]{3,2,1,0:T(8,128)} %refs_0_.1, f32[8,64,128]{2,1,0:T(8,128)} %refs_1_.1, f32[8,64,128]{2,1,0:T(8,128)} %refs_2_.1, f32[80,4,128]{2,1,0:T(4,128)} %copy-done.1, f32[80,4,128]{2,1,0:T(4,128)} %copy-done.2, f32[80,4,128]{2,1,0:T(4,128)} %copy-done.3, f32[80,4,128]{2,1,0:T(4,128)} %copy-done.4, ...), custom_call_target="tpu_custom_call" | custom-call | tf_op jit(solution)/shard_map/pallas_call | solution.py:168
  57.9 10.4 %reshape.28 = f32[40,65536]{1,0:T(8,128)} reshape(f32[5,8,8,64,128]{4,3,2,1,0:T(8,128)} %shard_map.59) | data formatting | bytes 20971520 | tf_op jit(solution)/shard_map/reshape | solution.py:197
  68.3 11.8 %fusion.24 = f32[40,40]{0,1:T(8,128)S(1)} fusion(f32[40,65536]{1,0:T(8,128)} %reshape.28), kind=kOutput, calls=%fused_computation.35 | convolution fusion | flops 1258291200 | bytes 10492160 | tf_op jit(solution)/shard_map/dot_general | solution.py:198
  80.2 3.8 %collective-permute-done.4 = f32[40,40]{0,1:T(8,128)S(1)} collective-permute-done((f32[40,40]{0,1:T(8,128)S(1)}, f32[40,40]{0,1:T(8,128)S(1)}, u32[]{:S(2)}, u32[]{:S(2)}) %collective-permute-start.4) | collective-permute-done | bytes 6432 | tf_op jit(solution)/shard_map/ppermute | solution.py:113
  84.0 5.3 %collective-permute-done.5 = f32[40,40]{0,1:T(8,128)S(1)} collective-permute-done((f32[40,40]{0,1:T(8,128)S(1)}, f32[40,40]{0,1:T(8,128)S(1)}, u32[]{:S(2)}, u32[]{:S(2)}) %collective-permute-start.5) | collective-permute-done | bytes 6432 | tf_op jit(solution)/shard_map/ppermute | solution.py:113
  89.3 3.8 %collective-permute-done.6 = f32[40,40]{0,1:T(8,128)S(1)} collective-permute-done((f32[40,40]{0,1:T(8,128)S(1)}, f32[40,40]{0,1:T(8,128)S(1)}, u32[]{:S(2)}, u32[]{:S(2)}) %collective-permute-start.6) | collective-permute-done | bytes 6432 | tf_op jit(solution)/shard_map/ppermute | solution.py:113
  93.1 5.3 %collective-permute-done.7 = f32[40,40]{0,1:T(8,128)S(1)} collective-permute-done((f32[40,40]{0,1:T(8,128)S(1)}, f32[40,40]{0,1:T(8,128)S(1)}, u32[]{:S(2)}, u32[]{:S(2)}) %collective-permute-start.7) | collective-permute-done | bytes 6432 | tf_op jit(solution)/shard_map/ppermute | solution.py:113
  98.4 1.2 collective-permute-done.8
  99.6 3.8 %collective-permute-done.9 = f32[40,40]{0,1:T(8,128)S(1)} collective-permute-done((f32[40,40]{0,1:T(8,128)S(1)}, f32[40,40]{0,1:T(8,128)S(1)}, u32[]{:S(2)}, u32[]{:S(2)}) %collective-permute-start.9) | collective-permute-done | bytes 6432 | tf_op jit(solution)/shard_map/ppermute | solution.py:113
  103.8 4.9 %collective-permute-done.10 = f32[40,40]{0,1:T(8,128)S(1)} collective-permute-done((f32[40,40]{0,1:T(8,128)S(1)}, f32[40,40]{0,1:T(8,128)S(1)}, u32[]{:S(2)}, u32[]{:S(2)}) %collective-permute-start.10) | collective-permute-done | bytes 6432 | tf_op jit(solution)/shard_map/ppermute | solution.py:113
  108.8 3.6 %cholesky.44 = f32[40,40]{1,0:T(8,128)S(1)} custom-call(f32[40,40]{1,0:T(8,128)S(1)} %fusion.4), custom_call_target="Cholesky" | custom-call | tf_op jit(solution)/shard_map/jit(cholesky)/cholesky | solution.py:203
  113.8 3.1 %custom-call.6 = f32[1,40,40]{1,2,0:T(8,128)S(1)} custom-call(f32[1,40,40]{2,1,0:T(8,128)S(1)} %get-tuple-element.19), custom_call_target="InvertDiagBlocksLowerTriangular" | custom-call | tf_op jit(solution)/shard_map/jit(_solve_triangular)/triangular_solve | solution.py:204
  116.8 11.9 %fusion.2 = f32[40,65536]{1,0:T(8,128)S(1)} fusion(f32[40,65536]{1,0:T(8,128)} %reshape.28, f32[1,40,40]{1,2,0:T(8,128)S(1)} %custom-call.6), kind=kOutput, calls=%fused_computation.6 | convolution fusion | flops 1258291200 | bytes 20977920 | tf_op jit(solution)/shard_map/jit(_solve_triangular)/triangular_solve | solution.py:204
  128.7 8.2 %fusion.25 = f32[40,40]{0,1:T(8,128)S(1)} fusion(f32[40,65536]{1,0:T(8,128)S(1)} %fusion.2), kind=kOutput, calls=%fused_computation.36 | convolution fusion | flops 1258291200 | bytes 10492160 | tf_op jit(solution)/shard_map/dot_general | solution.py:205
  137.1 3.8 %collective-permute-done.11 = f32[40,40]{0,1:T(8,128)S(1)} collective-permute-done((f32[40,40]{0,1:T(8,128)S(1)}, f32[40,40]{0,1:T(8,128)S(1)}, u32[]{:S(2)}, u32[]{:S(2)}) %collective-permute-start.11) | collective-permute-done | bytes 6432 | tf_op jit(solution)/shard_map/ppermute | solution.py:113
  140.9 5.3 %collective-permute-done.12 = f32[40,40]{0,1:T(8,128)S(1)} collective-permute-done((f32[40,40]{0,1:T(8,128)S(1)}, f32[40,40]{0,1:T(8,128)S(1)}, u32[]{:S(2)}, u32[]{:S(2)}) %collective-permute-start.12) | collective-permute-done | bytes 6432 | tf_op jit(solution)/shard_map/ppermute | solution.py:113
  146.2 3.8 %collective-permute-done.13 = f32[40,40]{0,1:T(8,128)S(1)} collective-permute-done((f32[40,40]{0,1:T(8,128)S(1)}, f32[40,40]{0,1:T(8,128)S(1)}, u32[]{:S(2)}, u32[]{:S(2)}) %collective-permute-start.13) | collective-permute-done | bytes 6432 | tf_op jit(solution)/shard_map/ppermute | solution.py:113
  150.0 5.3 %collective-permute-done.14 = f32[40,40]{0,1:T(8,128)S(1)} collective-permute-done((f32[40,40]{0,1:T(8,128)S(1)}, f32[40,40]{0,1:T(8,128)S(1)}, u32[]{:S(2)}, u32[]{:S(2)}) %collective-permute-start.14) | collective-permute-done | bytes 6432 | tf_op jit(solution)/shard_map/ppermute | solution.py:113
  156.4 3.8 %collective-permute-done.16 = f32[40,40]{0,1:T(8,128)S(1)} collective-permute-done((f32[40,40]{0,1:T(8,128)S(1)}, f32[40,40]{0,1:T(8,128)S(1)}, u32[]{:S(2)}, u32[]{:S(2)}) %collective-permute-start.16) | collective-permute-done | bytes 6432 | tf_op jit(solution)/shard_map/ppermute | solution.py:113
  161.3 4.2 %collective-permute-done.17 = f32[40,40]{0,1:T(8,128)S(1)} collective-permute-done((f32[40,40]{0,1:T(8,128)S(1)}, f32[40,40]{0,1:T(8,128)S(1)}, u32[]{:S(2)}, u32[]{:S(2)}) %collective-permute-start.17) | collective-permute-done | bytes 6432 | tf_op jit(solution)/shard_map/ppermute | solution.py:113
  165.6 3.6 %cholesky.55 = f32[40,40]{1,0:T(8,128)S(1)} custom-call(f32[40,40]{1,0:T(8,128)S(1)} %fusion.1), custom_call_target="Cholesky" | custom-call | tf_op jit(solution)/shard_map/jit(cholesky)/cholesky | solution.py:209
  170.0 2.1 %fusion.11 = f32[40,40]{1,0:T(8,128)} fusion(f32[40,40]{1,0:T(8,128)S(1)} %cholesky.55, f32[40,40]{1,0:T(8,128)S(1)} %cholesky.44, pred[]{:T(512)} %compare_reduce_fusion, pred[]{:T(512)} %compare_reduce_fusion.1), kind=kOutput, calls=%fused_computation.22 | convolution fusion | flops 777600 | bytes 19202 | tf_op jit(solution)/shard_map/dot_general | solution.py:211
  172.7 3.1 %custom-call.7 = f32[1,40,40]{1,2,0:T(8,128)S(1)} custom-call(f32[1,40,40]{2,1,0:T(8,128)S(1)} %select_bitcast_fusion), custom_call_target="InvertDiagBlocksLowerTriangular" | custom-call | tf_op jit(solution)/shard_map/jit(_solve_triangular)/triangular_solve | solution.py:210
  175.8 11.9 %convolution_bitcast_fusion = f32[5,8,512,128]{3,1,2,0:T(8,128)S(1)} fusion(f32[40,65536]{1,0:T(8,128)} %copy-done, f32[1,40,40]{1,2,0:T(8,128)S(1)} %custom-call.7), kind=kOutput, calls=%fused_computation | convolution fusion | flops 1258291200 | bytes 20977920 | tf_op jit(solution)/shard_map/jit(_solve_triangular)/triangular_solve | solution.py:210
  187.7 6.0 %copy.15 = f32[5,8,512,128]{3,2,1,0:T(8,128)} copy(f32[5,8,512,128]{3,1,2,0:T(8,128)S(1)} %convolution_bitcast_fusion) | data formatting | bytes 20971520
  (56 shorter events, 9.2 us)
Async XLA Ops:
  2.6 8.8 %collective-permute-start = (f32[80,4,128]{2,1,0:T(4,128)S(1)}, f32[80,4,128]{2,1,0:T(4,128)S(1)}, u32[]{:S(2)}, u32[]{:S(2)}) collective-permute-start(f32[80,4,128]{2,1,0:T(4,128)S(1)} %pad_maximum_fusion), channel_id=1, source_target_pairs={{8,0},{16,8},{24,16},{32,24},{40,32},{48,40},{56,48},{64,56},{72,6... | collective-permute-start | bytes 491528 | tf_op jit(solution)/shard_map/ppermute | solution.py:89
  8.0 9.0 %collective-permute-start.1 = (f32[80,4,128]{2,1,0:T(4,128)S(1)}, f32[80,4,128]{2,1,0:T(4,128)S(1)}, u32[]{:S(2)}, u32[]{:S(2)}) collective-permute-start(f32[80,4,128]{2,1,0:T(4,128)S(1)} %pad_maximum_fusion.1), channel_id=1, source_target_pairs={{0,8},{8,16},{16,24},{24,32},{32,40},{40,48},{48,56},{56,64},{64,7... | collective-permute-start | bytes 491528 | tf_op jit(solution)/shard_map/ppermute | solution.py:90
  11.4 5.6 %copy-start.1 = (f32[80,4,128]{2,1,0:T(4,128)}, f32[80,4,128]{2,1,0:T(4,128)S(1)}, u32[]{:S(2)}) copy-start(f32[80,4,128]{2,1,0:T(4,128)S(1)} %collective-permute-done.xn_ref.refs_3_.refs_7_.refs_11_) | copy-start | bytes 491524
  17.0 0.7 copy-start.2
  27.6 5.4 %collective-permute-start.2 = (f32[80,4,128]{2,1,0:T(4,128)}, f32[80,4,128]{2,1,0:T(4,128)S(1)}, u32[]{:S(2)}, u32[]{:S(2)}) collective-permute-start(f32[80,4,128]{2,1,0:T(4,128)} %get-tuple-element.7), channel_id=1, source_target_pairs={{1,0},{2,1},{3,2},{4,3},{5,4},{6,5},{7,6},{0,7},{9,8},{10,9},{11,1... | collective-permute-start | bytes 491528 | tf_op jit(solution)/shard_map/ppermute | solution.py:93
  29.8 6.2 %collective-permute-start.3 = (f32[80,4,128]{2,1,0:T(4,128)}, f32[80,4,128]{2,1,0:T(4,128)S(1)}, u32[]{:S(2)}, u32[]{:S(2)}) collective-permute-start(f32[80,4,128]{2,1,0:T(4,128)} %get-tuple-element.8), channel_id=1, source_target_pairs={{0,1},{1,2},{2,3},{3,4},{4,5},{5,6},{6,7},{7,0},{8,9},{9,10},{10,1... | collective-permute-start | bytes 491528 | tf_op jit(solution)/shard_map/ppermute | solution.py:94
  33.0 3.0 %copy-start.3 = (f32[80,4,128]{2,1,0:T(4,128)}, f32[80,4,128]{2,1,0:T(4,128)S(1)}, u32[]{:S(2)}) copy-start(f32[80,4,128]{2,1,0:T(4,128)S(1)} %collective-permute-done.2.refs_5_.refs_9_.refs_13_) | copy-start | bytes 491524
  36.0 0.7 copy-start.4
  80.1 3.9 %collective-permute-start.4 = (f32[40,40]{0,1:T(8,128)S(1)}, f32[40,40]{0,1:T(8,128)S(1)}, u32[]{:S(2)}, u32[]{:S(2)}) collective-permute-start(f32[40,40]{0,1:T(8,128)S(1)} %fusion.24), channel_id=1, source_target_pairs={{0,8},{8,0},{16,24},{24,16},{32,40},{40,32},{48,56},{56,48},{64,72... | collective-permute-start | bytes 19208 | tf_op jit(solution)/shard_map/ppermute | solution.py:113
  84.0 5.3 %collective-permute-start.5 = (f32[40,40]{0,1:T(8,128)S(1)}, f32[40,40]{0,1:T(8,128)S(1)}, u32[]{:S(2)}, u32[]{:S(2)}) collective-permute-start(f32[40,40]{0,1:T(8,128)S(1)} %add.51), channel_id=1, source_target_pairs={{0,16},{8,24},{16,0},{24,8},{32,48},{40,56},{48,32},{56,40},{64,80... | collective-permute-start | bytes 19208 | tf_op jit(solution)/shard_map/ppermute | solution.py:113
  89.3 3.8 %collective-permute-start.6 = (f32[40,40]{0,1:T(8,128)S(1)}, f32[40,40]{0,1:T(8,128)S(1)}, u32[]{:S(2)}, u32[]{:S(2)}) collective-permute-start(f32[40,40]{0,1:T(8,128)S(1)} %add.52), channel_id=1, source_target_pairs={{0,32},{8,40},{16,48},{24,56},{32,0},{40,8},{48,16},{56,24},{64,96... | collective-permute-start | bytes 19208 | tf_op jit(solution)/shard_map/ppermute | solution.py:113
  93.1 5.3 %collective-permute-start.7 = (f32[40,40]{0,1:T(8,128)S(1)}, f32[40,40]{0,1:T(8,128)S(1)}, u32[]{:S(2)}, u32[]{:S(2)}) collective-permute-start(f32[40,40]{0,1:T(8,128)S(1)} %add.53), channel_id=1, source_target_pairs={{0,64},{8,72},{16,80},{24,88},{32,96},{40,104},{48,112},{56,120},{... | collective-permute-start | bytes 19208 | tf_op jit(solution)/shard_map/ppermute | solution.py:113
  98.4 1.2 collective-permute-start.8
  99.6 3.8 %collective-permute-start.9 = (f32[40,40]{0,1:T(8,128)S(1)}, f32[40,40]{0,1:T(8,128)S(1)}, u32[]{:S(2)}, u32[]{:S(2)}) collective-permute-start(f32[40,40]{0,1:T(8,128)S(1)} %add.55), channel_id=1, source_target_pairs={{0,2},{1,3},{2,0},{3,1},{4,6},{5,7},{6,4},{7,5},{8,10},{9,11},{10,... | collective-permute-start | bytes 19208 | tf_op jit(solution)/shard_map/ppermute | solution.py:113
  103.4 5.3 %collective-permute-start.10 = (f32[40,40]{0,1:T(8,128)S(1)}, f32[40,40]{0,1:T(8,128)S(1)}, u32[]{:S(2)}, u32[]{:S(2)}) collective-permute-start(f32[40,40]{0,1:T(8,128)S(1)} %add.56), channel_id=1, source_target_pairs={{0,4},{1,5},{2,6},{3,7},{4,0},{5,1},{6,2},{7,3},{8,12},{9,13},{10,... | collective-permute-start | bytes 19208 | tf_op jit(solution)/shard_map/ppermute | solution.py:113
  128.7 8.3 %copy-start = (f32[40,65536]{1,0:T(8,128)}, f32[40,65536]{1,0:T(8,128)S(1)}, u32[]{:S(2)}) copy-start(f32[40,65536]{1,0:T(8,128)S(1)} %fusion.2) | copy-start | bytes 31457284
  137.0 3.9 %collective-permute-start.11 = (f32[40,40]{0,1:T(8,128)S(1)}, f32[40,40]{0,1:T(8,128)S(1)}, u32[]{:S(2)}, u32[]{:S(2)}) collective-permute-start(f32[40,40]{0,1:T(8,128)S(1)} %fusion.25), channel_id=1, source_target_pairs={{0,8},{8,0},{16,24},{24,16},{32,40},{40,32},{48,56},{56,48},{64,72... | collective-permute-start | bytes 19208 | tf_op jit(solution)/shard_map/ppermute | solution.py:113
  140.9 5.3 %collective-permute-start.12 = (f32[40,40]{0,1:T(8,128)S(1)}, f32[40,40]{0,1:T(8,128)S(1)}, u32[]{:S(2)}, u32[]{:S(2)}) collective-permute-start(f32[40,40]{0,1:T(8,128)S(1)} %add.58), channel_id=1, source_target_pairs={{0,16},{8,24},{16,0},{24,8},{32,48},{40,56},{48,32},{56,40},{64,80... | collective-permute-start | bytes 19208 | tf_op jit(solution)/shard_map/ppermute | solution.py:113
  146.2 3.8 %collective-permute-start.13 = (f32[40,40]{0,1:T(8,128)S(1)}, f32[40,40]{0,1:T(8,128)S(1)}, u32[]{:S(2)}, u32[]{:S(2)}) collective-permute-start(f32[40,40]{0,1:T(8,128)S(1)} %add.59), channel_id=1, source_target_pairs={{0,32},{8,40},{16,48},{24,56},{32,0},{40,8},{48,16},{56,24},{64,96... | collective-permute-start | bytes 19208 | tf_op jit(solution)/shard_map/ppermute | solution.py:113
  149.9 5.3 %collective-permute-start.14 = (f32[40,40]{0,1:T(8,128)S(1)}, f32[40,40]{0,1:T(8,128)S(1)}, u32[]{:S(2)}, u32[]{:S(2)}) collective-permute-start(f32[40,40]{0,1:T(8,128)S(1)} %add.60), channel_id=1, source_target_pairs={{0,64},{8,72},{16,80},{24,88},{32,96},{40,104},{48,112},{56,120},{... | collective-permute-start | bytes 19208 | tf_op jit(solution)/shard_map/ppermute | solution.py:113
  155.2 1.2 collective-permute-start.15
  156.4 3.8 %collective-permute-start.16 = (f32[40,40]{0,1:T(8,128)S(1)}, f32[40,40]{0,1:T(8,128)S(1)}, u32[]{:S(2)}, u32[]{:S(2)}) collective-permute-start(f32[40,40]{0,1:T(8,128)S(1)} %add.62), channel_id=1, source_target_pairs={{0,2},{1,3},{2,0},{3,1},{4,6},{5,7},{6,4},{7,5},{8,10},{9,11},{10,... | collective-permute-start | bytes 19208 | tf_op jit(solution)/shard_map/ppermute | solution.py:113
  160.2 5.3 %collective-permute-start.17 = (f32[40,40]{0,1:T(8,128)S(1)}, f32[40,40]{0,1:T(8,128)S(1)}, u32[]{:S(2)}, u32[]{:S(2)}) collective-permute-start(f32[40,40]{0,1:T(8,128)S(1)} %add.63), channel_id=1, source_target_pairs={{0,4},{1,5},{2,6},{3,7},{4,0},{5,1},{6,2},{7,3},{8,12},{9,13},{10,... | collective-permute-start | bytes 19208 | tf_op jit(solution)/shard_map/ppermute | solution.py:113
where the time goes:
time: 194 us
  waiting for transfers between devices  70.3 us (36%)
  matrix products  46 us (24%)
  Pallas kernels  31.1 us (16%)
  local copies, waits for them, and re-layouts  20.5 us (11%)
  other arithmetic  16.3 us (8%)
  starting transfers between devices  8.73 us (4%)
    ppermute x14, waiting for transfers between devices, tree_sum(): value = value + lax.ppermute(value, axis, pairs)  55.2 us
    pallas_call x1, Pallas kernels, krylov_powers(): pl.pallas_call(powers_kernel, grid=(rhs,), in_specs=[pl.BlockSpec((1, dep...  21.2 us
    another operation x1, matrix products, body(): first_q = jax.scipy.linalg.solve_triangular(lower_first, krylov, lower=True)  11.9 us
    another operation x1, matrix products, body(): basis = jax.scipy.linalg.solve_triangular(lower_second, first_q, lower=True)  11.9 us
    dot_general x1, matrix products, body(): jnp.dot(krylov, krylov.T, precision=lax.Precision.HIGHEST, preferred_elem...  11.8 us
    reshape x1, local copies, waits for them, and re-layouts, body(): krylov_powers(start_block, conductivity, reaction, strips).reshape(COLS, -1)  10.4 us
    pallas_call x1, Pallas kernels, edge_columns(): pl.pallas_call(columns_kernel, in_specs=[whole(start_block.shape), whole(...  9.84 us
    dot_general x1, matrix products, body(): jnp.dot(first_q, first_q.T, precision=lax.Precision.HIGHEST, preferred_el...  8.24 us
  transfers between devices with their start and end apart: 18, of which 18 were waited for; matrix products, arithmetic and copies ran while one was open for 0% of the time, Pallas kernels for 0%

commit v1 on v0

--- a/solution.py
+++ b/solution.py
@@ -203,11 +203,14 @@
     lower_first = jnp.linalg.cholesky(gram_first)
     first_q = jax.scipy.linalg.solve_triangular(lower_first, krylov, lower=True)
     local_again = jnp.dot(
-        first_q, first_q.T, precision=lax.Precision.HIGHEST, preferred_element_type=jnp.float32
+        first_q, first_q.T, precision=lax.Precision.HIGH, preferred_element_type=jnp.float32
     )
     gram_second = tree_sum(local_again, ("gx", "gy")) / cells_total
     lower_second = jnp.linalg.cholesky(gram_second)
-    basis = jax.scipy.linalg.solve_triangular(lower_second, first_q, lower=True)
+    inverse = jax.scipy.linalg.solve_triangular(
+        lower_second, jnp.eye(COLS, dtype=jnp.float32), lower=True
+    )
+    basis = jnp.dot(inverse, first_q, precision=lax.Precision.HIGH, preferred_element_type=jnp.float32)
     r_factor = jnp.dot(
         lower_second.T,
         lower_first.T,

time: 194 us -> 185 us (0.954)
  matrix products: 46 us -> 37.2 us
    another operation x1, matrix products: 11.9 us -> 0.23 us  [body(): jax.scipy.linalg.solve_triangular(lower_second, jnp.eye(COLS, dtype=jnp.f...]
    dot_general x1 -> x2, matrix products: 8.24 us -> 11.3 us  [the longest x1 7.14 us: body(): jnp.dot(inverse, first_q, precision=lax.Precision.HIGH, preferred_element...]
where the time goes in v1:
time: 185 us
  waiting for transfers between devices  70.3 us (38%)
  matrix products  37.2 us (20%)
  Pallas kernels  31.1 us (17%)
  local copies, waits for them, and re-layouts  20.5 us (11%)
  other arithmetic  16.3 us (9%)
  starting transfers between devices  8.73 us (5%)
    ppermute x14, waiting for transfers between devices, tree_sum(): value = value + lax.ppermute(value, axis, pairs)  55.2 us
    pallas_call x1, Pallas kernels, krylov_powers(): pl.pallas_call(powers_kernel, grid=(rhs,), in_specs=[pl.BlockSpec((1, dep...  21.2 us
    dot_general x1, matrix products, body(): jnp.dot(krylov, krylov.T, precision=lax.Precision.HIGHEST, preferred_elem...  11.8 us
    another operation x1, matrix products, body(): first_q = jax.scipy.linalg.solve_triangular(lower_first, krylov, lower=True)  11.7 us
    reshape x1, local copies, waits for them, and re-layouts, body(): krylov_powers(start_block, conductivity, reaction, strips).reshape(COLS, -1)  10.4 us
    pallas_call x1, Pallas kernels, edge_columns(): pl.pallas_call(columns_kernel, in_specs=[whole(start_block.shape), whole(...  9.84 us
    unnamed x12, local copies, waits for them, and re-layouts  7.99 us
    dot_general x1, matrix products, body(): jnp.dot(inverse, first_q, precision=lax.Precision.HIGH, preferred_element...  7.14 us
  transfers between devices with their start and end apart: 18, of which 18 were waited for; matrix products, arithmetic and copies ran while one was open for 0% of the time, Pallas kernels for 0%

profile of v1, /device:TPU:0, one launch (start us, length us, event | category | flops | bytes accessed | tf_op | source)
XLA Modules:
  0.0 184.9 jit_solution(5259473818495681875)
XLA Ops:
  2.6 5.4 %collective-permute-start = (f32[80,4,128]{2,1,0:T(4,128)S(1)}, f32[80,4,128]{2,1,0:T(4,128)S(1)}, u32[]{:S(2)}, u32[]{:S(2)}) collective-permute-start(f32[80,4,128]{2,1,0:T(4,128)S(1)} %pad_maximum_fusion), channel_id=1, source_target_pairs={{8,0},{16,8},{24,16},{32,24},{40,32},{48,40},{56,48},{64,56},{72,6... | collective-permute-start | bytes 491528 | tf_op jit(solution)/shard_map/ppermute | solution.py:89
  8.1 3.3 %collective-permute-done.xn_ref.refs_3_.refs_7_.refs_11_ = f32[80,4,128]{2,1,0:T(4,128)S(1)} collective-permute-done((f32[80,4,128]{2,1,0:T(4,128)S(1)}, f32[80,4,128]{2,1,0:T(4,128)S(1)}, u32[]{:S(2)}, u32[]{:S(2)}) %collective-permute-start) | collective-permute-done | bytes 163872 | tf_op jit(solution)/shard_map/ppermute | solution.py:89
  11.4 5.6 %collective-permute-done.1.xp_ref.refs_4_.refs_8_.refs_12_ = f32[80,4,128]{2,1,0:T(4,128)S(1)} collective-permute-done((f32[80,4,128]{2,1,0:T(4,128)S(1)}, f32[80,4,128]{2,1,0:T(4,128)S(1)}, u32[]{:S(2)}, u32[]{:S(2)}) %collective-permute-start.1) | collective-permute-done | bytes 163872 | tf_op jit(solution)/shard_map/ppermute | solution.py:90
  17.7 9.8 %shard_map.58 = (f32[80,4,128]{2,1,0:T(4,128)}, f32[80,4,128]{2,1,0:T(4,128)}) custom-call(f32[8,8,64,128]{3,2,1,0:T(8,128)} %refs_0_.1, f32[8,64,128]{2,1,0:T(8,128)} %refs_1_.1, f32[8,64,128]{2,1,0:T(8,128)} %refs_2_.1, f32[80,4,128]{2,1,0:T(4,128)} %copy-done.1, f32[80,4,128]{2,1,0:T(4,128)} %copy-done.2), custom_call_target="tpu_custom_call" | custom-call | tf_op jit(solution)/shard_map/pallas_call | solution.py:70
  27.6 2.3 %collective-permute-start.2 = (f32[80,4,128]{2,1,0:T(4,128)}, f32[80,4,128]{2,1,0:T(4,128)S(1)}, u32[]{:S(2)}, u32[]{:S(2)}) collective-permute-start(f32[80,4,128]{2,1,0:T(4,128)} %get-tuple-element.6), channel_id=1, source_target_pairs={{1,0},{2,1},{3,2},{4,3},{5,4},{6,5},{7,6},{0,7},{9,8},{10,9},{11,1... | collective-permute-start | bytes 491528 | tf_op jit(solution)/shard_map/ppermute | solution.py:93
  29.8 3.1 %collective-permute-done.2.refs_5_.refs_9_.refs_13_ = f32[80,4,128]{2,1,0:T(4,128)S(1)} collective-permute-done((f32[80,4,128]{2,1,0:T(4,128)}, f32[80,4,128]{2,1,0:T(4,128)S(1)}, u32[]{:S(2)}, u32[]{:S(2)}) %collective-permute-start.2) | collective-permute-done | bytes 163872 | tf_op jit(solution)/shard_map/ppermute | solution.py:93
  33.0 3.0 %collective-permute-done.3.refs_6_.refs_10_.refs_14_ = f32[80,4,128]{2,1,0:T(4,128)S(1)} collective-permute-done((f32[80,4,128]{2,1,0:T(4,128)}, f32[80,4,128]{2,1,0:T(4,128)S(1)}, u32[]{:S(2)}, u32[]{:S(2)}) %collective-permute-start.3) | collective-permute-done | bytes 163872 | tf_op jit(solution)/shard_map/ppermute | solution.py:94
  36.7 21.2 %shard_map.59 = f32[5,8,8,64,128]{4,3,2,1,0:T(8,128)} custom-call(f32[8,8,64,128]{3,2,1,0:T(8,128)} %refs_0_.1, f32[8,64,128]{2,1,0:T(8,128)} %refs_1_.1, f32[8,64,128]{2,1,0:T(8,128)} %refs_2_.1, f32[80,4,128]{2,1,0:T(4,128)} %copy-done.1, f32[80,4,128]{2,1,0:T(4,128)} %copy-done.2, f32[80,4,128]{2,1,0:T(4,128)} %copy-done.3, f32[80,4,128]{2,1,0:T(4,128)} %copy-done.4, ...), custom_call_target="tpu_custom_call" | custom-call | tf_op jit(solution)/shard_map/pallas_call | solution.py:168
  57.9 10.4 %reshape.33 = f32[40,65536]{1,0:T(8,128)} reshape(f32[5,8,8,64,128]{4,3,2,1,0:T(8,128)} %shard_map.59) | data formatting | bytes 20971520 | tf_op jit(solution)/shard_map/reshape | solution.py:197
  68.3 11.8 %fusion.19 = f32[40,40]{0,1:T(8,128)S(1)} fusion(f32[40,65536]{1,0:T(8,128)} %reshape.33), kind=kOutput, calls=%fused_computation.35 | convolution fusion | flops 1258291200 | bytes 10492160 | tf_op jit(solution)/shard_map/dot_general | solution.py:198
  80.2 3.8 %collective-permute-done.4 = f32[40,40]{0,1:T(8,128)S(1)} collective-permute-done((f32[40,40]{0,1:T(8,128)S(1)}, f32[40,40]{0,1:T(8,128)S(1)}, u32[]{:S(2)}, u32[]{:S(2)}) %collective-permute-start.4) | collective-permute-done | bytes 6432 | tf_op jit(solution)/shard_map/ppermute | solution.py:113
  84.0 5.3 %collective-permute-done.5 = f32[40,40]{0,1:T(8,128)S(1)} collective-permute-done((f32[40,40]{0,1:T(8,128)S(1)}, f32[40,40]{0,1:T(8,128)S(1)}, u32[]{:S(2)}, u32[]{:S(2)}) %collective-permute-start.5) | collective-permute-done | bytes 6432 | tf_op jit(solution)/shard_map/ppermute | solution.py:113
  89.3 3.8 %collective-permute-done.6 = f32[40,40]{0,1:T(8,128)S(1)} collective-permute-done((f32[40,40]{0,1:T(8,128)S(1)}, f32[40,40]{0,1:T(8,128)S(1)}, u32[]{:S(2)}, u32[]{:S(2)}) %collective-permute-start.6) | collective-permute-done | bytes 6432 | tf_op jit(solution)/shard_map/ppermute | solution.py:113
  93.1 5.3 %collective-permute-done.7 = f32[40,40]{0,1:T(8,128)S(1)} collective-permute-done((f32[40,40]{0,1:T(8,128)S(1)}, f32[40,40]{0,1:T(8,128)S(1)}, u32[]{:S(2)}, u32[]{:S(2)}) %collective-permute-start.7) | collective-permute-done | bytes 6432 | tf_op jit(solution)/shard_map/ppermute | solution.py:113
  98.4 1.2 collective-permute-done.8
  99.6 3.8 %collective-permute-done.9 = f32[40,40]{0,1:T(8,128)S(1)} collective-permute-done((f32[40,40]{0,1:T(8,128)S(1)}, f32[40,40]{0,1:T(8,128)S(1)}, u32[]{:S(2)}, u32[]{:S(2)}) %collective-permute-start.9) | collective-permute-done | bytes 6432 | tf_op jit(solution)/shard_map/ppermute | solution.py:113
  103.8 4.9 %collective-permute-done.10 = f32[40,40]{0,1:T(8,128)S(1)} collective-permute-done((f32[40,40]{0,1:T(8,128)S(1)}, f32[40,40]{0,1:T(8,128)S(1)}, u32[]{:S(2)}, u32[]{:S(2)}) %collective-permute-start.10) | collective-permute-done | bytes 6432 | tf_op jit(solution)/shard_map/ppermute | solution.py:113
  108.8 3.6 %cholesky.44 = f32[40,40]{1,0:T(8,128)S(1)} custom-call(f32[40,40]{1,0:T(8,128)S(1)} %fusion.5), custom_call_target="Cholesky" | custom-call | tf_op jit(solution)/shard_map/jit(cholesky)/cholesky | solution.py:203
  113.8 3.1 %custom-call.10 = f32[1,40,40]{1,2,0:T(8,128)S(1)} custom-call(f32[1,40,40]{2,1,0:T(8,128)S(1)} %get-tuple-element.18), custom_call_target="InvertDiagBlocksLowerTriangular" | custom-call | tf_op jit(solution)/shard_map/jit(_solve_triangular)/triangular_solve | solution.py:204
  116.8 11.7 %fusion.3 = f32[40,65536]{1,0:T(8,128)S(1)} fusion(f32[40,65536]{1,0:T(8,128)} %reshape.33, f32[1,40,40]{1,2,0:T(8,128)S(1)} %custom-call.10), kind=kOutput, calls=%fused_computation.7 | convolution fusion | flops 1258291200 | bytes 20977920 | tf_op jit(solution)/shard_map/jit(_solve_triangular)/triangular_solve | solution.py:204
  128.5 4.2 %fusion.20 = f32[40,40]{0,1:T(8,128)S(1)} fusion(f32[40,65536]{1,0:T(8,128)S(1)} %fusion.3), kind=kOutput, calls=%fused_computation.36 | convolution fusion | flops 629145600 | bytes 10492160 | tf_op jit(solution)/shard_map/dot_general | solution.py:205
  132.8 3.8 %collective-permute-done.11 = f32[40,40]{0,1:T(8,128)S(1)} collective-permute-done((f32[40,40]{0,1:T(8,128)S(1)}, f32[40,40]{0,1:T(8,128)S(1)}, u32[]{:S(2)}, u32[]{:S(2)}) %collective-permute-start.11) | collective-permute-done | bytes 6432 | tf_op jit(solution)/shard_map/ppermute | solution.py:113
  136.6 5.3 %collective-permute-done.12 = f32[40,40]{0,1:T(8,128)S(1)} collective-permute-done((f32[40,40]{0,1:T(8,128)S(1)}, f32[40,40]{0,1:T(8,128)S(1)}, u32[]{:S(2)}, u32[]{:S(2)}) %collective-permute-start.12) | collective-permute-done | bytes 6432 | tf_op jit(solution)/shard_map/ppermute | solution.py:113
  141.9 3.8 %collective-permute-done.13 = f32[40,40]{0,1:T(8,128)S(1)} collective-permute-done((f32[40,40]{0,1:T(8,128)S(1)}, f32[40,40]{0,1:T(8,128)S(1)}, u32[]{:S(2)}, u32[]{:S(2)}) %collective-permute-start.13) | collective-permute-done | bytes 6432 | tf_op jit(solution)/shard_map/ppermute | solution.py:113
  145.7 5.3 %collective-permute-done.14 = f32[40,40]{0,1:T(8,128)S(1)} collective-permute-done((f32[40,40]{0,1:T(8,128)S(1)}, f32[40,40]{0,1:T(8,128)S(1)}, u32[]{:S(2)}, u32[]{:S(2)}) %collective-permute-start.14) | collective-permute-done | bytes 6432 | tf_op jit(solution)/shard_map/ppermute | solution.py:113
  152.2 3.8 %collective-permute-done.16 = f32[40,40]{0,1:T(8,128)S(1)} collective-permute-done((f32[40,40]{0,1:T(8,128)S(1)}, f32[40,40]{0,1:T(8,128)S(1)}, u32[]{:S(2)}, u32[]{:S(2)}) %collective-permute-start.16) | collective-permute-done | bytes 6432 | tf_op jit(solution)/shard_map/ppermute | solution.py:113
  157.0 4.2 %collective-permute-done.17 = f32[40,40]{0,1:T(8,128)S(1)} collective-permute-done((f32[40,40]{0,1:T(8,128)S(1)}, f32[40,40]{0,1:T(8,128)S(1)}, u32[]{:S(2)}, u32[]{:S(2)}) %collective-permute-start.17) | collective-permute-done | bytes 6432 | tf_op jit(solution)/shard_map/ppermute | solution.py:113
  161.3 3.6 %cholesky.55 = f32[40,40]{1,0:T(8,128)S(1)} custom-call(f32[40,40]{1,0:T(8,128)S(1)} %fusion.2), custom_call_target="Cholesky" | custom-call | tf_op jit(solution)/shard_map/jit(cholesky)/cholesky | solution.py:209
  165.7 2.1 %fusion.8 = f32[40,40]{1,0:T(8,128)} fusion(f32[40,40]{1,0:T(8,128)S(1)} %cholesky.55, f32[40,40]{1,0:T(8,128)S(1)} %cholesky.44, pred[]{:T(512)} %compare_reduce_fusion, pred[]{:T(512)} %compare_reduce_fusion.1), kind=kOutput, calls=%fused_computation.22 | convolution fusion | flops 777600 | bytes 19202 | tf_op jit(solution)/shard_map/dot_general | solution.py:214
  168.4 3.1 %custom-call.11 = f32[1,40,40]{1,2,0:T(8,128)S(1)} custom-call(f32[1,40,40]{2,1,0:T(8,128)S(1)} %select_bitcast_fusion), custom_call_target="InvertDiagBlocksLowerTriangular" | custom-call | tf_op jit(solution)/shard_map/jit(_solve_triangular)/triangular_solve | solution.py:210
  171.7 7.1 %convolution_bitcast_fusion = f32[5,8,512,128]{3,1,2,0:T(8,128)S(1)} fusion(f32[40,40]{1,0:T(8,128)S(1)} %fusion, f32[40,65536]{1,0:T(8,128)} %copy-done), kind=kOutput, calls=%fused_computation | convolution fusion | flops 629145600 | bytes 20977920 | tf_op jit(solution)/shard_map/dot_general | solution.py:213
  178.9 6.0 %copy.15 = f32[5,8,512,128]{3,2,1,0:T(8,128)} copy(f32[5,8,512,128]{3,1,2,0:T(8,128)S(1)} %convolution_bitcast_fusion) | data formatting | bytes 20971520
  (57 shorter events, 9.4 us)
Async XLA Ops:
  2.6 8.8 %collective-permute-start = (f32[80,4,128]{2,1,0:T(4,128)S(1)}, f32[80,4,128]{2,1,0:T(4,128)S(1)}, u32[]{:S(2)}, u32[]{:S(2)}) collective-permute-start(f32[80,4,128]{2,1,0:T(4,128)S(1)} %pad_maximum_fusion), channel_id=1, source_target_pairs={{8,0},{16,8},{24,16},{32,24},{40,32},{48,40},{56,48},{64,56},{72,6... | collective-permute-start | bytes 491528 | tf_op jit(solution)/shard_map/ppermute | solution.py:89
  8.0 9.0 %collective-permute-start.1 = (f32[80,4,128]{2,1,0:T(4,128)S(1)}, f32[80,4,128]{2,1,0:T(4,128)S(1)}, u32[]{:S(2)}, u32[]{:S(2)}) collective-permute-start(f32[80,4,128]{2,1,0:T(4,128)S(1)} %pad_maximum_fusion.1), channel_id=1, source_target_pairs={{0,8},{8,16},{16,24},{24,32},{32,40},{40,48},{48,56},{56,64},{64,7... | collective-permute-start | bytes 491528 | tf_op jit(solution)/shard_map/ppermute | solution.py:90
  11.4 5.6 %copy-start.1 = (f32[80,4,128]{2,1,0:T(4,128)}, f32[80,4,128]{2,1,0:T(4,128)S(1)}, u32[]{:S(2)}) copy-start(f32[80,4,128]{2,1,0:T(4,128)S(1)} %collective-permute-done.xn_ref.refs_3_.refs_7_.refs_11_) | copy-start | bytes 491524
  17.0 0.7 copy-start.2
  27.6 5.4 %collective-permute-start.2 = (f32[80,4,128]{2,1,0:T(4,128)}, f32[80,4,128]{2,1,0:T(4,128)S(1)}, u32[]{:S(2)}, u32[]{:S(2)}) collective-permute-start(f32[80,4,128]{2,1,0:T(4,128)} %get-tuple-element.6), channel_id=1, source_target_pairs={{1,0},{2,1},{3,2},{4,3},{5,4},{6,5},{7,6},{0,7},{9,8},{10,9},{11,1... | collective-permute-start | bytes 491528 | tf_op jit(solution)/shard_map/ppermute | solution.py:93
  29.8 6.2 %collective-permute-start.3 = (f32[80,4,128]{2,1,0:T(4,128)}, f32[80,4,128]{2,1,0:T(4,128)S(1)}, u32[]{:S(2)}, u32[]{:S(2)}) collective-permute-start(f32[80,4,128]{2,1,0:T(4,128)} %get-tuple-element.7), channel_id=1, source_target_pairs={{0,1},{1,2},{2,3},{3,4},{4,5},{5,6},{6,7},{7,0},{8,9},{9,10},{10,1... | collective-permute-start | bytes 491528 | tf_op jit(solution)/shard_map/ppermute | solution.py:94
  33.0 3.0 %copy-start.3 = (f32[80,4,128]{2,1,0:T(4,128)}, f32[80,4,128]{2,1,0:T(4,128)S(1)}, u32[]{:S(2)}) copy-start(f32[80,4,128]{2,1,0:T(4,128)S(1)} %collective-permute-done.2.refs_5_.refs_9_.refs_13_) | copy-start | bytes 491524
  36.0 0.7 copy-start.4
  80.1 3.9 %collective-permute-start.4 = (f32[40,40]{0,1:T(8,128)S(1)}, f32[40,40]{0,1:T(8,128)S(1)}, u32[]{:S(2)}, u32[]{:S(2)}) collective-permute-start(f32[40,40]{0,1:T(8,128)S(1)} %fusion.19), channel_id=1, source_target_pairs={{0,8},{8,0},{16,24},{24,16},{32,40},{40,32},{48,56},{56,48},{64,72... | collective-permute-start | bytes 19208 | tf_op jit(solution)/shard_map/ppermute | solution.py:113
  84.0 5.3 %collective-permute-start.5 = (f32[40,40]{0,1:T(8,128)S(1)}, f32[40,40]{0,1:T(8,128)S(1)}, u32[]{:S(2)}, u32[]{:S(2)}) collective-permute-start(f32[40,40]{0,1:T(8,128)S(1)} %add.55), channel_id=1, source_target_pairs={{0,16},{8,24},{16,0},{24,8},{32,48},{40,56},{48,32},{56,40},{64,80... | collective-permute-start | bytes 19208 | tf_op jit(solution)/shard_map/ppermute | solution.py:113
  89.3 3.8 %collective-permute-start.6 = (f32[40,40]{0,1:T(8,128)S(1)}, f32[40,40]{0,1:T(8,128)S(1)}, u32[]{:S(2)}, u32[]{:S(2)}) collective-permute-start(f32[40,40]{0,1:T(8,128)S(1)} %add.56), channel_id=1, source_target_pairs={{0,32},{8,40},{16,48},{24,56},{32,0},{40,8},{48,16},{56,24},{64,96... | collective-permute-start | bytes 19208 | tf_op jit(solution)/shard_map/ppermute | solution.py:113
  93.1 5.3 %collective-permute-start.7 = (f32[40,40]{0,1:T(8,128)S(1)}, f32[40,40]{0,1:T(8,128)S(1)}, u32[]{:S(2)}, u32[]{:S(2)}) collective-permute-start(f32[40,40]{0,1:T(8,128)S(1)} %add.57), channel_id=1, source_target_pairs={{0,64},{8,72},{16,80},{24,88},{32,96},{40,104},{48,112},{56,120},{... | collective-permute-start | bytes 19208 | tf_op jit(solution)/shard_map/ppermute | solution.py:113
  98.4 1.2 collective-permute-start.8
  99.6 3.8 %collective-permute-start.9 = (f32[40,40]{0,1:T(8,128)S(1)}, f32[40,40]{0,1:T(8,128)S(1)}, u32[]{:S(2)}, u32[]{:S(2)}) collective-permute-start(f32[40,40]{0,1:T(8,128)S(1)} %add.59), channel_id=1, source_target_pairs={{0,2},{1,3},{2,0},{3,1},{4,6},{5,7},{6,4},{7,5},{8,10},{9,11},{10,... | collective-permute-start | bytes 19208 | tf_op jit(solution)/shard_map/ppermute | solution.py:113
  103.4 5.3 %collective-permute-start.10 = (f32[40,40]{0,1:T(8,128)S(1)}, f32[40,40]{0,1:T(8,128)S(1)}, u32[]{:S(2)}, u32[]{:S(2)}) collective-permute-start(f32[40,40]{0,1:T(8,128)S(1)} %add.60), channel_id=1, source_target_pairs={{0,4},{1,5},{2,6},{3,7},{4,0},{5,1},{6,2},{7,3},{8,12},{9,13},{10,... | collective-permute-start | bytes 19208 | tf_op jit(solution)/shard_map/ppermute | solution.py:113
  128.5 4.2 %copy-start = (f32[40,65536]{1,0:T(8,128)}, f32[40,65536]{1,0:T(8,128)S(1)}, u32[]{:S(2)}) copy-start(f32[40,65536]{1,0:T(8,128)S(1)} %fusion.3) | copy-start | bytes 31457284
  132.7 3.9 %collective-permute-start.11 = (f32[40,40]{0,1:T(8,128)S(1)}, f32[40,40]{0,1:T(8,128)S(1)}, u32[]{:S(2)}, u32[]{:S(2)}) collective-permute-start(f32[40,40]{0,1:T(8,128)S(1)} %fusion.20), channel_id=1, source_target_pairs={{0,8},{8,0},{16,24},{24,16},{32,40},{40,32},{48,56},{56,48},{64,72... | collective-permute-start | bytes 19208 | tf_op jit(solution)/shard_map/ppermute | solution.py:113
  136.6 5.3 %collective-permute-start.12 = (f32[40,40]{0,1:T(8,128)S(1)}, f32[40,40]{0,1:T(8,128)S(1)}, u32[]{:S(2)}, u32[]{:S(2)}) collective-permute-start(f32[40,40]{0,1:T(8,128)S(1)} %add.62), channel_id=1, source_target_pairs={{0,16},{8,24},{16,0},{24,8},{32,48},{40,56},{48,32},{56,40},{64,80... | collective-permute-start | bytes 19208 | tf_op jit(solution)/shard_map/ppermute | solution.py:113
  141.9 3.8 %collective-permute-start.13 = (f32[40,40]{0,1:T(8,128)S(1)}, f32[40,40]{0,1:T(8,128)S(1)}, u32[]{:S(2)}, u32[]{:S(2)}) collective-permute-start(f32[40,40]{0,1:T(8,128)S(1)} %add.63), channel_id=1, source_target_pairs={{0,32},{8,40},{16,48},{24,56},{32,0},{40,8},{48,16},{56,24},{64,96... | collective-permute-start | bytes 19208 | tf_op jit(solution)/shard_map/ppermute | solution.py:113
  145.7 5.3 %collective-permute-start.14 = (f32[40,40]{0,1:T(8,128)S(1)}, f32[40,40]{0,1:T(8,128)S(1)}, u32[]{:S(2)}, u32[]{:S(2)}) collective-permute-start(f32[40,40]{0,1:T(8,128)S(1)} %add.64), channel_id=1, source_target_pairs={{0,64},{8,72},{16,80},{24,88},{32,96},{40,104},{48,112},{56,120},{... | collective-permute-start | bytes 19208 | tf_op jit(solution)/shard_map/ppermute | solution.py:113
  151.0 1.2 collective-permute-start.15
  152.2 3.8 %collective-permute-start.16 = (f32[40,40]{0,1:T(8,128)S(1)}, f32[40,40]{0,1:T(8,128)S(1)}, u32[]{:S(2)}, u32[]{:S(2)}) collective-permute-start(f32[40,40]{0,1:T(8,128)S(1)} %add.66), channel_id=1, source_target_pairs={{0,2},{1,3},{2,0},{3,1},{4,6},{5,7},{6,4},{7,5},{8,10},{9,11},{10,... | collective-permute-start | bytes 19208 | tf_op jit(solution)/shard_map/ppermute | solution.py:113
  156.0 5.3 %collective-permute-start.17 = (f32[40,40]{0,1:T(8,128)S(1)}, f32[40,40]{0,1:T(8,128)S(1)}, u32[]{:S(2)}, u32[]{:S(2)}) collective-permute-start(f32[40,40]{0,1:T(8,128)S(1)} %add.67), channel_id=1, source_target_pairs={{0,4},{1,5},{2,6},{3,7},{4,0},{5,1},{6,2},{7,3},{8,12},{9,13},{10,... | collective-permute-start | bytes 19208 | tf_op jit(solution)/shard_map/ppermute | solution.py:113

commit v2 on v1

--- a/solution.py
+++ b/solution.py
@@ -184,6 +184,39 @@
     )(start_block, conductivity, reaction, *(strips * 3))
 
 
+def factor_kernel(gram_ref, upper_ref, inverse_ref):
+    size = gram_ref.shape[0]
+    rows = lax.broadcasted_iota(jnp.int32, (size, size), 0)
+    cols = lax.broadcasted_iota(jnp.int32, (size, size), 1)
+    work = gram_ref[...]
+    lower = jnp.zeros((size, size), jnp.float32)
+    upper = jnp.zeros((size, size), jnp.float32)
+    for j in range(size):
+        pivot = jnp.sqrt(work[j : j + 1, j : j + 1])
+        column = jnp.where(rows[:, j : j + 1] >= j, work[:, j : j + 1] / pivot, 0.0)
+        row = jnp.where(cols[j : j + 1, :] >= j, work[j : j + 1, :] / pivot, 0.0)
+        lower = jnp.where(cols == j, column, lower)
+        upper = jnp.where(rows == j, row, upper)
+        work = work - column * row
+    pending = jnp.where(rows == cols, 1.0, 0.0).astype(jnp.float32)
+    inverse = jnp.zeros((size, size), jnp.float32)
+    for k in range(size):
+        solved = pending[k : k + 1, :] / lower[k : k + 1, k : k + 1]
+        inverse = jnp.where(rows == k, solved, inverse)
+        below = jnp.where(rows[:, k : k + 1] > k, lower[:, k : k + 1], 0.0)
+        pending = pending - below * solved
+    upper_ref[...] = upper
+    inverse_ref[...] = inverse
+
+
+def cholesky_factors(gram, cells_total):
+    size = gram.shape[0]
+    square = jax.ShapeDtypeStruct((size, size), jnp.float32)
+    scaled = gram / cells_total
+    symmetric = (scaled + scaled.T) / 2
+    return pl.pallas_call(factor_kernel, out_shape=[square, square])(symmetric)
+
+
 def body(start_block, conductivity, reaction):
     cells_total = (
         start_block.shape[1]
@@ -198,29 +231,27 @@
     local_gram = jnp.dot(
         krylov, krylov.T, precision=lax.Precision.HIGHEST, preferred_element_type=jnp.float32
     )
-    gram_first = tree_sum(local_gram, ("gx", "gy"))
-    gram_first = gram_first / cells_total
-    lower_first = jnp.linalg.cholesky(gram_first)
-    first_q = jax.scipy.linalg.solve_triangular(lower_first, krylov, lower=True)
+    upper_first, inverse_first = cholesky_factors(tree_sum(local_gram, ("gx", "gy")), cells_total)
+    first_q = jnp.dot(
+        inverse_first, krylov, precision=lax.Precision.HIGHEST, preferred_element_type=jnp.float32
+    )
     local_again = jnp.dot(
         first_q, first_q.T, precision=lax.Precision.HIGH, preferred_element_type=jnp.float32
     )
-    gram_second = tree_sum(local_again, ("gx", "gy")) / cells_total
-    lower_second = jnp.linalg.cholesky(gram_second)
-    inverse = jax.scipy.linalg.solve_triangular(
-        lower_second, jnp.eye(COLS, dtype=jnp.float32), lower=True
-    )
-    basis = jnp.dot(inverse, first_q, precision=lax.Precision.HIGH, preferred_element_type=jnp.float32)
+    upper_second, inverse_second = cholesky_factors(tree_sum(local_again, ("gx", "gy")), cells_total)
+    basis = jnp.dot(
+        inverse_second, first_q, precision=lax.Precision.HIGH, preferred_element_type=jnp.float32
+    )
     r_factor = jnp.dot(
-        lower_second.T,
-        lower_first.T,
+        upper_second,
+        upper_first,
         precision=lax.Precision.HIGHEST,
         preferred_element_type=jnp.float32,
     )
     return (
         basis.reshape(COLS, start_block.shape[1], start_block.shape[2], start_block.shape[3]),
         r_factor,
-        lower_first.T,
+        upper_first,
     )
 
 

time: 185 us -> 179 us (0.968)
  other arithmetic: 16.3 us -> 1.39 us
  Pallas kernels: 31.1 us -> 41.7 us
    another operation x9 -> x0, other arithmetic: 15.5 us -> none  [the longest x3 4.39 us: body(): lower_second = jnp.linalg.cholesky(gram_second)]
    another operation x2 -> x0, matrix products: 11.9 us -> none  [the longest x1 11.7 us: body(): first_q = jax.scipy.linalg.solve_triangular(lower_first, krylov, lower=True)]
    pallas_call x0 -> x2, Pallas kernels: none -> 10.6 us  [cholesky_factors(): return pl.pallas_call(factor_kernel, out_shape=[square, square])(symmetric)]
    dot_general x2 -> x3, matrix products: 9.22 us -> 19.5 us  [the longest x1 11.6 us: body(): jnp.dot(inverse_first, krylov, precision=lax.Precision.HIGHEST, preferred...]
    unnamed x12 -> x15, local copies, waits for them, and re-layouts: 7.99 us -> 7.33 us
where the time goes in v2:
time: 179 us
  waiting for transfers between devices  71 us (40%)
  Pallas kernels  41.7 us (23%)
  matrix products  35.5 us (20%)
  local copies, waits for them, and re-layouts  19.9 us (11%)
  starting transfers between devices  8.76 us (5%)
    ppermute x14, waiting for transfers between devices, tree_sum(): value = value + lax.ppermute(value, axis, pairs)  55.9 us
    pallas_call x1, Pallas kernels, krylov_powers(): pl.pallas_call(powers_kernel, grid=(rhs,), in_specs=[pl.BlockSpec((1, dep...  21.2 us
    dot_general x1, matrix products, body(): jnp.dot(krylov, krylov.T, precision=lax.Precision.HIGHEST, preferred_elem...  11.8 us
    dot_general x1, matrix products, body(): jnp.dot(inverse_first, krylov, precision=lax.Precision.HIGHEST, preferred...  11.6 us
    pallas_call x2, Pallas kernels, cholesky_factors(): return pl.pallas_call(factor_kernel, out_shape=[square, square])(symmetric)  10.6 us
    reshape x1, local copies, waits for them, and re-layouts, body(): krylov_powers(start_block, conductivity, reaction, strips).reshape(COLS, -1)  10.4 us
    pallas_call x1, Pallas kernels, edge_columns(): pl.pallas_call(columns_kernel, in_specs=[whole(start_block.shape), whole(...  9.85 us
    unnamed x15, local copies, waits for them, and re-layouts  7.33 us
  transfers between devices with their start and end apart: 18, of which 18 were waited for; matrix products, arithmetic and copies ran while one was open for 0% of the time, Pallas kernels for 0%

profile of v2, /device:TPU:0, one launch (start us, length us, event | category | flops | bytes accessed | tf_op | source)
XLA Modules:
  0.0 179.0 jit_solution(10630823970038335208)
XLA Ops:
  0.6 1.1 fusion.1
  1.7 0.8 fusion.2
  2.6 5.4 %collective-permute-start = (f32[80,4,128]{2,1,0:T(4,128)S(1)}, f32[80,4,128]{2,1,0:T(4,128)S(1)}, u32[]{:S(2)}, u32[]{:S(2)}) collective-permute-start(f32[80,4,128]{2,1,0:T(4,128)S(1)} %pad_maximum_fusion), channel_id=1, source_target_pairs={{8,0},{16,8},{24,16},{32,24},{40,32},{48,40},{56,48},{64,56},{72,6... | collective-permute-start | bytes 491528 | tf_op jit(solution)/shard_map/ppermute | solution.py:89
  8.1 3.3 %collective-permute-done.xn_ref.refs_3_.refs_7_.refs_11_ = f32[80,4,128]{2,1,0:T(4,128)S(1)} collective-permute-done((f32[80,4,128]{2,1,0:T(4,128)S(1)}, f32[80,4,128]{2,1,0:T(4,128)S(1)}, u32[]{:S(2)}, u32[]{:S(2)}) %collective-permute-start) | collective-permute-done | bytes 163872 | tf_op jit(solution)/shard_map/ppermute | solution.py:89
  11.4 5.6 %collective-permute-done.1.xp_ref.refs_4_.refs_8_.refs_12_ = f32[80,4,128]{2,1,0:T(4,128)S(1)} collective-permute-done((f32[80,4,128]{2,1,0:T(4,128)S(1)}, f32[80,4,128]{2,1,0:T(4,128)S(1)}, u32[]{:S(2)}, u32[]{:S(2)}) %collective-permute-start.1) | collective-permute-done | bytes 163872 | tf_op jit(solution)/shard_map/ppermute | solution.py:90
  17.7 9.9 %shard_map.58 = (f32[80,4,128]{2,1,0:T(4,128)}, f32[80,4,128]{2,1,0:T(4,128)}) custom-call(f32[8,8,64,128]{3,2,1,0:T(8,128)} %refs_0_.1, f32[8,64,128]{2,1,0:T(8,128)} %refs_1_.1, f32[8,64,128]{2,1,0:T(8,128)} %refs_2_.1, f32[80,4,128]{2,1,0:T(4,128)} %copy-done.1, f32[80,4,128]{2,1,0:T(4,128)} %copy-done.2), custom_call_target="tpu_custom_call" | custom-call | tf_op jit(solution)/shard_map/pallas_call | solution.py:70
  27.6 2.3 %collective-permute-start.2 = (f32[80,4,128]{2,1,0:T(4,128)}, f32[80,4,128]{2,1,0:T(4,128)S(1)}, u32[]{:S(2)}, u32[]{:S(2)}) collective-permute-start(f32[80,4,128]{2,1,0:T(4,128)} %get-tuple-element.9), channel_id=1, source_target_pairs={{1,0},{2,1},{3,2},{4,3},{5,4},{6,5},{7,6},{0,7},{9,8},{10,9},{11,1... | collective-permute-start | bytes 491528 | tf_op jit(solution)/shard_map/ppermute | solution.py:93
  29.8 3.1 %collective-permute-done.2.refs_5_.refs_9_.refs_13_ = f32[80,4,128]{2,1,0:T(4,128)S(1)} collective-permute-done((f32[80,4,128]{2,1,0:T(4,128)}, f32[80,4,128]{2,1,0:T(4,128)S(1)}, u32[]{:S(2)}, u32[]{:S(2)}) %collective-permute-start.2) | collective-permute-done | bytes 163872 | tf_op jit(solution)/shard_map/ppermute | solution.py:93
  33.0 3.0 %collective-permute-done.3.refs_6_.refs_10_.refs_14_ = f32[80,4,128]{2,1,0:T(4,128)S(1)} collective-permute-done((f32[80,4,128]{2,1,0:T(4,128)}, f32[80,4,128]{2,1,0:T(4,128)S(1)}, u32[]{:S(2)}, u32[]{:S(2)}) %collective-permute-start.3) | collective-permute-done | bytes 163872 | tf_op jit(solution)/shard_map/ppermute | solution.py:94
  36.7 21.2 %shard_map.59 = f32[5,8,8,64,128]{4,3,2,1,0:T(8,128)} custom-call(f32[8,8,64,128]{3,2,1,0:T(8,128)} %refs_0_.1, f32[8,64,128]{2,1,0:T(8,128)} %refs_1_.1, f32[8,64,128]{2,1,0:T(8,128)} %refs_2_.1, f32[80,4,128]{2,1,0:T(4,128)} %copy-done.1, f32[80,4,128]{2,1,0:T(4,128)} %copy-done.2, f32[80,4,128]{2,1,0:T(4,128)} %copy-done.3, f32[80,4,128]{2,1,0:T(4,128)} %copy-done.4, ...), custom_call_target="tpu_custom_call" | custom-call | tf_op jit(solution)/shard_map/pallas_call | solution.py:168
  57.9 10.4 %reshape.20 = f32[40,65536]{1,0:T(8,128)} reshape(f32[5,8,8,64,128]{4,3,2,1,0:T(8,128)} %shard_map.59) | data formatting | bytes 20971520 | tf_op jit(solution)/shard_map/reshape | solution.py:230
  68.3 11.8 %fusion.4 = f32[40,40]{0,1:T(8,128)S(1)} fusion(f32[40,65536]{1,0:T(8,128)} %reshape.20), kind=kOutput, calls=%fused_computation.12 | convolution fusion | flops 1258291200 | bytes 10492160 | tf_op jit(solution)/shard_map/dot_general | solution.py:231
  80.3 3.8 %collective-permute-done.4 = f32[40,40]{0,1:T(8,128)S(1)} collective-permute-done((f32[40,40]{0,1:T(8,128)S(1)}, f32[40,40]{0,1:T(8,128)S(1)}, u32[]{:S(2)}, u32[]{:S(2)}) %collective-permute-start.4) | collective-permute-done | bytes 6432 | tf_op jit(solution)/shard_map/ppermute | solution.py:113
  84.0 5.3 %collective-permute-done.5 = f32[40,40]{0,1:T(8,128)S(1)} collective-permute-done((f32[40,40]{0,1:T(8,128)S(1)}, f32[40,40]{0,1:T(8,128)S(1)}, u32[]{:S(2)}, u32[]{:S(2)}) %collective-permute-start.5) | collective-permute-done | bytes 6432 | tf_op jit(solution)/shard_map/ppermute | solution.py:113
  89.3 3.8 %collective-permute-done.6 = f32[40,40]{0,1:T(8,128)S(1)} collective-permute-done((f32[40,40]{0,1:T(8,128)S(1)}, f32[40,40]{0,1:T(8,128)S(1)}, u32[]{:S(2)}, u32[]{:S(2)}) %collective-permute-start.6) | collective-permute-done | bytes 6432 | tf_op jit(solution)/shard_map/ppermute | solution.py:113
  93.1 5.3 %collective-permute-done.7 = f32[40,40]{0,1:T(8,128)S(1)} collective-permute-done((f32[40,40]{0,1:T(8,128)S(1)}, f32[40,40]{0,1:T(8,128)S(1)}, u32[]{:S(2)}, u32[]{:S(2)}) %collective-permute-start.7) | collective-permute-done | bytes 6432 | tf_op jit(solution)/shard_map/ppermute | solution.py:113
  98.4 1.2 collective-permute-done.8
  99.6 3.8 %collective-permute-done.9 = f32[40,40]{0,1:T(8,128)S(1)} collective-permute-done((f32[40,40]{0,1:T(8,128)S(1)}, f32[40,40]{0,1:T(8,128)S(1)}, u32[]{:S(2)}, u32[]{:S(2)}) %collective-permute-start.9) | collective-permute-done | bytes 6432 | tf_op jit(solution)/shard_map/ppermute | solution.py:113
  103.8 4.9 %collective-permute-done.10 = f32[40,40]{0,1:T(8,128)S(1)} collective-permute-done((f32[40,40]{0,1:T(8,128)S(1)}, f32[40,40]{0,1:T(8,128)S(1)}, u32[]{:S(2)}, u32[]{:S(2)}) %collective-permute-start.10) | collective-permute-done | bytes 6432 | tf_op jit(solution)/shard_map/ppermute | solution.py:113
  109.4 5.3 %shard_map.60 = (f32[40,40]{1,0:T(8,128)}, f32[40,40]{1,0:T(8,128)}) custom-call(f32[40,40]{1,0:T(8,128)} %fusion.gram_ref), custom_call_target="tpu_custom_call" | custom-call | tf_op jit(solution)/shard_map/pallas_call | solution.py:217
  114.7 11.6 %fusion.5 = f32[40,65536]{1,0:T(8,128)S(1)} fusion(f32[40,40]{1,0:T(8,128)} %get-tuple-element.11, f32[40,65536]{1,0:T(8,128)} %reshape.20), kind=kOutput, calls=%fused_computation.13 | convolution fusion | flops 1258291200 | bytes 20977920 | tf_op jit(solution)/shard_map/dot_general | solution.py:235
  126.3 4.2 %fusion.6 = f32[40,40]{0,1:T(8,128)S(1)} fusion(f32[40,65536]{1,0:T(8,128)S(1)} %fusion.5), kind=kOutput, calls=%fused_computation.14 | convolution fusion | flops 629145600 | bytes 10492160 | tf_op jit(solution)/shard_map/dot_general | solution.py:238
  130.6 3.8 %collective-permute-done.11 = f32[40,40]{0,1:T(8,128)S(1)} collective-permute-done((f32[40,40]{0,1:T(8,128)S(1)}, f32[40,40]{0,1:T(8,128)S(1)}, u32[]{:S(2)}, u32[]{:S(2)}) %collective-permute-start.11) | collective-permute-done | bytes 6432 | tf_op jit(solution)/shard_map/ppermute | solution.py:113
  134.4 5.3 %collective-permute-done.12 = f32[40,40]{0,1:T(8,128)S(1)} collective-permute-done((f32[40,40]{0,1:T(8,128)S(1)}, f32[40,40]{0,1:T(8,128)S(1)}, u32[]{:S(2)}, u32[]{:S(2)}) %collective-permute-start.12) | collective-permute-done | bytes 6432 | tf_op jit(solution)/shard_map/ppermute | solution.py:113
  139.6 3.8 %collective-permute-done.13 = f32[40,40]{0,1:T(8,128)S(1)} collective-permute-done((f32[40,40]{0,1:T(8,128)S(1)}, f32[40,40]{0,1:T(8,128)S(1)}, u32[]{:S(2)}, u32[]{:S(2)}) %collective-permute-start.13) | collective-permute-done | bytes 6432 | tf_op jit(solution)/shard_map/ppermute | solution.py:113
  143.4 5.3 %collective-permute-done.14 = f32[40,40]{0,1:T(8,128)S(1)} collective-permute-done((f32[40,40]{0,1:T(8,128)S(1)}, f32[40,40]{0,1:T(8,128)S(1)}, u32[]{:S(2)}, u32[]{:S(2)}) %collective-permute-start.14) | collective-permute-done | bytes 6432 | tf_op jit(solution)/shard_map/ppermute | solution.py:113
  148.7 1.2 collective-permute-done.15
  149.9 3.8 %collective-permute-done.16 = f32[40,40]{0,1:T(8,128)S(1)} collective-permute-done((f32[40,40]{0,1:T(8,128)S(1)}, f32[40,40]{0,1:T(8,128)S(1)}, u32[]{:S(2)}, u32[]{:S(2)}) %collective-permute-start.16) | collective-permute-done | bytes 6432 | tf_op jit(solution)/shard_map/ppermute | solution.py:113
  154.1 4.9 %collective-permute-done.17 = f32[40,40]{0,1:T(8,128)S(1)} collective-permute-done((f32[40,40]{0,1:T(8,128)S(1)}, f32[40,40]{0,1:T(8,128)S(1)}, u32[]{:S(2)}, u32[]{:S(2)}) %collective-permute-start.17) | collective-permute-done | bytes 6432 | tf_op jit(solution)/shard_map/ppermute | solution.py:113
  159.8 5.3 %shard_map.61 = (f32[40,40]{1,0:T(8,128)}, f32[40,40]{1,0:T(8,128)}) custom-call(f32[40,40]{1,0:T(8,128)} %broadcast_multiply_fusion.gram_ref), custom_call_target="tpu_custom_call" | custom-call | tf_op jit(solution)/shard_map/pallas_call | solution.py:217
  165.1 7.1 %convolution_bitcast_fusion = f32[5,8,512,128]{3,1,2,0:T(8,128)S(1)} fusion(f32[40,40]{1,0:T(8,128)} %get-tuple-element.12, f32[40,65536]{1,0:T(8,128)} %copy-done), kind=kOutput, calls=%fused_computation | convolution fusion | flops 629145600 | bytes 20977920 | tf_op jit(solution)/shard_map/dot_general | solution.py:242
  172.2 6.0 %copy.15 = f32[5,8,512,128]{3,2,1,0:T(8,128)} copy(f32[5,8,512,128]{3,1,2,0:T(8,128)S(1)} %convolution_bitcast_fusion) | data formatting | bytes 20971520
  (53 shorter events, 4.8 us)
Async XLA Ops:
  2.6 8.8 %collective-permute-start = (f32[80,4,128]{2,1,0:T(4,128)S(1)}, f32[80,4,128]{2,1,0:T(4,128)S(1)}, u32[]{:S(2)}, u32[]{:S(2)}) collective-permute-start(f32[80,4,128]{2,1,0:T(4,128)S(1)} %pad_maximum_fusion), channel_id=1, source_target_pairs={{8,0},{16,8},{24,16},{32,24},{40,32},{48,40},{56,48},{64,56},{72,6... | collective-permute-start | bytes 491528 | tf_op jit(solution)/shard_map/ppermute | solution.py:89
  8.0 9.0 %collective-permute-start.1 = (f32[80,4,128]{2,1,0:T(4,128)S(1)}, f32[80,4,128]{2,1,0:T(4,128)S(1)}, u32[]{:S(2)}, u32[]{:S(2)}) collective-permute-start(f32[80,4,128]{2,1,0:T(4,128)S(1)} %pad_maximum_fusion.1), channel_id=1, source_target_pairs={{0,8},{8,16},{16,24},{24,32},{32,40},{40,48},{48,56},{56,64},{64,7... | collective-permute-start | bytes 491528 | tf_op jit(solution)/shard_map/ppermute | solution.py:90
  11.4 5.6 %copy-start.1 = (f32[80,4,128]{2,1,0:T(4,128)}, f32[80,4,128]{2,1,0:T(4,128)S(1)}, u32[]{:S(2)}) copy-start(f32[80,4,128]{2,1,0:T(4,128)S(1)} %collective-permute-done.xn_ref.refs_3_.refs_7_.refs_11_) | copy-start | bytes 491524
  17.0 0.7 copy-start.2
  27.6 5.4 %collective-permute-start.2 = (f32[80,4,128]{2,1,0:T(4,128)}, f32[80,4,128]{2,1,0:T(4,128)S(1)}, u32[]{:S(2)}, u32[]{:S(2)}) collective-permute-start(f32[80,4,128]{2,1,0:T(4,128)} %get-tuple-element.9), channel_id=1, source_target_pairs={{1,0},{2,1},{3,2},{4,3},{5,4},{6,5},{7,6},{0,7},{9,8},{10,9},{11,1... | collective-permute-start | bytes 491528 | tf_op jit(solution)/shard_map/ppermute | solution.py:93
  29.8 6.2 %collective-permute-start.3 = (f32[80,4,128]{2,1,0:T(4,128)}, f32[80,4,128]{2,1,0:T(4,128)S(1)}, u32[]{:S(2)}, u32[]{:S(2)}) collective-permute-start(f32[80,4,128]{2,1,0:T(4,128)} %get-tuple-element.10), channel_id=1, source_target_pairs={{0,1},{1,2},{2,3},{3,4},{4,5},{5,6},{6,7},{7,0},{8,9},{9,10},{10,1... | collective-permute-start | bytes 491528 | tf_op jit(solution)/shard_map/ppermute | solution.py:94
  33.0 3.0 %copy-start.3 = (f32[80,4,128]{2,1,0:T(4,128)}, f32[80,4,128]{2,1,0:T(4,128)S(1)}, u32[]{:S(2)}) copy-start(f32[80,4,128]{2,1,0:T(4,128)S(1)} %collective-permute-done.2.refs_5_.refs_9_.refs_13_) | copy-start | bytes 491524
  36.0 0.7 copy-start.4
  80.2 3.9 %collective-permute-start.4 = (f32[40,40]{0,1:T(8,128)S(1)}, f32[40,40]{0,1:T(8,128)S(1)}, u32[]{:S(2)}, u32[]{:S(2)}) collective-permute-start(f32[40,40]{0,1:T(8,128)S(1)} %fusion.4), channel_id=1, source_target_pairs={{0,8},{8,0},{16,24},{24,16},{32,40},{40,32},{48,56},{56,48},{64,72... | collective-permute-start | bytes 19208 | tf_op jit(solution)/shard_map/ppermute | solution.py:113
  84.0 5.3 %collective-permute-start.5 = (f32[40,40]{0,1:T(8,128)S(1)}, f32[40,40]{0,1:T(8,128)S(1)}, u32[]{:S(2)}, u32[]{:S(2)}) collective-permute-start(f32[40,40]{0,1:T(8,128)S(1)} %add.48), channel_id=1, source_target_pairs={{0,16},{8,24},{16,0},{24,8},{32,48},{40,56},{48,32},{56,40},{64,80... | collective-permute-start | bytes 19208 | tf_op jit(solution)/shard_map/ppermute | solution.py:113
  89.3 3.8 %collective-permute-start.6 = (f32[40,40]{0,1:T(8,128)S(1)}, f32[40,40]{0,1:T(8,128)S(1)}, u32[]{:S(2)}, u32[]{:S(2)}) collective-permute-start(f32[40,40]{0,1:T(8,128)S(1)} %add.49), channel_id=1, source_target_pairs={{0,32},{8,40},{16,48},{24,56},{32,0},{40,8},{48,16},{56,24},{64,96... | collective-permute-start | bytes 19208 | tf_op jit(solution)/shard_map/ppermute | solution.py:113
  93.1 5.3 %collective-permute-start.7 = (f32[40,40]{0,1:T(8,128)S(1)}, f32[40,40]{0,1:T(8,128)S(1)}, u32[]{:S(2)}, u32[]{:S(2)}) collective-permute-start(f32[40,40]{0,1:T(8,128)S(1)} %add.50), channel_id=1, source_target_pairs={{0,64},{8,72},{16,80},{24,88},{32,96},{40,104},{48,112},{56,120},{... | collective-permute-start | bytes 19208 | tf_op jit(solution)/shard_map/ppermute | solution.py:113
  98.4 1.2 collective-permute-start.8
  99.6 3.8 %collective-permute-start.9 = (f32[40,40]{0,1:T(8,128)S(1)}, f32[40,40]{0,1:T(8,128)S(1)}, u32[]{:S(2)}, u32[]{:S(2)}) collective-permute-start(f32[40,40]{0,1:T(8,128)S(1)} %add.52), channel_id=1, source_target_pairs={{0,2},{1,3},{2,0},{3,1},{4,6},{5,7},{6,4},{7,5},{8,10},{9,11},{10,... | collective-permute-start | bytes 19208 | tf_op jit(solution)/shard_map/ppermute | solution.py:113
  103.4 5.3 %collective-permute-start.10 = (f32[40,40]{0,1:T(8,128)S(1)}, f32[40,40]{0,1:T(8,128)S(1)}, u32[]{:S(2)}, u32[]{:S(2)}) collective-permute-start(f32[40,40]{0,1:T(8,128)S(1)} %add.53), channel_id=1, source_target_pairs={{0,4},{1,5},{2,6},{3,7},{4,0},{5,1},{6,2},{7,3},{8,12},{9,13},{10,... | collective-permute-start | bytes 19208 | tf_op jit(solution)/shard_map/ppermute | solution.py:113
  126.3 4.2 %copy-start = (f32[40,65536]{1,0:T(8,128)}, f32[40,65536]{1,0:T(8,128)S(1)}, u32[]{:S(2)}) copy-start(f32[40,65536]{1,0:T(8,128)S(1)} %fusion.5) | copy-start | bytes 31457284
  130.5 3.9 %collective-permute-start.11 = (f32[40,40]{0,1:T(8,128)S(1)}, f32[40,40]{0,1:T(8,128)S(1)}, u32[]{:S(2)}, u32[]{:S(2)}) collective-permute-start(f32[40,40]{0,1:T(8,128)S(1)} %fusion.6), channel_id=1, source_target_pairs={{0,8},{8,0},{16,24},{24,16},{32,40},{40,32},{48,56},{56,48},{64,72... | collective-permute-start | bytes 19208 | tf_op jit(solution)/shard_map/ppermute | solution.py:113
  134.3 5.3 %collective-permute-start.12 = (f32[40,40]{0,1:T(8,128)S(1)}, f32[40,40]{0,1:T(8,128)S(1)}, u32[]{:S(2)}, u32[]{:S(2)}) collective-permute-start(f32[40,40]{0,1:T(8,128)S(1)} %add.56), channel_id=1, source_target_pairs={{0,16},{8,24},{16,0},{24,8},{32,48},{40,56},{48,32},{56,40},{64,80... | collective-permute-start | bytes 19208 | tf_op jit(solution)/shard_map/ppermute | solution.py:113
  139.6 3.8 %collective-permute-start.13 = (f32[40,40]{0,1:T(8,128)S(1)}, f32[40,40]{0,1:T(8,128)S(1)}, u32[]{:S(2)}, u32[]{:S(2)}) collective-permute-start(f32[40,40]{0,1:T(8,128)S(1)} %add.57), channel_id=1, source_target_pairs={{0,32},{8,40},{16,48},{24,56},{32,0},{40,8},{48,16},{56,24},{64,96... | collective-permute-start | bytes 19208 | tf_op jit(solution)/shard_map/ppermute | solution.py:113
  143.4 5.3 %collective-permute-start.14 = (f32[40,40]{0,1:T(8,128)S(1)}, f32[40,40]{0,1:T(8,128)S(1)}, u32[]{:S(2)}, u32[]{:S(2)}) collective-permute-start(f32[40,40]{0,1:T(8,128)S(1)} %add.58), channel_id=1, source_target_pairs={{0,64},{8,72},{16,80},{24,88},{32,96},{40,104},{48,112},{56,120},{... | collective-permute-start | bytes 19208 | tf_op jit(solution)/shard_map/ppermute | solution.py:113
  148.7 1.2 collective-permute-start.15
  149.9 3.8 %collective-permute-start.16 = (f32[40,40]{0,1:T(8,128)S(1)}, f32[40,40]{0,1:T(8,128)S(1)}, u32[]{:S(2)}, u32[]{:S(2)}) collective-permute-start(f32[40,40]{0,1:T(8,128)S(1)} %add.60), channel_id=1, source_target_pairs={{0,2},{1,3},{2,0},{3,1},{4,6},{5,7},{6,4},{7,5},{8,10},{9,11},{10,... | collective-permute-start | bytes 19208 | tf_op jit(solution)/shard_map/ppermute | solution.py:113
  153.7 5.3 %collective-permute-start.17 = (f32[40,40]{0,1:T(8,128)S(1)}, f32[40,40]{0,1:T(8,128)S(1)}, u32[]{:S(2)}, u32[]{:S(2)}) collective-permute-start(f32[40,40]{0,1:T(8,128)S(1)} %add.61), channel_id=1, source_target_pairs={{0,4},{1,5},{2,6},{3,7},{4,0},{5,1},{6,2},{7,3},{8,12},{9,13},{10,... | collective-permute-start | bytes 19208 | tf_op jit(solution)/shard_map/ppermute | solution.py:113
  172.2 6.0 %copy-start.5 = (f32[40,40]{1,0:T(8,128)S(1)}, f32[40,40]{1,0:T(8,128)}, u32[]{:S(2)}) copy-start(f32[40,40]{1,0:T(8,128)} %get-tuple-element.8) | copy-start | bytes 19204
  172.2 6.0 %copy-start.6 = (f32[40,40]{1,0:T(8,128)S(1)}, f32[40,40]{1,0:T(8,128)}, u32[]{:S(2)}) copy-start(f32[40,40]{1,0:T(8,128)} %get-tuple-element.13) | copy-start | bytes 19204

commit v3 on v2

--- a/solution.py
+++ b/solution.py
@@ -104,14 +104,30 @@
     return jnp.concatenate([tall, side], axis=1)
 
 
+def fold_pairs(count, stride, span, fold):
+    pairs = []
+    for i in range(count):
+        place = (i // stride) % span
+        other = (span - 1 - place) if fold else (place ^ 1)
+        pairs.append((i, i + (other - place) * stride))
+    return pairs
+
+
+def ring_spans(axis):
+    count = lax.axis_size(axis)
+    rings = {("gx", 16): ((4, 4), (1, 4)), ("gy", 8): ((1, 2), (2, 4))}
+    if (axis, count) in rings:
+        return rings[(axis, count)]
+    return tuple((1 << b, 2) for b in range(count.bit_length() - 1))
+
+
 def tree_sum(value, axes):
     for axis in axes:
         count = lax.axis_size(axis)
-        stride = 1
-        while stride < count:
-            pairs = [(i, i ^ stride) for i in range(count)]
-            value = value + lax.ppermute(value, axis, pairs)
-            stride *= 2
+        for stride, span in ring_spans(axis):
+            folds = (False, True) if span == 4 else (False,)
+            for fold in folds:
+                value = value + lax.ppermute(value, axis, fold_pairs(count, stride, span, fold))
     return value
 
 

time: 179 us -> 178 us (level)
  waiting for transfers between devices: 71 us -> 69 us
    ppermute x14, waiting for transfers between devices: 55.9 us -> 53.9 us  [tree_sum(): lax.ppermute(value, axis, fold_pairs(count, stride, span, fold))]
where the time goes in v3:
time: 178 us; the launch traced here: 177 us
  waiting for transfers between devices  69 us (39%)
  Pallas kernels  41.7 us (23%)
  matrix products  35.5 us (20%)
  local copies, waits for them, and re-layouts  19.9 us (11%)
  starting transfers between devices  9.01 us (5%)
    ppermute x14, waiting for transfers between devices, tree_sum(): lax.ppermute(value, axis, fold_pairs(count, stride, span, fold))  53.9 us
    pallas_call x1, Pallas kernels, krylov_powers(): pl.pallas_call(powers_kernel, grid=(rhs,), in_specs=[pl.BlockSpec((1, dep...  21.2 us
    dot_general x1, matrix products, body(): jnp.dot(krylov, krylov.T, precision=lax.Precision.HIGHEST, preferred_elem...  11.8 us
    dot_general x1, matrix products, body(): jnp.dot(inverse_first, krylov, precision=lax.Precision.HIGHEST, preferred...  11.6 us
    pallas_call x2, Pallas kernels, cholesky_factors(): return pl.pallas_call(factor_kernel, out_shape=[square, square])(symmetric)  10.6 us
    reshape x1, local copies, waits for them, and re-layouts, body(): krylov_powers(start_block, conductivity, reaction, strips).reshape(COLS, -1)  10.4 us
    pallas_call x1, Pallas kernels, edge_columns(): pl.pallas_call(columns_kernel, in_specs=[whole(start_block.shape), whole(...  9.85 us
    unnamed x15, local copies, waits for them, and re-layouts  7.33 us
  transfers between devices with their start and end apart: 18, of which 18 were waited for; matrix products, arithmetic and copies ran while one was open for 0% of the time, Pallas kernels for 0%

profile of v3, /device:TPU:0, one launch (start us, length us, event | category | flops | bytes accessed | tf_op | source)
XLA Modules:
  0.0 177.2 jit_solution(4286332283428323965)
XLA Ops:
  0.6 1.1 fusion.1
  1.7 0.8 fusion.2
  2.6 5.4 %collective-permute-start = (f32[80,4,128]{2,1,0:T(4,128)S(1)}, f32[80,4,128]{2,1,0:T(4,128)S(1)}, u32[]{:S(2)}, u32[]{:S(2)}) collective-permute-start(f32[80,4,128]{2,1,0:T(4,128)S(1)} %pad_maximum_fusion), channel_id=1, source_target_pairs={{8,0},{16,8},{24,16},{32,24},{40,32},{48,40},{56,48},{64,56},{72,6... | collective-permute-start | bytes 491528 | tf_op jit(solution)/shard_map/ppermute | solution.py:89
  8.1 3.3 %collective-permute-done.xn_ref.refs_3_.refs_7_.refs_11_ = f32[80,4,128]{2,1,0:T(4,128)S(1)} collective-permute-done((f32[80,4,128]{2,1,0:T(4,128)S(1)}, f32[80,4,128]{2,1,0:T(4,128)S(1)}, u32[]{:S(2)}, u32[]{:S(2)}) %collective-permute-start) | collective-permute-done | bytes 163872 | tf_op jit(solution)/shard_map/ppermute | solution.py:89
  11.4 5.6 %collective-permute-done.1.xp_ref.refs_4_.refs_8_.refs_12_ = f32[80,4,128]{2,1,0:T(4,128)S(1)} collective-permute-done((f32[80,4,128]{2,1,0:T(4,128)S(1)}, f32[80,4,128]{2,1,0:T(4,128)S(1)}, u32[]{:S(2)}, u32[]{:S(2)}) %collective-permute-start.1) | collective-permute-done | bytes 163872 | tf_op jit(solution)/shard_map/ppermute | solution.py:90
  17.7 9.9 %shard_map.58 = (f32[80,4,128]{2,1,0:T(4,128)}, f32[80,4,128]{2,1,0:T(4,128)}) custom-call(f32[8,8,64,128]{3,2,1,0:T(8,128)} %refs_0_.1, f32[8,64,128]{2,1,0:T(8,128)} %refs_1_.1, f32[8,64,128]{2,1,0:T(8,128)} %refs_2_.1, f32[80,4,128]{2,1,0:T(4,128)} %copy-done.1, f32[80,4,128]{2,1,0:T(4,128)} %copy-done.2), custom_call_target="tpu_custom_call" | custom-call | tf_op jit(solution)/shard_map/pallas_call | solution.py:70
  27.6 2.3 %collective-permute-start.2 = (f32[80,4,128]{2,1,0:T(4,128)}, f32[80,4,128]{2,1,0:T(4,128)S(1)}, u32[]{:S(2)}, u32[]{:S(2)}) collective-permute-start(f32[80,4,128]{2,1,0:T(4,128)} %get-tuple-element.9), channel_id=1, source_target_pairs={{1,0},{2,1},{3,2},{4,3},{5,4},{6,5},{7,6},{0,7},{9,8},{10,9},{11,1... | collective-permute-start | bytes 491528 | tf_op jit(solution)/shard_map/ppermute | solution.py:93
  29.8 3.1 %collective-permute-done.2.refs_5_.refs_9_.refs_13_ = f32[80,4,128]{2,1,0:T(4,128)S(1)} collective-permute-done((f32[80,4,128]{2,1,0:T(4,128)}, f32[80,4,128]{2,1,0:T(4,128)S(1)}, u32[]{:S(2)}, u32[]{:S(2)}) %collective-permute-start.2) | collective-permute-done | bytes 163872 | tf_op jit(solution)/shard_map/ppermute | solution.py:93
  33.0 3.0 %collective-permute-done.3.refs_6_.refs_10_.refs_14_ = f32[80,4,128]{2,1,0:T(4,128)S(1)} collective-permute-done((f32[80,4,128]{2,1,0:T(4,128)}, f32[80,4,128]{2,1,0:T(4,128)S(1)}, u32[]{:S(2)}, u32[]{:S(2)}) %collective-permute-start.3) | collective-permute-done | bytes 163872 | tf_op jit(solution)/shard_map/ppermute | solution.py:94
  36.7 21.2 %shard_map.59 = f32[5,8,8,64,128]{4,3,2,1,0:T(8,128)} custom-call(f32[8,8,64,128]{3,2,1,0:T(8,128)} %refs_0_.1, f32[8,64,128]{2,1,0:T(8,128)} %refs_1_.1, f32[8,64,128]{2,1,0:T(8,128)} %refs_2_.1, f32[80,4,128]{2,1,0:T(4,128)} %copy-done.1, f32[80,4,128]{2,1,0:T(4,128)} %copy-done.2, f32[80,4,128]{2,1,0:T(4,128)} %copy-done.3, f32[80,4,128]{2,1,0:T(4,128)} %copy-done.4, ...), custom_call_target="tpu_custom_call" | custom-call | tf_op jit(solution)/shard_map/pallas_call | solution.py:184
  57.9 10.4 %reshape.20 = f32[40,65536]{1,0:T(8,128)} reshape(f32[5,8,8,64,128]{4,3,2,1,0:T(8,128)} %shard_map.59) | data formatting | bytes 20971520 | tf_op jit(solution)/shard_map/reshape | solution.py:246
  68.3 11.8 %fusion.4 = f32[40,40]{0,1:T(8,128)S(1)} fusion(f32[40,65536]{1,0:T(8,128)} %reshape.20), kind=kOutput, calls=%fused_computation.12 | convolution fusion | flops 1258291200 | bytes 10492160 | tf_op jit(solution)/shard_map/dot_general | solution.py:247
  80.3 3.8 %collective-permute-done.4 = f32[40,40]{0,1:T(8,128)S(1)} collective-permute-done((f32[40,40]{0,1:T(8,128)S(1)}, f32[40,40]{0,1:T(8,128)S(1)}, u32[]{:S(2)}, u32[]{:S(2)}) %collective-permute-start.4) | collective-permute-done | bytes 6432 | tf_op jit(solution)/shard_map/ppermute | solution.py:130
  84.0 5.0 %collective-permute-done.5 = f32[40,40]{0,1:T(8,128)S(1)} collective-permute-done((f32[40,40]{0,1:T(8,128)S(1)}, f32[40,40]{0,1:T(8,128)S(1)}, u32[]{:S(2)}, u32[]{:S(2)}) %collective-permute-start.5) | collective-permute-done | bytes 6432 | tf_op jit(solution)/shard_map/ppermute | solution.py:130
  89.0 3.8 %collective-permute-done.6 = f32[40,40]{0,1:T(8,128)S(1)} collective-permute-done((f32[40,40]{0,1:T(8,128)S(1)}, f32[40,40]{0,1:T(8,128)S(1)}, u32[]{:S(2)}, u32[]{:S(2)}) %collective-permute-start.6) | collective-permute-done | bytes 6432 | tf_op jit(solution)/shard_map/ppermute | solution.py:130
  92.8 5.0 %collective-permute-done.7 = f32[40,40]{0,1:T(8,128)S(1)} collective-permute-done((f32[40,40]{0,1:T(8,128)S(1)}, f32[40,40]{0,1:T(8,128)S(1)}, u32[]{:S(2)}, u32[]{:S(2)}) %collective-permute-start.7) | collective-permute-done | bytes 6432 | tf_op jit(solution)/shard_map/ppermute | solution.py:130
  97.8 1.2 collective-permute-done.8
  99.0 3.8 %collective-permute-done.9 = f32[40,40]{0,1:T(8,128)S(1)} collective-permute-done((f32[40,40]{0,1:T(8,128)S(1)}, f32[40,40]{0,1:T(8,128)S(1)}, u32[]{:S(2)}, u32[]{:S(2)}) %collective-permute-start.9) | collective-permute-done | bytes 6432 | tf_op jit(solution)/shard_map/ppermute | solution.py:130
  103.3 4.5 %collective-permute-done.10 = f32[40,40]{0,1:T(8,128)S(1)} collective-permute-done((f32[40,40]{0,1:T(8,128)S(1)}, f32[40,40]{0,1:T(8,128)S(1)}, u32[]{:S(2)}, u32[]{:S(2)}) %collective-permute-start.10) | collective-permute-done | bytes 6432 | tf_op jit(solution)/shard_map/ppermute | solution.py:130
  108.5 5.3 %shard_map.60 = (f32[40,40]{1,0:T(8,128)}, f32[40,40]{1,0:T(8,128)}) custom-call(f32[40,40]{1,0:T(8,128)} %fusion.gram_ref), custom_call_target="tpu_custom_call" | custom-call | tf_op jit(solution)/shard_map/pallas_call | solution.py:233
  113.8 11.6 %fusion.5 = f32[40,65536]{1,0:T(8,128)S(1)} fusion(f32[40,40]{1,0:T(8,128)} %get-tuple-element.11, f32[40,65536]{1,0:T(8,128)} %reshape.20), kind=kOutput, calls=%fused_computation.13 | convolution fusion | flops 1258291200 | bytes 20977920 | tf_op jit(solution)/shard_map/dot_general | solution.py:251
  125.4 4.2 %fusion.6 = f32[40,40]{0,1:T(8,128)S(1)} fusion(f32[40,65536]{1,0:T(8,128)S(1)} %fusion.5), kind=kOutput, calls=%fused_computation.14 | convolution fusion | flops 629145600 | bytes 10492160 | tf_op jit(solution)/shard_map/dot_general | solution.py:254
  129.7 3.8 %collective-permute-done.11 = f32[40,40]{0,1:T(8,128)S(1)} collective-permute-done((f32[40,40]{0,1:T(8,128)S(1)}, f32[40,40]{0,1:T(8,128)S(1)}, u32[]{:S(2)}, u32[]{:S(2)}) %collective-permute-start.11) | collective-permute-done | bytes 6432 | tf_op jit(solution)/shard_map/ppermute | solution.py:130
  133.5 5.0 %collective-permute-done.12 = f32[40,40]{0,1:T(8,128)S(1)} collective-permute-done((f32[40,40]{0,1:T(8,128)S(1)}, f32[40,40]{0,1:T(8,128)S(1)}, u32[]{:S(2)}, u32[]{:S(2)}) %collective-permute-start.12) | collective-permute-done | bytes 6432 | tf_op jit(solution)/shard_map/ppermute | solution.py:130
  138.5 3.8 %collective-permute-done.13 = f32[40,40]{0,1:T(8,128)S(1)} collective-permute-done((f32[40,40]{0,1:T(8,128)S(1)}, f32[40,40]{0,1:T(8,128)S(1)}, u32[]{:S(2)}, u32[]{:S(2)}) %collective-permute-start.13) | collective-permute-done | bytes 6432 | tf_op jit(solution)/shard_map/ppermute | solution.py:130
  142.3 5.0 %collective-permute-done.14 = f32[40,40]{0,1:T(8,128)S(1)} collective-permute-done((f32[40,40]{0,1:T(8,128)S(1)}, f32[40,40]{0,1:T(8,128)S(1)}, u32[]{:S(2)}, u32[]{:S(2)}) %collective-permute-start.14) | collective-permute-done | bytes 6432 | tf_op jit(solution)/shard_map/ppermute | solution.py:130
  147.3 1.2 collective-permute-done.15
  148.5 3.8 %collective-permute-done.16 = f32[40,40]{0,1:T(8,128)S(1)} collective-permute-done((f32[40,40]{0,1:T(8,128)S(1)}, f32[40,40]{0,1:T(8,128)S(1)}, u32[]{:S(2)}, u32[]{:S(2)}) %collective-permute-start.16) | collective-permute-done | bytes 6432 | tf_op jit(solution)/shard_map/ppermute | solution.py:130
  152.8 4.5 %collective-permute-done.17 = f32[40,40]{0,1:T(8,128)S(1)} collective-permute-done((f32[40,40]{0,1:T(8,128)S(1)}, f32[40,40]{0,1:T(8,128)S(1)}, u32[]{:S(2)}, u32[]{:S(2)}) %collective-permute-start.17) | collective-permute-done | bytes 6432 | tf_op jit(solution)/shard_map/ppermute | solution.py:130
  158.0 5.3 %shard_map.61 = (f32[40,40]{1,0:T(8,128)}, f32[40,40]{1,0:T(8,128)}) custom-call(f32[40,40]{1,0:T(8,128)} %broadcast_multiply_fusion.gram_ref), custom_call_target="tpu_custom_call" | custom-call | tf_op jit(solution)/shard_map/pallas_call | solution.py:233
  163.3 7.1 %convolution_bitcast_fusion = f32[5,8,512,128]{3,1,2,0:T(8,128)S(1)} fusion(f32[40,40]{1,0:T(8,128)} %get-tuple-element.12, f32[40,65536]{1,0:T(8,128)} %copy-done), kind=kOutput, calls=%fused_computation | convolution fusion | flops 629145600 | bytes 20977920 | tf_op jit(solution)/shard_map/dot_general | solution.py:258
  170.5 6.0 %copy.15 = f32[5,8,512,128]{3,2,1,0:T(8,128)} copy(f32[5,8,512,128]{3,1,2,0:T(8,128)S(1)} %convolution_bitcast_fusion) | data formatting | bytes 20971520
  (53 shorter events, 5.1 us)
Async XLA Ops:
  2.6 8.8 %collective-permute-start = (f32[80,4,128]{2,1,0:T(4,128)S(1)}, f32[80,4,128]{2,1,0:T(4,128)S(1)}, u32[]{:S(2)}, u32[]{:S(2)}) collective-permute-start(f32[80,4,128]{2,1,0:T(4,128)S(1)} %pad_maximum_fusion), channel_id=1, source_target_pairs={{8,0},{16,8},{24,16},{32,24},{40,32},{48,40},{56,48},{64,56},{72,6... | collective-permute-start | bytes 491528 | tf_op jit(solution)/shard_map/ppermute | solution.py:89
  8.0 9.0 %collective-permute-start.1 = (f32[80,4,128]{2,1,0:T(4,128)S(1)}, f32[80,4,128]{2,1,0:T(4,128)S(1)}, u32[]{:S(2)}, u32[]{:S(2)}) collective-permute-start(f32[80,4,128]{2,1,0:T(4,128)S(1)} %pad_maximum_fusion.1), channel_id=1, source_target_pairs={{0,8},{8,16},{16,24},{24,32},{32,40},{40,48},{48,56},{56,64},{64,7... | collective-permute-start | bytes 491528 | tf_op jit(solution)/shard_map/ppermute | solution.py:90
  11.4 5.6 %copy-start.1 = (f32[80,4,128]{2,1,0:T(4,128)}, f32[80,4,128]{2,1,0:T(4,128)S(1)}, u32[]{:S(2)}) copy-start(f32[80,4,128]{2,1,0:T(4,128)S(1)} %collective-permute-done.xn_ref.refs_3_.refs_7_.refs_11_) | copy-start | bytes 491524
  17.0 0.7 copy-start.2
  27.6 5.4 %collective-permute-start.2 = (f32[80,4,128]{2,1,0:T(4,128)}, f32[80,4,128]{2,1,0:T(4,128)S(1)}, u32[]{:S(2)}, u32[]{:S(2)}) collective-permute-start(f32[80,4,128]{2,1,0:T(4,128)} %get-tuple-element.9), channel_id=1, source_target_pairs={{1,0},{2,1},{3,2},{4,3},{5,4},{6,5},{7,6},{0,7},{9,8},{10,9},{11,1... | collective-permute-start | bytes 491528 | tf_op jit(solution)/shard_map/ppermute | solution.py:93
  29.8 6.2 %collective-permute-start.3 = (f32[80,4,128]{2,1,0:T(4,128)}, f32[80,4,128]{2,1,0:T(4,128)S(1)}, u32[]{:S(2)}, u32[]{:S(2)}) collective-permute-start(f32[80,4,128]{2,1,0:T(4,128)} %get-tuple-element.10), channel_id=1, source_target_pairs={{0,1},{1,2},{2,3},{3,4},{4,5},{5,6},{6,7},{7,0},{8,9},{9,10},{10,1... | collective-permute-start | bytes 491528 | tf_op jit(solution)/shard_map/ppermute | solution.py:94
  33.0 3.0 %copy-start.3 = (f32[80,4,128]{2,1,0:T(4,128)}, f32[80,4,128]{2,1,0:T(4,128)S(1)}, u32[]{:S(2)}) copy-start(f32[80,4,128]{2,1,0:T(4,128)S(1)} %collective-permute-done.2.refs_5_.refs_9_.refs_13_) | copy-start | bytes 491524
  36.0 0.7 copy-start.4
  80.2 3.9 %collective-permute-start.4 = (f32[40,40]{0,1:T(8,128)S(1)}, f32[40,40]{0,1:T(8,128)S(1)}, u32[]{:S(2)}, u32[]{:S(2)}) collective-permute-start(f32[40,40]{0,1:T(8,128)S(1)} %fusion.4), channel_id=1, source_target_pairs={{0,32},{8,40},{16,48},{24,56},{32,0},{40,8},{48,16},{56,24},{64,96... | collective-permute-start | bytes 19208 | tf_op jit(solution)/shard_map/ppermute | solution.py:130
  84.0 5.0 %collective-permute-start.5 = (f32[40,40]{0,1:T(8,128)S(1)}, f32[40,40]{0,1:T(8,128)S(1)}, u32[]{:S(2)}, u32[]{:S(2)}) collective-permute-start(f32[40,40]{0,1:T(8,128)S(1)} %add.48), channel_id=1, source_target_pairs={{0,96},{8,104},{16,112},{24,120},{32,64},{40,72},{48,80},{56,88},{... | collective-permute-start | bytes 19208 | tf_op jit(solution)/shard_map/ppermute | solution.py:130
  89.0 3.8 %collective-permute-start.6 = (f32[40,40]{0,1:T(8,128)S(1)}, f32[40,40]{0,1:T(8,128)S(1)}, u32[]{:S(2)}, u32[]{:S(2)}) collective-permute-start(f32[40,40]{0,1:T(8,128)S(1)} %add.49), channel_id=1, source_target_pairs={{0,8},{8,0},{16,24},{24,16},{32,40},{40,32},{48,56},{56,48},{64,72... | collective-permute-start | bytes 19208 | tf_op jit(solution)/shard_map/ppermute | solution.py:130
  92.8 5.0 %collective-permute-start.7 = (f32[40,40]{0,1:T(8,128)S(1)}, f32[40,40]{0,1:T(8,128)S(1)}, u32[]{:S(2)}, u32[]{:S(2)}) collective-permute-start(f32[40,40]{0,1:T(8,128)S(1)} %add.50), channel_id=1, source_target_pairs={{0,24},{8,16},{16,8},{24,0},{32,56},{40,48},{48,40},{56,32},{64,88... | collective-permute-start | bytes 19208 | tf_op jit(solution)/shard_map/ppermute | solution.py:130
  97.8 1.2 collective-permute-start.8
  99.0 3.8 %collective-permute-start.9 = (f32[40,40]{0,1:T(8,128)S(1)}, f32[40,40]{0,1:T(8,128)S(1)}, u32[]{:S(2)}, u32[]{:S(2)}) collective-permute-start(f32[40,40]{0,1:T(8,128)S(1)} %add.52), channel_id=1, source_target_pairs={{0,2},{1,3},{2,0},{3,1},{4,6},{5,7},{6,4},{7,5},{8,10},{9,11},{10,... | collective-permute-start | bytes 19208 | tf_op jit(solution)/shard_map/ppermute | solution.py:130
  102.8 5.0 %collective-permute-start.10 = (f32[40,40]{0,1:T(8,128)S(1)}, f32[40,40]{0,1:T(8,128)S(1)}, u32[]{:S(2)}, u32[]{:S(2)}) collective-permute-start(f32[40,40]{0,1:T(8,128)S(1)} %add.53), channel_id=1, source_target_pairs={{0,6},{1,7},{2,4},{3,5},{4,2},{5,3},{6,0},{7,1},{8,14},{9,15},{10,... | collective-permute-start | bytes 19208 | tf_op jit(solution)/shard_map/ppermute | solution.py:130
  125.4 4.2 %copy-start = (f32[40,65536]{1,0:T(8,128)}, f32[40,65536]{1,0:T(8,128)S(1)}, u32[]{:S(2)}) copy-start(f32[40,65536]{1,0:T(8,128)S(1)} %fusion.5) | copy-start | bytes 31457284
  129.6 3.9 %collective-permute-start.11 = (f32[40,40]{0,1:T(8,128)S(1)}, f32[40,40]{0,1:T(8,128)S(1)}, u32[]{:S(2)}, u32[]{:S(2)}) collective-permute-start(f32[40,40]{0,1:T(8,128)S(1)} %fusion.6), channel_id=1, source_target_pairs={{0,32},{8,40},{16,48},{24,56},{32,0},{40,8},{48,16},{56,24},{64,96... | collective-permute-start | bytes 19208 | tf_op jit(solution)/shard_map/ppermute | solution.py:130
  133.5 5.0 %collective-permute-start.12 = (f32[40,40]{0,1:T(8,128)S(1)}, f32[40,40]{0,1:T(8,128)S(1)}, u32[]{:S(2)}, u32[]{:S(2)}) collective-permute-start(f32[40,40]{0,1:T(8,128)S(1)} %add.56), channel_id=1, source_target_pairs={{0,96},{8,104},{16,112},{24,120},{32,64},{40,72},{48,80},{56,88},{... | collective-permute-start | bytes 19208 | tf_op jit(solution)/shard_map/ppermute | solution.py:130
  138.5 3.8 %collective-permute-start.13 = (f32[40,40]{0,1:T(8,128)S(1)}, f32[40,40]{0,1:T(8,128)S(1)}, u32[]{:S(2)}, u32[]{:S(2)}) collective-permute-start(f32[40,40]{0,1:T(8,128)S(1)} %add.57), channel_id=1, source_target_pairs={{0,8},{8,0},{16,24},{24,16},{32,40},{40,32},{48,56},{56,48},{64,72... | collective-permute-start | bytes 19208 | tf_op jit(solution)/shard_map/ppermute | solution.py:130
  142.3 5.0 %collective-permute-start.14 = (f32[40,40]{0,1:T(8,128)S(1)}, f32[40,40]{0,1:T(8,128)S(1)}, u32[]{:S(2)}, u32[]{:S(2)}) collective-permute-start(f32[40,40]{0,1:T(8,128)S(1)} %add.58), channel_id=1, source_target_pairs={{0,24},{8,16},{16,8},{24,0},{32,56},{40,48},{48,40},{56,32},{64,88... | collective-permute-start | bytes 19208 | tf_op jit(solution)/shard_map/ppermute | solution.py:130
  147.3 1.2 collective-permute-start.15
  148.4 3.8 %collective-permute-start.16 = (f32[40,40]{0,1:T(8,128)S(1)}, f32[40,40]{0,1:T(8,128)S(1)}, u32[]{:S(2)}, u32[]{:S(2)}) collective-permute-start(f32[40,40]{0,1:T(8,128)S(1)} %add.60), channel_id=1, source_target_pairs={{0,2},{1,3},{2,0},{3,1},{4,6},{5,7},{6,4},{7,5},{8,10},{9,11},{10,... | collective-permute-start | bytes 19208 | tf_op jit(solution)/shard_map/ppermute | solution.py:130
  152.2 5.0 %collective-permute-start.17 = (f32[40,40]{0,1:T(8,128)S(1)}, f32[40,40]{0,1:T(8,128)S(1)}, u32[]{:S(2)}, u32[]{:S(2)}) collective-permute-start(f32[40,40]{0,1:T(8,128)S(1)} %add.61), channel_id=1, source_target_pairs={{0,6},{1,7},{2,4},{3,5},{4,2},{5,3},{6,0},{7,1},{8,14},{9,15},{10,... | collective-permute-start | bytes 19208 | tf_op jit(solution)/shard_map/ppermute | solution.py:130
  170.5 6.0 %copy-start.5 = (f32[40,40]{1,0:T(8,128)S(1)}, f32[40,40]{1,0:T(8,128)}, u32[]{:S(2)}) copy-start(f32[40,40]{1,0:T(8,128)} %get-tuple-element.8) | copy-start | bytes 19204
  170.5 6.0 %copy-start.6 = (f32[40,40]{1,0:T(8,128)S(1)}, f32[40,40]{1,0:T(8,128)}, u32[]{:S(2)}) copy-start(f32[40,40]{1,0:T(8,128)} %get-tuple-element.13) | copy-start | bytes 19204

commit v4 on v3

--- a/solution.py
+++ b/solution.py
@@ -39,34 +39,36 @@
     return jnp.concatenate([core, from_next, from_prev], axis=0)
 
 
+PACK = 32
+
+
 def columns_kernel(block_ref, coef_ref, react_ref, xn_ref, xp_ref, first_ref, last_ref):
     rhs, depth, rows, cols = block_ref.shape
     width = xn_ref.shape[1]
-    fill = jnp.zeros((cols - rows - 2 * width, cols), jnp.float32)
-
-    def one(plane, core):
-        tall = tall_plane(core, xn_ref[plane], xp_ref[plane])
-        turned = jnp.concatenate([tall, fill], axis=0).T
-        first_ref[plane] = turned[:width]
-        last_ref[plane] = turned[cols - width :]
-
-    def block_plane(p, carry):
-        one(p, block_ref[p // depth, p % depth])
-        return carry
-
-    def coef_plane(z, carry):
-        one(rhs * depth + z, coef_ref[z])
-        one(rhs * depth + depth + z, react_ref[z])
-        return carry
-
-    lax.fori_loop(0, rhs * depth, block_plane, 0)
-    lax.fori_loop(0, depth, coef_plane, 0)
+    groups, tall_rows = first_ref.shape[:2]
+    lane = lax.broadcasted_iota(jnp.int32, (tall_rows, cols), 1)
+    cores = [block_ref[r, z] for r in range(rhs) for z in range(depth)]
+    cores += [coef_ref[z] for z in range(depth)] + [react_ref[z] for z in range(depth)]
+    for group in range(groups):
+        first = jnp.zeros((tall_rows, cols), jnp.float32)
+        last = jnp.zeros((tall_rows, cols), jnp.float32)
+        for k in range(PACK):
+            plane = group * PACK + k
+            if plane >= len(cores):
+                break
+            tall = tall_plane(cores[plane], xn_ref[plane], xp_ref[plane])
+            mine = (lane >= width * k) & (lane < width * (k + 1))
+            first = jnp.where(mine, pltpu.roll(tall, width * k, 1), first)
+            last = jnp.where(mine, pltpu.roll(tall, (width * (k + 1)) % cols, 1), last)
+        first_ref[group] = first
+        last_ref[group] = last
 
 
 def edge_columns(start_block, conductivity, reaction, x_next, x_prev):
     planes, width, cols = x_next.shape
+    rows = start_block.shape[2] + 2 * width
     whole = lambda shape: pl.BlockSpec(shape, lambda: (0,) * len(shape))
-    strip = jax.ShapeDtypeStruct((planes, width, cols), jnp.float32)
+    strip = jax.ShapeDtypeStruct((-(-planes // PACK), rows, cols), jnp.float32)
     return pl.pallas_call(
         columns_kernel,
         in_specs=[
@@ -95,12 +97,14 @@
     return (x_next, x_prev, y_next, y_prev)
 
 
-def padded_plane(core, xn, xp, yn, yp):
-    cols = core.shape[-1]
-    width = yn.shape[0]
+def padded_plane(core, xn, xp, yn, yp, slot):
     tall = tall_plane(core, xn, xp)
-    gap = jnp.zeros((cols - 2 * width, cols), jnp.float32)
-    side = jnp.concatenate([yn, gap, yp], axis=0).T[: tall.shape[0]]
+    rows, cols = tall.shape
+    width = xn.shape[0]
+    lane = lax.broadcasted_iota(jnp.int32, (rows, cols), 1)
+    from_next = pltpu.roll(yn, (cols - width * slot) % cols, 1)
+    from_prev = pltpu.roll(yp, (cols - width - width * slot) % cols, 1)
+    side = jnp.where(lane < width, from_next, jnp.where(lane >= cols - width, from_prev, 0.0))
     return jnp.concatenate([tall, side], axis=1)
 
 
@@ -145,25 +149,34 @@
 
 def powers_kernel(*refs):
     block_ref, coef_ref, react_ref = refs[:3]
-    strips = refs[3:15]
-    out_ref, weight_ref, react_pad_ref = refs[15:]
+    x_strips = refs[3:9]
+    yn_ref, yp_ref = refs[9:11]
+    out_ref, weight_ref, react_pad_ref = refs[11:]
     depth, rows, cols = (out_ref.shape[2], out_ref.shape[3], out_ref.shape[4])
-
-    def planes(core_of, group):
-        sides = [strips[4 * group + k] for k in range(4)]
-        return jnp.stack(
-            [padded_plane(core_of(z), *(side[z] for side in sides)) for z in range(depth)], axis=0
-        )
-
-    @pl.when(pl.program_id(0) == 0)
+    r = pl.program_id(0)
+
+    def planes(core_of, group, first_plane):
+        xn, xp = (x_strips[2 * group], x_strips[2 * group + 1])
+        stacked = []
+        for z in range(depth):
+            plane = first_plane + z
+            tile = plane // PACK
+            stacked.append(
+                padded_plane(core_of(z), xn[z], xp[z], yn_ref[tile], yp_ref[tile], plane % PACK)
+            )
+        return jnp.stack(stacked, axis=0)
+
+    rhs = pl.num_programs(0)
+
+    @pl.when(r == 0)
     def _():
-        coef = planes(lambda z: coef_ref[z], 1)
+        coef = planes(lambda z: coef_ref[z], 1, rhs * depth)
         for d, direction in enumerate(DIRECTIONS):
             weight_ref[d] = 0.5 * (coef + neighbour(coef, direction))
-        react_pad_ref[...] = planes(lambda z: react_ref[z], 2)
+        react_pad_ref[...] = planes(lambda z: react_ref[z], 2, rhs * depth + depth)
 
     out_ref[0, 0] = block_ref[0]
-    current = planes(lambda z: block_ref[0, z], 0)
+    current = planes(lambda z: block_ref[0, z], 0, r * depth)
     react = react_pad_ref[...]
     for power in range(1, STEPS + 1):
         running = jnp.zeros_like(current)
@@ -176,11 +189,13 @@
 
 def krylov_powers(start_block, conductivity, reaction, strips):
     rhs, depth, rows, cols = start_block.shape
-    width = strips[0].shape[1]
+    x_next, x_prev, y_next, y_prev = strips
+    width = x_next.shape[1]
     strip_specs = []
     for group in (lambda r: r, lambda r: rhs, lambda r: rhs + 1):
-        for _ in strips:
+        for _ in range(2):
             strip_specs.append(pl.BlockSpec((depth, width, cols), lambda r, g=group: (g(r), 0, 0)))
+    packed = pl.BlockSpec(y_next.shape, lambda r: (0, 0, 0))
     return pl.pallas_call(
         powers_kernel,
         grid=(rhs,),
@@ -189,7 +204,8 @@
             pl.BlockSpec((depth, rows, cols), lambda r: (0, 0, 0)),
             pl.BlockSpec((depth, rows, cols), lambda r: (0, 0, 0)),
         ]
-        + strip_specs,
+        + strip_specs
+        + [packed, packed],
         out_specs=pl.BlockSpec((STEPS + 1, 1, depth, rows, cols), lambda r: (0, r, 0, 0, 0)),
         out_shape=jax.ShapeDtypeStruct((STEPS + 1, rhs, depth, rows, cols), jnp.float32),
         scratch_shapes=[
@@ -197,7 +213,7 @@
             pltpu.VMEM((depth, rows + 2 * width, LANES), jnp.float32),
         ],
         compiler_params=pltpu.CompilerParams(dimension_semantics=("arbitrary",)),
-    )(start_block, conductivity, reaction, *(strips * 3))
+    )(start_block, conductivity, reaction, *([x_next, x_prev] * 3), y_next, y_prev)
 
 
 def factor_kernel(gram_ref, upper_ref, inverse_ref):

time: 178 us -> 172 us (0.966)
  Pallas kernels: 41.7 us -> 36.1 us
    pallas_call x1, Pallas kernels: 9.85 us -> 4.05 us  [edge_columns(): pl.pallas_call(columns_kernel, in_specs=[whole(start_block.shape), whole(...]
where the time goes in v4:
time: 172 us; the launch traced here: 171 us
  waiting for transfers between devices  68.4 us (40%)
  Pallas kernels  36.1 us (21%)
  matrix products  35.5 us (21%)
  local copies, waits for them, and re-layouts  19.9 us (12%)
  starting transfers between devices  9.02 us (5%)
    ppermute x14, waiting for transfers between devices, tree_sum(): lax.ppermute(value, axis, fold_pairs(count, stride, span, fold))  53.9 us
    pallas_call x1, Pallas kernels, krylov_powers(): pl.pallas_call(powers_kernel, grid=(rhs,), in_specs=[pl.BlockSpec((1, dep...  21.5 us
    dot_general x1, matrix products, body(): jnp.dot(krylov, krylov.T, precision=lax.Precision.HIGHEST, preferred_elem...  11.8 us
    dot_general x1, matrix products, body(): jnp.dot(inverse_first, krylov, precision=lax.Precision.HIGHEST, preferred...  11.6 us
    pallas_call x2, Pallas kernels, cholesky_factors(): return pl.pallas_call(factor_kernel, out_shape=[square, square])(symmetric)  10.6 us
    reshape x1, local copies, waits for them, and re-layouts, body(): krylov_powers(start_block, conductivity, reaction, strips).reshape(COLS, -1)  10.4 us
    unnamed x15, local copies, waits for them, and re-layouts  7.31 us
    dot_general x1, matrix products, body(): jnp.dot(inverse_second, first_q, precision=lax.Precision.HIGH, preferred_...  7.14 us
  transfers between devices with their start and end apart: 18, of which 18 were waited for; matrix products, arithmetic and copies ran while one was open for 0% of the time, Pallas kernels for 0%

profile of v4, /device:TPU:0, one launch (start us, length us, event | category | flops | bytes accessed | tf_op | source)
XLA Modules:
  0.0 171.1 jit_solution(16450973264560495149)
XLA Ops:
  0.6 1.1 fusion.1
  1.7 0.8 fusion.2
  2.6 5.4 %collective-permute-start = (f32[80,4,128]{2,1,0:T(4,128)S(1)}, f32[80,4,128]{2,1,0:T(4,128)S(1)}, u32[]{:S(2)}, u32[]{:S(2)}) collective-permute-start(f32[80,4,128]{2,1,0:T(4,128)S(1)} %pad_maximum_fusion), channel_id=1, source_target_pairs={{8,0},{16,8},{24,16},{32,24},{40,32},{48,40},{56,48},{64,56},{72,6... | collective-permute-start | bytes 491528 | tf_op jit(solution)/shard_map/ppermute | solution.py:91
  8.1 3.3 %collective-permute-done.xn_ref.refs_3_.refs_5_.refs_7_ = f32[80,4,128]{2,1,0:T(4,128)S(1)} collective-permute-done((f32[80,4,128]{2,1,0:T(4,128)S(1)}, f32[80,4,128]{2,1,0:T(4,128)S(1)}, u32[]{:S(2)}, u32[]{:S(2)}) %collective-permute-start) | collective-permute-done | bytes 163872 | tf_op jit(solution)/shard_map/ppermute | solution.py:91
  11.4 5.6 %collective-permute-done.1.xp_ref.refs_4_.refs_6_.refs_8_ = f32[80,4,128]{2,1,0:T(4,128)S(1)} collective-permute-done((f32[80,4,128]{2,1,0:T(4,128)S(1)}, f32[80,4,128]{2,1,0:T(4,128)S(1)}, u32[]{:S(2)}, u32[]{:S(2)}) %collective-permute-start.1) | collective-permute-done | bytes 163872 | tf_op jit(solution)/shard_map/ppermute | solution.py:92
  17.7 4.0 %shard_map.58 = (f32[3,72,128]{2,1,0:T(8,128)}, f32[3,72,128]{2,1,0:T(8,128)}) custom-call(f32[8,8,64,128]{3,2,1,0:T(8,128)} %refs_0_.1, f32[8,64,128]{2,1,0:T(8,128)} %refs_1_.1, f32[8,64,128]{2,1,0:T(8,128)} %refs_2_.1, f32[80,4,128]{2,1,0:T(4,128)} %copy-done.1, f32[80,4,128]{2,1,0:T(4,128)} %copy-done.2), custom_call_target="tpu_custom_call" | custom-call | tf_op jit(solution)/shard_map/pallas_call | solution.py:72
  21.8 2.3 %collective-permute-start.2 = (f32[3,72,128]{2,1,0:T(8,128)}, f32[3,72,128]{2,1,0:T(8,128)S(1)}, u32[]{:S(2)}, u32[]{:S(2)}) collective-permute-start(f32[3,72,128]{2,1,0:T(8,128)} %get-tuple-element.9), channel_id=1, source_target_pairs={{1,0},{2,1},{3,2},{4,3},{5,4},{6,5},{7,6},{0,7},{9,8},{10,9},{11,1... | collective-permute-start | bytes 331784 | tf_op jit(solution)/shard_map/ppermute | solution.py:95
  24.0 2.6 %collective-permute-done.2.refs_9_ = f32[3,72,128]{2,1,0:T(8,128)S(1)} collective-permute-done((f32[3,72,128]{2,1,0:T(8,128)}, f32[3,72,128]{2,1,0:T(8,128)S(1)}, u32[]{:S(2)}, u32[]{:S(2)}) %collective-permute-start.2) | collective-permute-done | bytes 110624 | tf_op jit(solution)/shard_map/ppermute | solution.py:95
  26.7 2.9 %collective-permute-done.3.refs_10_ = f32[3,72,128]{2,1,0:T(8,128)S(1)} collective-permute-done((f32[3,72,128]{2,1,0:T(8,128)}, f32[3,72,128]{2,1,0:T(8,128)S(1)}, u32[]{:S(2)}, u32[]{:S(2)}) %collective-permute-start.3) | collective-permute-done | bytes 110624 | tf_op jit(solution)/shard_map/ppermute | solution.py:96
  30.3 21.5 %shard_map.59 = f32[5,8,8,64,128]{4,3,2,1,0:T(8,128)} custom-call(f32[8,8,64,128]{3,2,1,0:T(8,128)} %refs_0_.1, f32[8,64,128]{2,1,0:T(8,128)} %refs_1_.1, f32[8,64,128]{2,1,0:T(8,128)} %refs_2_.1, f32[80,4,128]{2,1,0:T(4,128)} %copy-done.1, f32[80,4,128]{2,1,0:T(4,128)} %copy-done.2, f32[80,4,128]{2,1,0:T(4,128)} %copy-done.1, f32[80,4,128]{2,1,0:T(4,128)} %copy-done.2, ...), custom_call_target="tpu_custom_call" | custom-call | tf_op jit(solution)/shard_map/pallas_call | solution.py:199
  51.8 10.4 %reshape.20 = f32[40,65536]{1,0:T(8,128)} reshape(f32[5,8,8,64,128]{4,3,2,1,0:T(8,128)} %shard_map.59) | data formatting | bytes 20971520 | tf_op jit(solution)/shard_map/reshape | solution.py:262
  62.2 11.8 %fusion.4 = f32[40,40]{0,1:T(8,128)S(1)} fusion(f32[40,65536]{1,0:T(8,128)} %reshape.20), kind=kOutput, calls=%fused_computation.12 | convolution fusion | flops 1258291200 | bytes 10492160 | tf_op jit(solution)/shard_map/dot_general | solution.py:263
  74.1 3.8 %collective-permute-done.4 = f32[40,40]{0,1:T(8,128)S(1)} collective-permute-done((f32[40,40]{0,1:T(8,128)S(1)}, f32[40,40]{0,1:T(8,128)S(1)}, u32[]{:S(2)}, u32[]{:S(2)}) %collective-permute-start.4) | collective-permute-done | bytes 6432 | tf_op jit(solution)/shard_map/ppermute | solution.py:134
  77.9 5.0 %collective-permute-done.5 = f32[40,40]{0,1:T(8,128)S(1)} collective-permute-done((f32[40,40]{0,1:T(8,128)S(1)}, f32[40,40]{0,1:T(8,128)S(1)}, u32[]{:S(2)}, u32[]{:S(2)}) %collective-permute-start.5) | collective-permute-done | bytes 6432 | tf_op jit(solution)/shard_map/ppermute | solution.py:134
  82.9 3.8 %collective-permute-done.6 = f32[40,40]{0,1:T(8,128)S(1)} collective-permute-done((f32[40,40]{0,1:T(8,128)S(1)}, f32[40,40]{0,1:T(8,128)S(1)}, u32[]{:S(2)}, u32[]{:S(2)}) %collective-permute-start.6) | collective-permute-done | bytes 6432 | tf_op jit(solution)/shard_map/ppermute | solution.py:134
  86.7 5.0 %collective-permute-done.7 = f32[40,40]{0,1:T(8,128)S(1)} collective-permute-done((f32[40,40]{0,1:T(8,128)S(1)}, f32[40,40]{0,1:T(8,128)S(1)}, u32[]{:S(2)}, u32[]{:S(2)}) %collective-permute-start.7) | collective-permute-done | bytes 6432 | tf_op jit(solution)/shard_map/ppermute | solution.py:134
  91.7 1.2 collective-permute-done.8
  92.9 3.8 %collective-permute-done.9 = f32[40,40]{0,1:T(8,128)S(1)} collective-permute-done((f32[40,40]{0,1:T(8,128)S(1)}, f32[40,40]{0,1:T(8,128)S(1)}, u32[]{:S(2)}, u32[]{:S(2)}) %collective-permute-start.9) | collective-permute-done | bytes 6432 | tf_op jit(solution)/shard_map/ppermute | solution.py:134
  97.2 4.5 %collective-permute-done.10 = f32[40,40]{0,1:T(8,128)S(1)} collective-permute-done((f32[40,40]{0,1:T(8,128)S(1)}, f32[40,40]{0,1:T(8,128)S(1)}, u32[]{:S(2)}, u32[]{:S(2)}) %collective-permute-start.10) | collective-permute-done | bytes 6432 | tf_op jit(solution)/shard_map/ppermute | solution.py:134
  102.3 5.3 %shard_map.60 = (f32[40,40]{1,0:T(8,128)}, f32[40,40]{1,0:T(8,128)}) custom-call(f32[40,40]{1,0:T(8,128)} %fusion.gram_ref), custom_call_target="tpu_custom_call" | custom-call | tf_op jit(solution)/shard_map/pallas_call | solution.py:249
  107.6 11.6 %fusion.5 = f32[40,65536]{1,0:T(8,128)S(1)} fusion(f32[40,40]{1,0:T(8,128)} %get-tuple-element.11, f32[40,65536]{1,0:T(8,128)} %reshape.20), kind=kOutput, calls=%fused_computation.13 | convolution fusion | flops 1258291200 | bytes 20977920 | tf_op jit(solution)/shard_map/dot_general | solution.py:267
  119.2 4.2 %fusion.6 = f32[40,40]{0,1:T(8,128)S(1)} fusion(f32[40,65536]{1,0:T(8,128)S(1)} %fusion.5), kind=kOutput, calls=%fused_computation.14 | convolution fusion | flops 629145600 | bytes 10492160 | tf_op jit(solution)/shard_map/dot_general | solution.py:270
  123.5 3.8 %collective-permute-done.11 = f32[40,40]{0,1:T(8,128)S(1)} collective-permute-done((f32[40,40]{0,1:T(8,128)S(1)}, f32[40,40]{0,1:T(8,128)S(1)}, u32[]{:S(2)}, u32[]{:S(2)}) %collective-permute-start.11) | collective-permute-done | bytes 6432 | tf_op jit(solution)/shard_map/ppermute | solution.py:134
  127.3 5.0 %collective-permute-done.12 = f32[40,40]{0,1:T(8,128)S(1)} collective-permute-done((f32[40,40]{0,1:T(8,128)S(1)}, f32[40,40]{0,1:T(8,128)S(1)}, u32[]{:S(2)}, u32[]{:S(2)}) %collective-permute-start.12) | collective-permute-done | bytes 6432 | tf_op jit(solution)/shard_map/ppermute | solution.py:134
  132.3 3.8 %collective-permute-done.13 = f32[40,40]{0,1:T(8,128)S(1)} collective-permute-done((f32[40,40]{0,1:T(8,128)S(1)}, f32[40,40]{0,1:T(8,128)S(1)}, u32[]{:S(2)}, u32[]{:S(2)}) %collective-permute-start.13) | collective-permute-done | bytes 6432 | tf_op jit(solution)/shard_map/ppermute | solution.py:134
  136.1 5.0 %collective-permute-done.14 = f32[40,40]{0,1:T(8,128)S(1)} collective-permute-done((f32[40,40]{0,1:T(8,128)S(1)}, f32[40,40]{0,1:T(8,128)S(1)}, u32[]{:S(2)}, u32[]{:S(2)}) %collective-permute-start.14) | collective-permute-done | bytes 6432 | tf_op jit(solution)/shard_map/ppermute | solution.py:134
  141.1 1.2 collective-permute-done.15
  142.3 3.8 %collective-permute-done.16 = f32[40,40]{0,1:T(8,128)S(1)} collective-permute-done((f32[40,40]{0,1:T(8,128)S(1)}, f32[40,40]{0,1:T(8,128)S(1)}, u32[]{:S(2)}, u32[]{:S(2)}) %collective-permute-start.16) | collective-permute-done | bytes 6432 | tf_op jit(solution)/shard_map/ppermute | solution.py:134
  146.6 4.4 %collective-permute-done.17 = f32[40,40]{0,1:T(8,128)S(1)} collective-permute-done((f32[40,40]{0,1:T(8,128)S(1)}, f32[40,40]{0,1:T(8,128)S(1)}, u32[]{:S(2)}, u32[]{:S(2)}) %collective-permute-start.17) | collective-permute-done | bytes 6432 | tf_op jit(solution)/shard_map/ppermute | solution.py:134
  151.8 5.3 %shard_map.61 = (f32[40,40]{1,0:T(8,128)}, f32[40,40]{1,0:T(8,128)}) custom-call(f32[40,40]{1,0:T(8,128)} %broadcast_multiply_fusion.gram_ref), custom_call_target="tpu_custom_call" | custom-call | tf_op jit(solution)/shard_map/pallas_call | solution.py:249
  157.1 7.1 %convolution_bitcast_fusion = f32[5,8,512,128]{3,1,2,0:T(8,128)S(1)} fusion(f32[40,40]{1,0:T(8,128)} %get-tuple-element.12, f32[40,65536]{1,0:T(8,128)} %copy-done), kind=kOutput, calls=%fused_computation | convolution fusion | flops 629145600 | bytes 20977920 | tf_op jit(solution)/shard_map/dot_general | solution.py:274
  164.3 6.0 %copy.15 = f32[5,8,512,128]{3,2,1,0:T(8,128)} copy(f32[5,8,512,128]{3,1,2,0:T(8,128)S(1)} %convolution_bitcast_fusion) | data formatting | bytes 20971520
  (53 shorter events, 5.1 us)
Async XLA Ops:
  2.6 8.8 %collective-permute-start = (f32[80,4,128]{2,1,0:T(4,128)S(1)}, f32[80,4,128]{2,1,0:T(4,128)S(1)}, u32[]{:S(2)}, u32[]{:S(2)}) collective-permute-start(f32[80,4,128]{2,1,0:T(4,128)S(1)} %pad_maximum_fusion), channel_id=1, source_target_pairs={{8,0},{16,8},{24,16},{32,24},{40,32},{48,40},{56,48},{64,56},{72,6... | collective-permute-start | bytes 491528 | tf_op jit(solution)/shard_map/ppermute | solution.py:91
  8.0 9.0 %collective-permute-start.1 = (f32[80,4,128]{2,1,0:T(4,128)S(1)}, f32[80,4,128]{2,1,0:T(4,128)S(1)}, u32[]{:S(2)}, u32[]{:S(2)}) collective-permute-start(f32[80,4,128]{2,1,0:T(4,128)S(1)} %pad_maximum_fusion.1), channel_id=1, source_target_pairs={{0,8},{8,16},{16,24},{24,32},{32,40},{40,48},{48,56},{56,64},{64,7... | collective-permute-start | bytes 491528 | tf_op jit(solution)/shard_map/ppermute | solution.py:92
  11.4 5.6 %copy-start.1 = (f32[80,4,128]{2,1,0:T(4,128)}, f32[80,4,128]{2,1,0:T(4,128)S(1)}, u32[]{:S(2)}) copy-start(f32[80,4,128]{2,1,0:T(4,128)S(1)} %collective-permute-done.xn_ref.refs_3_.refs_5_.refs_7_) | copy-start | bytes 491524
  17.0 0.7 copy-start.2
  21.8 4.9 %collective-permute-start.2 = (f32[3,72,128]{2,1,0:T(8,128)}, f32[3,72,128]{2,1,0:T(8,128)S(1)}, u32[]{:S(2)}, u32[]{:S(2)}) collective-permute-start(f32[3,72,128]{2,1,0:T(8,128)} %get-tuple-element.9), channel_id=1, source_target_pairs={{1,0},{2,1},{3,2},{4,3},{5,4},{6,5},{7,6},{0,7},{9,8},{10,9},{11,1... | collective-permute-start | bytes 331784 | tf_op jit(solution)/shard_map/ppermute | solution.py:95
  24.0 5.6 %collective-permute-start.3 = (f32[3,72,128]{2,1,0:T(8,128)}, f32[3,72,128]{2,1,0:T(8,128)S(1)}, u32[]{:S(2)}, u32[]{:S(2)}) collective-permute-start(f32[3,72,128]{2,1,0:T(8,128)} %get-tuple-element.10), channel_id=1, source_target_pairs={{0,1},{1,2},{2,3},{3,4},{4,5},{5,6},{6,7},{7,0},{8,9},{9,10},{10,1... | collective-permute-start | bytes 331784 | tf_op jit(solution)/shard_map/ppermute | solution.py:96
  26.7 3.0 %copy-start.3 = (f32[3,72,128]{2,1,0:T(8,128)}, f32[3,72,128]{2,1,0:T(8,128)S(1)}, u32[]{:S(2)}) copy-start(f32[3,72,128]{2,1,0:T(8,128)S(1)} %collective-permute-done.2.refs_9_) | copy-start | bytes 331780
  29.6 0.7 copy-start.4
  74.0 3.9 %collective-permute-start.4 = (f32[40,40]{0,1:T(8,128)S(1)}, f32[40,40]{0,1:T(8,128)S(1)}, u32[]{:S(2)}, u32[]{:S(2)}) collective-permute-start(f32[40,40]{0,1:T(8,128)S(1)} %fusion.4), channel_id=1, source_target_pairs={{0,32},{8,40},{16,48},{24,56},{32,0},{40,8},{48,16},{56,24},{64,96... | collective-permute-start | bytes 19208 | tf_op jit(solution)/shard_map/ppermute | solution.py:134
  77.9 5.0 %collective-permute-start.5 = (f32[40,40]{0,1:T(8,128)S(1)}, f32[40,40]{0,1:T(8,128)S(1)}, u32[]{:S(2)}, u32[]{:S(2)}) collective-permute-start(f32[40,40]{0,1:T(8,128)S(1)} %add.48), channel_id=1, source_target_pairs={{0,96},{8,104},{16,112},{24,120},{32,64},{40,72},{48,80},{56,88},{... | collective-permute-start | bytes 19208 | tf_op jit(solution)/shard_map/ppermute | solution.py:134
  82.9 3.8 %collective-permute-start.6 = (f32[40,40]{0,1:T(8,128)S(1)}, f32[40,40]{0,1:T(8,128)S(1)}, u32[]{:S(2)}, u32[]{:S(2)}) collective-permute-start(f32[40,40]{0,1:T(8,128)S(1)} %add.49), channel_id=1, source_target_pairs={{0,8},{8,0},{16,24},{24,16},{32,40},{40,32},{48,56},{56,48},{64,72... | collective-permute-start | bytes 19208 | tf_op jit(solution)/shard_map/ppermute | solution.py:134
  86.7 5.0 %collective-permute-start.7 = (f32[40,40]{0,1:T(8,128)S(1)}, f32[40,40]{0,1:T(8,128)S(1)}, u32[]{:S(2)}, u32[]{:S(2)}) collective-permute-start(f32[40,40]{0,1:T(8,128)S(1)} %add.50), channel_id=1, source_target_pairs={{0,24},{8,16},{16,8},{24,0},{32,56},{40,48},{48,40},{56,32},{64,88... | collective-permute-start | bytes 19208 | tf_op jit(solution)/shard_map/ppermute | solution.py:134
  91.7 1.2 collective-permute-start.8
  92.8 3.8 %collective-permute-start.9 = (f32[40,40]{0,1:T(8,128)S(1)}, f32[40,40]{0,1:T(8,128)S(1)}, u32[]{:S(2)}, u32[]{:S(2)}) collective-permute-start(f32[40,40]{0,1:T(8,128)S(1)} %add.52), channel_id=1, source_target_pairs={{0,2},{1,3},{2,0},{3,1},{4,6},{5,7},{6,4},{7,5},{8,10},{9,11},{10,... | collective-permute-start | bytes 19208 | tf_op jit(solution)/shard_map/ppermute | solution.py:134
  96.6 5.0 %collective-permute-start.10 = (f32[40,40]{0,1:T(8,128)S(1)}, f32[40,40]{0,1:T(8,128)S(1)}, u32[]{:S(2)}, u32[]{:S(2)}) collective-permute-start(f32[40,40]{0,1:T(8,128)S(1)} %add.53), channel_id=1, source_target_pairs={{0,6},{1,7},{2,4},{3,5},{4,2},{5,3},{6,0},{7,1},{8,14},{9,15},{10,... | collective-permute-start | bytes 19208 | tf_op jit(solution)/shard_map/ppermute | solution.py:134
  119.2 4.2 %copy-start = (f32[40,65536]{1,0:T(8,128)}, f32[40,65536]{1,0:T(8,128)S(1)}, u32[]{:S(2)}) copy-start(f32[40,65536]{1,0:T(8,128)S(1)} %fusion.5) | copy-start | bytes 31457284
  123.4 3.9 %collective-permute-start.11 = (f32[40,40]{0,1:T(8,128)S(1)}, f32[40,40]{0,1:T(8,128)S(1)}, u32[]{:S(2)}, u32[]{:S(2)}) collective-permute-start(f32[40,40]{0,1:T(8,128)S(1)} %fusion.6), channel_id=1, source_target_pairs={{0,32},{8,40},{16,48},{24,56},{32,0},{40,8},{48,16},{56,24},{64,96... | collective-permute-start | bytes 19208 | tf_op jit(solution)/shard_map/ppermute | solution.py:134
  127.3 5.0 %collective-permute-start.12 = (f32[40,40]{0,1:T(8,128)S(1)}, f32[40,40]{0,1:T(8,128)S(1)}, u32[]{:S(2)}, u32[]{:S(2)}) collective-permute-start(f32[40,40]{0,1:T(8,128)S(1)} %add.56), channel_id=1, source_target_pairs={{0,96},{8,104},{16,112},{24,120},{32,64},{40,72},{48,80},{56,88},{... | collective-permute-start | bytes 19208 | tf_op jit(solution)/shard_map/ppermute | solution.py:134
  132.3 3.8 %collective-permute-start.13 = (f32[40,40]{0,1:T(8,128)S(1)}, f32[40,40]{0,1:T(8,128)S(1)}, u32[]{:S(2)}, u32[]{:S(2)}) collective-permute-start(f32[40,40]{0,1:T(8,128)S(1)} %add.57), channel_id=1, source_target_pairs={{0,8},{8,0},{16,24},{24,16},{32,40},{40,32},{48,56},{56,48},{64,72... | collective-permute-start | bytes 19208 | tf_op jit(solution)/shard_map/ppermute | solution.py:134
  136.1 5.0 %collective-permute-start.14 = (f32[40,40]{0,1:T(8,128)S(1)}, f32[40,40]{0,1:T(8,128)S(1)}, u32[]{:S(2)}, u32[]{:S(2)}) collective-permute-start(f32[40,40]{0,1:T(8,128)S(1)} %add.58), channel_id=1, source_target_pairs={{0,24},{8,16},{16,8},{24,0},{32,56},{40,48},{48,40},{56,32},{64,88... | collective-permute-start | bytes 19208 | tf_op jit(solution)/shard_map/ppermute | solution.py:134
  141.1 1.2 collective-permute-start.15
  142.3 3.8 %collective-permute-start.16 = (f32[40,40]{0,1:T(8,128)S(1)}, f32[40,40]{0,1:T(8,128)S(1)}, u32[]{:S(2)}, u32[]{:S(2)}) collective-permute-start(f32[40,40]{0,1:T(8,128)S(1)} %add.60), channel_id=1, source_target_pairs={{0,2},{1,3},{2,0},{3,1},{4,6},{5,7},{6,4},{7,5},{8,10},{9,11},{10,... | collective-permute-start | bytes 19208 | tf_op jit(solution)/shard_map/ppermute | solution.py:134
  146.1 5.0 %collective-permute-start.17 = (f32[40,40]{0,1:T(8,128)S(1)}, f32[40,40]{0,1:T(8,128)S(1)}, u32[]{:S(2)}, u32[]{:S(2)}) collective-permute-start(f32[40,40]{0,1:T(8,128)S(1)} %add.61), channel_id=1, source_target_pairs={{0,6},{1,7},{2,4},{3,5},{4,2},{5,3},{6,0},{7,1},{8,14},{9,15},{10,... | collective-permute-start | bytes 19208 | tf_op jit(solution)/shard_map/ppermute | solution.py:134
  164.3 6.0 %copy-start.5 = (f32[40,40]{1,0:T(8,128)S(1)}, f32[40,40]{1,0:T(8,128)}, u32[]{:S(2)}) copy-start(f32[40,40]{1,0:T(8,128)} %get-tuple-element.8) | copy-start | bytes 19204
  164.3 6.0 %copy-start.6 = (f32[40,40]{1,0:T(8,128)S(1)}, f32[40,40]{1,0:T(8,128)}, u32[]{:S(2)}) copy-start(f32[40,40]{1,0:T(8,128)} %get-tuple-element.13) | copy-start | bytes 19204

commit v5 on v4

--- a/solution.py
+++ b/solution.py
@@ -151,7 +151,8 @@
     block_ref, coef_ref, react_ref = refs[:3]
     x_strips = refs[3:9]
     yn_ref, yp_ref = refs[9:11]
-    out_ref, weight_ref, react_pad_ref = refs[11:]
+    out_ref, weight_ref, react_pad_ref = refs[11:14]
+    buffers = refs[14:]
     depth, rows, cols = (out_ref.shape[2], out_ref.shape[3], out_ref.shape[4])
     r = pl.program_id(0)
 
@@ -176,15 +177,22 @@
         react_pad_ref[...] = planes(lambda z: react_ref[z], 2, rhs * depth + depth)
 
     out_ref[0, 0] = block_ref[0]
-    current = planes(lambda z: block_ref[0, z], 0, r * depth)
-    react = react_pad_ref[...]
+    buffers[0][...] = planes(lambda z: block_ref[0, z], 0, r * depth)
     for power in range(1, STEPS + 1):
-        running = jnp.zeros_like(current)
-        for d, direction in enumerate(DIRECTIONS):
-            beside = neighbour(current, direction)
-            running = running + weight_ref[d] * (current - beside)
-        current = (react * current + running - center_shift * current) * step_scale
-        out_ref[power, 0] = current[:, :rows, :cols]
+        source, target = (buffers[(power - 1) % 2], buffers[power % 2])
+        for z in range(depth):
+            current = source[z]
+            running = jnp.zeros_like(current)
+            for d, (axis, offset) in enumerate(DIRECTIONS):
+                if axis == 0:
+                    beside = source[(z + offset) % depth]
+                else:
+                    beside = pltpu.roll(current, (-offset) % current.shape[axis - 1], axis - 1)
+                running = running + weight_ref[d, z] * (current - beside)
+            current = (react_pad_ref[z] * current + running - center_shift * current) * step_scale
+            if power < STEPS:
+                target[z] = current
+            out_ref[power, 0, z] = current[:rows, :cols]
 
 
 def krylov_powers(start_block, conductivity, reaction, strips):
@@ -211,6 +219,8 @@
         scratch_shapes=[
             pltpu.VMEM((len(DIRECTIONS), depth, rows + 2 * width, LANES), jnp.float32),
             pltpu.VMEM((depth, rows + 2 * width, LANES), jnp.float32),
+            pltpu.VMEM((depth, rows + 2 * width, LANES), jnp.float32),
+            pltpu.VMEM((depth, rows + 2 * width, LANES), jnp.float32),
         ],
         compiler_params=pltpu.CompilerParams(dimension_semantics=("arbitrary",)),
     )(start_block, conductivity, reaction, *([x_next, x_prev] * 3), y_next, y_prev)

time: 172 us -> 171 us (level)
  no operation moved by 1% of the time
where the time goes in v5:
time: 171 us
  waiting for transfers between devices  68.4 us (40%)
  Pallas kernels  35.6 us (21%)
  matrix products  35.5 us (21%)
  local copies, waits for them, and re-layouts  19.9 us (12%)
  starting transfers between devices  9.02 us (5%)
    ppermute x14, waiting for transfers between devices, tree_sum(): lax.ppermute(value, axis, fold_pairs(count, stride, span, fold))  53.9 us
    pallas_call x1, Pallas kernels, krylov_powers(): pl.pallas_call(powers_kernel, grid=(rhs,), in_specs=[pl.BlockSpec((1, dep...  20.9 us
    dot_general x1, matrix products, body(): jnp.dot(krylov, krylov.T, precision=lax.Precision.HIGHEST, preferred_elem...  11.8 us
    dot_general x1, matrix products, body(): jnp.dot(inverse_first, krylov, precision=lax.Precision.HIGHEST, preferred...  11.6 us
    pallas_call x2, Pallas kernels, cholesky_factors(): return pl.pallas_call(factor_kernel, out_shape=[square, square])(symmetric)  10.6 us
    reshape x1, local copies, waits for them, and re-layouts, body(): krylov_powers(start_block, conductivity, reaction, strips).reshape(COLS, -1)  10.4 us
    unnamed x15, local copies, waits for them, and re-layouts  7.31 us
    dot_general x1, matrix products, body(): jnp.dot(inverse_second, first_q, precision=lax.Precision.HIGH, preferred_...  7.14 us
  transfers between devices with their start and end apart: 18, of which 18 were waited for; matrix products, arithmetic and copies ran while one was open for 0% of the time, Pallas kernels for 0%

profile of v5, /device:TPU:0, one launch (start us, length us, event | category | flops | bytes accessed | tf_op | source)
XLA Modules:
  0.0 170.5 jit_solution(4421326518891321543)
XLA Ops:
  0.6 1.1 fusion.1
  1.7 0.8 fusion.2
  2.6 5.4 %collective-permute-start = (f32[80,4,128]{2,1,0:T(4,128)S(1)}, f32[80,4,128]{2,1,0:T(4,128)S(1)}, u32[]{:S(2)}, u32[]{:S(2)}) collective-permute-start(f32[80,4,128]{2,1,0:T(4,128)S(1)} %pad_maximum_fusion), channel_id=1, source_target_pairs={{8,0},{16,8},{24,16},{32,24},{40,32},{48,40},{56,48},{64,56},{72,6... | collective-permute-start | bytes 491528 | tf_op jit(solution)/shard_map/ppermute | solution.py:91
  8.1 3.3 %collective-permute-done.xn_ref.refs_3_.refs_5_.refs_7_ = f32[80,4,128]{2,1,0:T(4,128)S(1)} collective-permute-done((f32[80,4,128]{2,1,0:T(4,128)S(1)}, f32[80,4,128]{2,1,0:T(4,128)S(1)}, u32[]{:S(2)}, u32[]{:S(2)}) %collective-permute-start) | collective-permute-done | bytes 163872 | tf_op jit(solution)/shard_map/ppermute | solution.py:91
  11.4 5.6 %collective-permute-done.1.xp_ref.refs_4_.refs_6_.refs_8_ = f32[80,4,128]{2,1,0:T(4,128)S(1)} collective-permute-done((f32[80,4,128]{2,1,0:T(4,128)S(1)}, f32[80,4,128]{2,1,0:T(4,128)S(1)}, u32[]{:S(2)}, u32[]{:S(2)}) %collective-permute-start.1) | collective-permute-done | bytes 163872 | tf_op jit(solution)/shard_map/ppermute | solution.py:92
  17.7 4.0 %shard_map.58 = (f32[3,72,128]{2,1,0:T(8,128)}, f32[3,72,128]{2,1,0:T(8,128)}) custom-call(f32[8,8,64,128]{3,2,1,0:T(8,128)} %refs_0_.1, f32[8,64,128]{2,1,0:T(8,128)} %refs_1_.1, f32[8,64,128]{2,1,0:T(8,128)} %refs_2_.1, f32[80,4,128]{2,1,0:T(4,128)} %copy-done.1, f32[80,4,128]{2,1,0:T(4,128)} %copy-done.2), custom_call_target="tpu_custom_call" | custom-call | tf_op jit(solution)/shard_map/pallas_call | solution.py:72
  21.8 2.3 %collective-permute-start.2 = (f32[3,72,128]{2,1,0:T(8,128)}, f32[3,72,128]{2,1,0:T(8,128)S(1)}, u32[]{:S(2)}, u32[]{:S(2)}) collective-permute-start(f32[3,72,128]{2,1,0:T(8,128)} %get-tuple-element.9), channel_id=1, source_target_pairs={{1,0},{2,1},{3,2},{4,3},{5,4},{6,5},{7,6},{0,7},{9,8},{10,9},{11,1... | collective-permute-start | bytes 331784 | tf_op jit(solution)/shard_map/ppermute | solution.py:95
  24.0 2.6 %collective-permute-done.2.refs_9_ = f32[3,72,128]{2,1,0:T(8,128)S(1)} collective-permute-done((f32[3,72,128]{2,1,0:T(8,128)}, f32[3,72,128]{2,1,0:T(8,128)S(1)}, u32[]{:S(2)}, u32[]{:S(2)}) %collective-permute-start.2) | collective-permute-done | bytes 110624 | tf_op jit(solution)/shard_map/ppermute | solution.py:95
  26.7 2.9 %collective-permute-done.3.refs_10_ = f32[3,72,128]{2,1,0:T(8,128)S(1)} collective-permute-done((f32[3,72,128]{2,1,0:T(8,128)}, f32[3,72,128]{2,1,0:T(8,128)S(1)}, u32[]{:S(2)}, u32[]{:S(2)}) %collective-permute-start.3) | collective-permute-done | bytes 110624 | tf_op jit(solution)/shard_map/ppermute | solution.py:96
  30.3 20.9 %shard_map.59 = f32[5,8,8,64,128]{4,3,2,1,0:T(8,128)} custom-call(f32[8,8,64,128]{3,2,1,0:T(8,128)} %refs_0_.1, f32[8,64,128]{2,1,0:T(8,128)} %refs_1_.1, f32[8,64,128]{2,1,0:T(8,128)} %refs_2_.1, f32[80,4,128]{2,1,0:T(4,128)} %copy-done.1, f32[80,4,128]{2,1,0:T(4,128)} %copy-done.2, f32[80,4,128]{2,1,0:T(4,128)} %copy-done.1, f32[80,4,128]{2,1,0:T(4,128)} %copy-done.2, ...), custom_call_target="tpu_custom_call" | custom-call | tf_op jit(solution)/shard_map/pallas_call | solution.py:207
  51.2 10.4 %reshape.20 = f32[40,65536]{1,0:T(8,128)} reshape(f32[5,8,8,64,128]{4,3,2,1,0:T(8,128)} %shard_map.59) | data formatting | bytes 20971520 | tf_op jit(solution)/shard_map/reshape | solution.py:272
  61.6 11.8 %fusion.4 = f32[40,40]{0,1:T(8,128)S(1)} fusion(f32[40,65536]{1,0:T(8,128)} %reshape.20), kind=kOutput, calls=%fused_computation.12 | convolution fusion | flops 1258291200 | bytes 10492160 | tf_op jit(solution)/shard_map/dot_general | solution.py:273
  73.6 3.8 %collective-permute-done.4 = f32[40,40]{0,1:T(8,128)S(1)} collective-permute-done((f32[40,40]{0,1:T(8,128)S(1)}, f32[40,40]{0,1:T(8,128)S(1)}, u32[]{:S(2)}, u32[]{:S(2)}) %collective-permute-start.4) | collective-permute-done | bytes 6432 | tf_op jit(solution)/shard_map/ppermute | solution.py:134
  77.3 5.0 %collective-permute-done.5 = f32[40,40]{0,1:T(8,128)S(1)} collective-permute-done((f32[40,40]{0,1:T(8,128)S(1)}, f32[40,40]{0,1:T(8,128)S(1)}, u32[]{:S(2)}, u32[]{:S(2)}) %collective-permute-start.5) | collective-permute-done | bytes 6432 | tf_op jit(solution)/shard_map/ppermute | solution.py:134
  82.3 3.8 %collective-permute-done.6 = f32[40,40]{0,1:T(8,128)S(1)} collective-permute-done((f32[40,40]{0,1:T(8,128)S(1)}, f32[40,40]{0,1:T(8,128)S(1)}, u32[]{:S(2)}, u32[]{:S(2)}) %collective-permute-start.6) | collective-permute-done | bytes 6432 | tf_op jit(solution)/shard_map/ppermute | solution.py:134
  86.1 5.0 %collective-permute-done.7 = f32[40,40]{0,1:T(8,128)S(1)} collective-permute-done((f32[40,40]{0,1:T(8,128)S(1)}, f32[40,40]{0,1:T(8,128)S(1)}, u32[]{:S(2)}, u32[]{:S(2)}) %collective-permute-start.7) | collective-permute-done | bytes 6432 | tf_op jit(solution)/shard_map/ppermute | solution.py:134
  91.1 1.2 collective-permute-done.8
  92.3 3.8 %collective-permute-done.9 = f32[40,40]{0,1:T(8,128)S(1)} collective-permute-done((f32[40,40]{0,1:T(8,128)S(1)}, f32[40,40]{0,1:T(8,128)S(1)}, u32[]{:S(2)}, u32[]{:S(2)}) %collective-permute-start.9) | collective-permute-done | bytes 6432 | tf_op jit(solution)/shard_map/ppermute | solution.py:134
  96.6 4.4 %collective-permute-done.10 = f32[40,40]{0,1:T(8,128)S(1)} collective-permute-done((f32[40,40]{0,1:T(8,128)S(1)}, f32[40,40]{0,1:T(8,128)S(1)}, u32[]{:S(2)}, u32[]{:S(2)}) %collective-permute-start.10) | collective-permute-done | bytes 6432 | tf_op jit(solution)/shard_map/ppermute | solution.py:134
  101.8 5.3 %shard_map.60 = (f32[40,40]{1,0:T(8,128)}, f32[40,40]{1,0:T(8,128)}) custom-call(f32[40,40]{1,0:T(8,128)} %fusion.gram_ref), custom_call_target="tpu_custom_call" | custom-call | tf_op jit(solution)/shard_map/pallas_call | solution.py:259
  107.1 11.6 %fusion.5 = f32[40,65536]{1,0:T(8,128)S(1)} fusion(f32[40,40]{1,0:T(8,128)} %get-tuple-element.11, f32[40,65536]{1,0:T(8,128)} %reshape.20), kind=kOutput, calls=%fused_computation.13 | convolution fusion | flops 1258291200 | bytes 20977920 | tf_op jit(solution)/shard_map/dot_general | solution.py:277
  118.7 4.2 %fusion.6 = f32[40,40]{0,1:T(8,128)S(1)} fusion(f32[40,65536]{1,0:T(8,128)S(1)} %fusion.5), kind=kOutput, calls=%fused_computation.14 | convolution fusion | flops 629145600 | bytes 10492160 | tf_op jit(solution)/shard_map/dot_general | solution.py:280
  123.0 3.8 %collective-permute-done.11 = f32[40,40]{0,1:T(8,128)S(1)} collective-permute-done((f32[40,40]{0,1:T(8,128)S(1)}, f32[40,40]{0,1:T(8,128)S(1)}, u32[]{:S(2)}, u32[]{:S(2)}) %collective-permute-start.11) | collective-permute-done | bytes 6432 | tf_op jit(solution)/shard_map/ppermute | solution.py:134
  126.8 5.0 %collective-permute-done.12 = f32[40,40]{0,1:T(8,128)S(1)} collective-permute-done((f32[40,40]{0,1:T(8,128)S(1)}, f32[40,40]{0,1:T(8,128)S(1)}, u32[]{:S(2)}, u32[]{:S(2)}) %collective-permute-start.12) | collective-permute-done | bytes 6432 | tf_op jit(solution)/shard_map/ppermute | solution.py:134
  131.8 3.8 %collective-permute-done.13 = f32[40,40]{0,1:T(8,128)S(1)} collective-permute-done((f32[40,40]{0,1:T(8,128)S(1)}, f32[40,40]{0,1:T(8,128)S(1)}, u32[]{:S(2)}, u32[]{:S(2)}) %collective-permute-start.13) | collective-permute-done | bytes 6432 | tf_op jit(solution)/shard_map/ppermute | solution.py:134
  135.6 5.0 %collective-permute-done.14 = f32[40,40]{0,1:T(8,128)S(1)} collective-permute-done((f32[40,40]{0,1:T(8,128)S(1)}, f32[40,40]{0,1:T(8,128)S(1)}, u32[]{:S(2)}, u32[]{:S(2)}) %collective-permute-start.14) | collective-permute-done | bytes 6432 | tf_op jit(solution)/shard_map/ppermute | solution.py:134
  140.5 1.2 collective-permute-done.15
  141.7 3.8 %collective-permute-done.16 = f32[40,40]{0,1:T(8,128)S(1)} collective-permute-done((f32[40,40]{0,1:T(8,128)S(1)}, f32[40,40]{0,1:T(8,128)S(1)}, u32[]{:S(2)}, u32[]{:S(2)}) %collective-permute-start.16) | collective-permute-done | bytes 6432 | tf_op jit(solution)/shard_map/ppermute | solution.py:134
  146.1 4.4 %collective-permute-done.17 = f32[40,40]{0,1:T(8,128)S(1)} collective-permute-done((f32[40,40]{0,1:T(8,128)S(1)}, f32[40,40]{0,1:T(8,128)S(1)}, u32[]{:S(2)}, u32[]{:S(2)}) %collective-permute-start.17) | collective-permute-done | bytes 6432 | tf_op jit(solution)/shard_map/ppermute | solution.py:134
  151.3 5.3 %shard_map.61 = (f32[40,40]{1,0:T(8,128)}, f32[40,40]{1,0:T(8,128)}) custom-call(f32[40,40]{1,0:T(8,128)} %broadcast_multiply_fusion.gram_ref), custom_call_target="tpu_custom_call" | custom-call | tf_op jit(solution)/shard_map/pallas_call | solution.py:259
  156.6 7.1 %convolution_bitcast_fusion = f32[5,8,512,128]{3,1,2,0:T(8,128)S(1)} fusion(f32[40,40]{1,0:T(8,128)} %get-tuple-element.12, f32[40,65536]{1,0:T(8,128)} %copy-done), kind=kOutput, calls=%fused_computation | convolution fusion | flops 629145600 | bytes 20977920 | tf_op jit(solution)/shard_map/dot_general | solution.py:284
  163.8 6.0 %copy.15 = f32[5,8,512,128]{3,2,1,0:T(8,128)} copy(f32[5,8,512,128]{3,1,2,0:T(8,128)S(1)} %convolution_bitcast_fusion) | data formatting | bytes 20971520
  (53 shorter events, 5.1 us)
Async XLA Ops:
  2.6 8.8 %collective-permute-start = (f32[80,4,128]{2,1,0:T(4,128)S(1)}, f32[80,4,128]{2,1,0:T(4,128)S(1)}, u32[]{:S(2)}, u32[]{:S(2)}) collective-permute-start(f32[80,4,128]{2,1,0:T(4,128)S(1)} %pad_maximum_fusion), channel_id=1, source_target_pairs={{8,0},{16,8},{24,16},{32,24},{40,32},{48,40},{56,48},{64,56},{72,6... | collective-permute-start | bytes 491528 | tf_op jit(solution)/shard_map/ppermute | solution.py:91
  8.0 9.0 %collective-permute-start.1 = (f32[80,4,128]{2,1,0:T(4,128)S(1)}, f32[80,4,128]{2,1,0:T(4,128)S(1)}, u32[]{:S(2)}, u32[]{:S(2)}) collective-permute-start(f32[80,4,128]{2,1,0:T(4,128)S(1)} %pad_maximum_fusion.1), channel_id=1, source_target_pairs={{0,8},{8,16},{16,24},{24,32},{32,40},{40,48},{48,56},{56,64},{64,7... | collective-permute-start | bytes 491528 | tf_op jit(solution)/shard_map/ppermute | solution.py:92
  11.4 5.6 %copy-start.1 = (f32[80,4,128]{2,1,0:T(4,128)}, f32[80,4,128]{2,1,0:T(4,128)S(1)}, u32[]{:S(2)}) copy-start(f32[80,4,128]{2,1,0:T(4,128)S(1)} %collective-permute-done.xn_ref.refs_3_.refs_5_.refs_7_) | copy-start | bytes 491524
  17.0 0.7 copy-start.2
  21.8 4.9 %collective-permute-start.2 = (f32[3,72,128]{2,1,0:T(8,128)}, f32[3,72,128]{2,1,0:T(8,128)S(1)}, u32[]{:S(2)}, u32[]{:S(2)}) collective-permute-start(f32[3,72,128]{2,1,0:T(8,128)} %get-tuple-element.9), channel_id=1, source_target_pairs={{1,0},{2,1},{3,2},{4,3},{5,4},{6,5},{7,6},{0,7},{9,8},{10,9},{11,1... | collective-permute-start | bytes 331784 | tf_op jit(solution)/shard_map/ppermute | solution.py:95
  24.0 5.6 %collective-permute-start.3 = (f32[3,72,128]{2,1,0:T(8,128)}, f32[3,72,128]{2,1,0:T(8,128)S(1)}, u32[]{:S(2)}, u32[]{:S(2)}) collective-permute-start(f32[3,72,128]{2,1,0:T(8,128)} %get-tuple-element.10), channel_id=1, source_target_pairs={{0,1},{1,2},{2,3},{3,4},{4,5},{5,6},{6,7},{7,0},{8,9},{9,10},{10,1... | collective-permute-start | bytes 331784 | tf_op jit(solution)/shard_map/ppermute | solution.py:96
  26.7 3.0 %copy-start.3 = (f32[3,72,128]{2,1,0:T(8,128)}, f32[3,72,128]{2,1,0:T(8,128)S(1)}, u32[]{:S(2)}) copy-start(f32[3,72,128]{2,1,0:T(8,128)S(1)} %collective-permute-done.2.refs_9_) | copy-start | bytes 331780
  29.6 0.7 copy-start.4
  73.5 3.9 %collective-permute-start.4 = (f32[40,40]{0,1:T(8,128)S(1)}, f32[40,40]{0,1:T(8,128)S(1)}, u32[]{:S(2)}, u32[]{:S(2)}) collective-permute-start(f32[40,40]{0,1:T(8,128)S(1)} %fusion.4), channel_id=1, source_target_pairs={{0,32},{8,40},{16,48},{24,56},{32,0},{40,8},{48,16},{56,24},{64,96... | collective-permute-start | bytes 19208 | tf_op jit(solution)/shard_map/ppermute | solution.py:134
  77.3 5.0 %collective-permute-start.5 = (f32[40,40]{0,1:T(8,128)S(1)}, f32[40,40]{0,1:T(8,128)S(1)}, u32[]{:S(2)}, u32[]{:S(2)}) collective-permute-start(f32[40,40]{0,1:T(8,128)S(1)} %add.48), channel_id=1, source_target_pairs={{0,96},{8,104},{16,112},{24,120},{32,64},{40,72},{48,80},{56,88},{... | collective-permute-start | bytes 19208 | tf_op jit(solution)/shard_map/ppermute | solution.py:134
  82.3 3.8 %collective-permute-start.6 = (f32[40,40]{0,1:T(8,128)S(1)}, f32[40,40]{0,1:T(8,128)S(1)}, u32[]{:S(2)}, u32[]{:S(2)}) collective-permute-start(f32[40,40]{0,1:T(8,128)S(1)} %add.49), channel_id=1, source_target_pairs={{0,8},{8,0},{16,24},{24,16},{32,40},{40,32},{48,56},{56,48},{64,72... | collective-permute-start | bytes 19208 | tf_op jit(solution)/shard_map/ppermute | solution.py:134
  86.1 5.0 %collective-permute-start.7 = (f32[40,40]{0,1:T(8,128)S(1)}, f32[40,40]{0,1:T(8,128)S(1)}, u32[]{:S(2)}, u32[]{:S(2)}) collective-permute-start(f32[40,40]{0,1:T(8,128)S(1)} %add.50), channel_id=1, source_target_pairs={{0,24},{8,16},{16,8},{24,0},{32,56},{40,48},{48,40},{56,32},{64,88... | collective-permute-start | bytes 19208 | tf_op jit(solution)/shard_map/ppermute | solution.py:134
  91.1 1.2 collective-permute-start.8
  92.3 3.8 %collective-permute-start.9 = (f32[40,40]{0,1:T(8,128)S(1)}, f32[40,40]{0,1:T(8,128)S(1)}, u32[]{:S(2)}, u32[]{:S(2)}) collective-permute-start(f32[40,40]{0,1:T(8,128)S(1)} %add.52), channel_id=1, source_target_pairs={{0,2},{1,3},{2,0},{3,1},{4,6},{5,7},{6,4},{7,5},{8,10},{9,11},{10,... | collective-permute-start | bytes 19208 | tf_op jit(solution)/shard_map/ppermute | solution.py:134
  96.1 5.0 %collective-permute-start.10 = (f32[40,40]{0,1:T(8,128)S(1)}, f32[40,40]{0,1:T(8,128)S(1)}, u32[]{:S(2)}, u32[]{:S(2)}) collective-permute-start(f32[40,40]{0,1:T(8,128)S(1)} %add.53), channel_id=1, source_target_pairs={{0,6},{1,7},{2,4},{3,5},{4,2},{5,3},{6,0},{7,1},{8,14},{9,15},{10,... | collective-permute-start | bytes 19208 | tf_op jit(solution)/shard_map/ppermute | solution.py:134
  118.7 4.2 %copy-start = (f32[40,65536]{1,0:T(8,128)}, f32[40,65536]{1,0:T(8,128)S(1)}, u32[]{:S(2)}) copy-start(f32[40,65536]{1,0:T(8,128)S(1)} %fusion.5) | copy-start | bytes 31457284
  122.9 3.9 %collective-permute-start.11 = (f32[40,40]{0,1:T(8,128)S(1)}, f32[40,40]{0,1:T(8,128)S(1)}, u32[]{:S(2)}, u32[]{:S(2)}) collective-permute-start(f32[40,40]{0,1:T(8,128)S(1)} %fusion.6), channel_id=1, source_target_pairs={{0,32},{8,40},{16,48},{24,56},{32,0},{40,8},{48,16},{56,24},{64,96... | collective-permute-start | bytes 19208 | tf_op jit(solution)/shard_map/ppermute | solution.py:134
  126.8 5.0 %collective-permute-start.12 = (f32[40,40]{0,1:T(8,128)S(1)}, f32[40,40]{0,1:T(8,128)S(1)}, u32[]{:S(2)}, u32[]{:S(2)}) collective-permute-start(f32[40,40]{0,1:T(8,128)S(1)} %add.56), channel_id=1, source_target_pairs={{0,96},{8,104},{16,112},{24,120},{32,64},{40,72},{48,80},{56,88},{... | collective-permute-start | bytes 19208 | tf_op jit(solution)/shard_map/ppermute | solution.py:134
  131.8 3.8 %collective-permute-start.13 = (f32[40,40]{0,1:T(8,128)S(1)}, f32[40,40]{0,1:T(8,128)S(1)}, u32[]{:S(2)}, u32[]{:S(2)}) collective-permute-start(f32[40,40]{0,1:T(8,128)S(1)} %add.57), channel_id=1, source_target_pairs={{0,8},{8,0},{16,24},{24,16},{32,40},{40,32},{48,56},{56,48},{64,72... | collective-permute-start | bytes 19208 | tf_op jit(solution)/shard_map/ppermute | solution.py:134
  135.5 5.0 %collective-permute-start.14 = (f32[40,40]{0,1:T(8,128)S(1)}, f32[40,40]{0,1:T(8,128)S(1)}, u32[]{:S(2)}, u32[]{:S(2)}) collective-permute-start(f32[40,40]{0,1:T(8,128)S(1)} %add.58), channel_id=1, source_target_pairs={{0,24},{8,16},{16,8},{24,0},{32,56},{40,48},{48,40},{56,32},{64,88... | collective-permute-start | bytes 19208 | tf_op jit(solution)/shard_map/ppermute | solution.py:134
  140.5 1.2 collective-permute-start.15
  141.7 3.8 %collective-permute-start.16 = (f32[40,40]{0,1:T(8,128)S(1)}, f32[40,40]{0,1:T(8,128)S(1)}, u32[]{:S(2)}, u32[]{:S(2)}) collective-permute-start(f32[40,40]{0,1:T(8,128)S(1)} %add.60), channel_id=1, source_target_pairs={{0,2},{1,3},{2,0},{3,1},{4,6},{5,7},{6,4},{7,5},{8,10},{9,11},{10,... | collective-permute-start | bytes 19208 | tf_op jit(solution)/shard_map/ppermute | solution.py:134
  145.5 5.0 %collective-permute-start.17 = (f32[40,40]{0,1:T(8,128)S(1)}, f32[40,40]{0,1:T(8,128)S(1)}, u32[]{:S(2)}, u32[]{:S(2)}) collective-permute-start(f32[40,40]{0,1:T(8,128)S(1)} %add.61), channel_id=1, source_target_pairs={{0,6},{1,7},{2,4},{3,5},{4,2},{5,3},{6,0},{7,1},{8,14},{9,15},{10,... | collective-permute-start | bytes 19208 | tf_op jit(solution)/shard_map/ppermute | solution.py:134
  163.7 6.0 %copy-start.5 = (f32[40,40]{1,0:T(8,128)S(1)}, f32[40,40]{1,0:T(8,128)}, u32[]{:S(2)}) copy-start(f32[40,40]{1,0:T(8,128)} %get-tuple-element.8) | copy-start | bytes 19204
  163.8 6.0 %copy-start.6 = (f32[40,40]{1,0:T(8,128)S(1)}, f32[40,40]{1,0:T(8,128)}, u32[]{:S(2)}) copy-start(f32[40,40]{1,0:T(8,128)} %get-tuple-element.13) | copy-start | bytes 19204

commit v6 on v5

--- a/solution.py
+++ b/solution.py
@@ -147,13 +147,19 @@
 DIRECTIONS = ((1, 1), (1, -1), (2, 1), (2, -1), (0, 1), (0, -1))
 
 
+def store_plane(out_ref, power, r, z, plane):
+    rhs = pl.num_programs(0)
+    rows = plane.shape[0]
+    out_ref[power, pl.ds(z * rows * rhs + r, rows, stride=rhs), :] = plane
+
+
 def powers_kernel(*refs):
     block_ref, coef_ref, react_ref = refs[:3]
     x_strips = refs[3:9]
     yn_ref, yp_ref = refs[9:11]
     out_ref, weight_ref, react_pad_ref = refs[11:14]
     buffers = refs[14:]
-    depth, rows, cols = (out_ref.shape[2], out_ref.shape[3], out_ref.shape[4])
+    depth, rows, cols = block_ref.shape[1:]
     r = pl.program_id(0)
 
     def planes(core_of, group, first_plane):
@@ -176,7 +182,8 @@
             weight_ref[d] = 0.5 * (coef + neighbour(coef, direction))
         react_pad_ref[...] = planes(lambda z: react_ref[z], 2, rhs * depth + depth)
 
-    out_ref[0, 0] = block_ref[0]
+    for z in range(depth):
+        store_plane(out_ref, 0, r, z, block_ref[0, z])
     buffers[0][...] = planes(lambda z: block_ref[0, z], 0, r * depth)
     for power in range(1, STEPS + 1):
         source, target = (buffers[(power - 1) % 2], buffers[power % 2])
@@ -192,7 +199,7 @@
             current = (react_pad_ref[z] * current + running - center_shift * current) * step_scale
             if power < STEPS:
                 target[z] = current
-            out_ref[power, 0, z] = current[:rows, :cols]
+            store_plane(out_ref, power, r, z, current[:rows, :cols])
 
 
 def krylov_powers(start_block, conductivity, reaction, strips):
@@ -214,8 +221,8 @@
         ]
         + strip_specs
         + [packed, packed],
-        out_specs=pl.BlockSpec((STEPS + 1, 1, depth, rows, cols), lambda r: (0, r, 0, 0, 0)),
-        out_shape=jax.ShapeDtypeStruct((STEPS + 1, rhs, depth, rows, cols), jnp.float32),
+        out_specs=pl.BlockSpec((STEPS + 1, depth * rows * rhs, cols), lambda r: (0, 0, 0)),
+        out_shape=jax.ShapeDtypeStruct((STEPS + 1, depth * rows * rhs, cols), jnp.float32),
         scratch_shapes=[
             pltpu.VMEM((len(DIRECTIONS), depth, rows + 2 * width, LANES), jnp.float32),
             pltpu.VMEM((depth, rows + 2 * width, LANES), jnp.float32),
@@ -269,7 +276,10 @@
     )
     rhs, depth, rows, cols = start_block.shape
     strips = halo_strips(start_block, conductivity, reaction)
-    krylov = krylov_powers(start_block, conductivity, reaction, strips).reshape(COLS, -1)
+    tiles = krylov_powers(start_block, conductivity, reaction, strips)
+    krylov = (
+        tiles.reshape(STEPS + 1, depth * rows, rhs, cols).transpose(0, 2, 1, 3).reshape(COLS, -1)
+    )
     local_gram = jnp.dot(
         krylov, krylov.T, precision=lax.Precision.HIGHEST, preferred_element_type=jnp.float32
     )

time: 171 us -> 166 us (0.971)
  local copies, waits for them, and re-layouts: 19.9 us -> 9.47 us
  Pallas kernels: 35.6 us -> 41 us
    reshape x1 -> x0, local copies, waits for them, and re-layouts: 10.4 us -> none  [body(): krylov_powers(start_block, conductivity, reaction, strips).reshape(COLS, -1)]
    pallas_call x1, Pallas kernels: 20.9 us -> 26.4 us  [krylov_powers(): pl.pallas_call(powers_kernel, grid=(rhs,), in_specs=[pl.BlockSpec((1, dep...]
where the time goes in v6:
time: 166 us
  waiting for transfers between devices  68.4 us (41%)
  Pallas kernels  41 us (25%)
  matrix products  35.5 us (21%)
  local copies, waits for them, and re-layouts  9.47 us (6%)
  starting transfers between devices  9.01 us (5%)
    ppermute x14, waiting for transfers between devices, tree_sum(): lax.ppermute(value, axis, fold_pairs(count, stride, span, fold))  53.9 us
    pallas_call x1, Pallas kernels, krylov_powers(): pl.pallas_call(powers_kernel, grid=(rhs,), in_specs=[pl.BlockSpec((1, dep...  26.4 us
    dot_general x1, matrix products, body(): jnp.dot(krylov, krylov.T, precision=lax.Precision.HIGHEST, preferred_elem...  11.8 us
    dot_general x1, matrix products, body(): jnp.dot(inverse_first, krylov, precision=lax.Precision.HIGHEST, preferred...  11.6 us
    pallas_call x2, Pallas kernels, cholesky_factors(): return pl.pallas_call(factor_kernel, out_shape=[square, square])(symmetric)  10.6 us
    unnamed x15, local copies, waits for them, and re-layouts  7.31 us
    dot_general x1, matrix products, body(): jnp.dot(inverse_second, first_q, precision=lax.Precision.HIGH, preferred_...  7.14 us
    ppermute x1, waiting for transfers between devices, halo_strips(): x_prev = lax.ppermute(last, 'gx', x_next_pairs)  5.63 us
  transfers between devices with their start and end apart: 18, of which 18 were waited for; matrix products, arithmetic and copies ran while one was open for 0% of the time, Pallas kernels for 0%

profile of v6, /device:TPU:0, one launch (start us, length us, event | category | flops | bytes accessed | tf_op | source)
XLA Modules:
  0.0 165.6 jit_solution(7669857486508157328)
XLA Ops:
  0.6 1.1 fusion.5
  1.7 0.9 fusion.6
  2.6 5.4 %collective-permute-start = (f32[80,4,128]{2,1,0:T(4,128)S(1)}, f32[80,4,128]{2,1,0:T(4,128)S(1)}, u32[]{:S(2)}, u32[]{:S(2)}) collective-permute-start(f32[80,4,128]{2,1,0:T(4,128)S(1)} %pad_maximum_fusion), channel_id=1, source_target_pairs={{8,0},{16,8},{24,16},{32,24},{40,32},{48,40},{56,48},{64,56},{72,6... | collective-permute-start | bytes 491528 | tf_op jit(solution)/shard_map/ppermute | solution.py:91
  8.1 3.3 %collective-permute-done.xn_ref.refs_3_.refs_5_.refs_7_ = f32[80,4,128]{2,1,0:T(4,128)S(1)} collective-permute-done((f32[80,4,128]{2,1,0:T(4,128)S(1)}, f32[80,4,128]{2,1,0:T(4,128)S(1)}, u32[]{:S(2)}, u32[]{:S(2)}) %collective-permute-start) | collective-permute-done | bytes 163872 | tf_op jit(solution)/shard_map/ppermute | solution.py:91
  11.4 5.6 %collective-permute-done.1.xp_ref.refs_4_.refs_6_.refs_8_ = f32[80,4,128]{2,1,0:T(4,128)S(1)} collective-permute-done((f32[80,4,128]{2,1,0:T(4,128)S(1)}, f32[80,4,128]{2,1,0:T(4,128)S(1)}, u32[]{:S(2)}, u32[]{:S(2)}) %collective-permute-start.1) | collective-permute-done | bytes 163872 | tf_op jit(solution)/shard_map/ppermute | solution.py:92
  17.7 4.0 %shard_map.58 = (f32[3,72,128]{2,1,0:T(8,128)}, f32[3,72,128]{2,1,0:T(8,128)}) custom-call(f32[8,8,64,128]{3,2,1,0:T(8,128)} %refs_0_.1, f32[8,64,128]{2,1,0:T(8,128)} %refs_1_.1, f32[8,64,128]{2,1,0:T(8,128)} %refs_2_.1, f32[80,4,128]{2,1,0:T(4,128)} %copy-done.1, f32[80,4,128]{2,1,0:T(4,128)} %copy-done.2), custom_call_target="tpu_custom_call" | custom-call | tf_op jit(solution)/shard_map/pallas_call | solution.py:72
  21.8 2.3 %collective-permute-start.2 = (f32[3,72,128]{2,1,0:T(8,128)}, f32[3,72,128]{2,1,0:T(8,128)S(1)}, u32[]{:S(2)}, u32[]{:S(2)}) collective-permute-start(f32[3,72,128]{2,1,0:T(8,128)} %get-tuple-element.9), channel_id=1, source_target_pairs={{1,0},{2,1},{3,2},{4,3},{5,4},{6,5},{7,6},{0,7},{9,8},{10,9},{11,1... | collective-permute-start | bytes 331784 | tf_op jit(solution)/shard_map/ppermute | solution.py:95
  24.1 2.6 %collective-permute-done.2.refs_9_ = f32[3,72,128]{2,1,0:T(8,128)S(1)} collective-permute-done((f32[3,72,128]{2,1,0:T(8,128)}, f32[3,72,128]{2,1,0:T(8,128)S(1)}, u32[]{:S(2)}, u32[]{:S(2)}) %collective-permute-start.2) | collective-permute-done | bytes 110624 | tf_op jit(solution)/shard_map/ppermute | solution.py:95
  26.7 2.9 %collective-permute-done.3.refs_10_ = f32[3,72,128]{2,1,0:T(8,128)S(1)} collective-permute-done((f32[3,72,128]{2,1,0:T(8,128)}, f32[3,72,128]{2,1,0:T(8,128)S(1)}, u32[]{:S(2)}, u32[]{:S(2)}) %collective-permute-start.3) | collective-permute-done | bytes 110624 | tf_op jit(solution)/shard_map/ppermute | solution.py:96
  30.3 26.4 %shard_map.59 = f32[5,4096,128]{2,1,0:T(8,128)} custom-call(f32[8,8,64,128]{3,2,1,0:T(8,128)} %refs_0_.1, f32[8,64,128]{2,1,0:T(8,128)} %refs_1_.1, f32[8,64,128]{2,1,0:T(8,128)} %refs_2_.1, f32[80,4,128]{2,1,0:T(4,128)} %copy-done.1, f32[80,4,128]{2,1,0:T(4,128)} %copy-done.2, f32[80,4,128]{2,1,0:T(4,128)} %copy-done.1, f32[80,4,128]{2,1,0:T(4,128)} %copy-done.2, ...), custom_call_target="tpu_custom_call" | custom-call | tf_op jit(solution)/shard_map/pallas_call | solution.py:214
  56.7 11.8 %fusion.2 = f32[40,40]{0,1:T(8,128)S(1)} fusion(f32[5,4096,128]{2,1,0:T(8,128)} %shard_map.59), kind=kOutput, calls=%fused_computation.2 | convolution fusion | flops 1258291200 | bytes 10492160 | tf_op jit(solution)/shard_map/dot_general | solution.py:283
  68.6 3.8 %collective-permute-done.4 = f32[40,40]{0,1:T(8,128)S(1)} collective-permute-done((f32[40,40]{0,1:T(8,128)S(1)}, f32[40,40]{0,1:T(8,128)S(1)}, u32[]{:S(2)}, u32[]{:S(2)}) %collective-permute-start.4) | collective-permute-done | bytes 6432 | tf_op jit(solution)/shard_map/ppermute | solution.py:134
  72.4 5.0 %collective-permute-done.5 = f32[40,40]{0,1:T(8,128)S(1)} collective-permute-done((f32[40,40]{0,1:T(8,128)S(1)}, f32[40,40]{0,1:T(8,128)S(1)}, u32[]{:S(2)}, u32[]{:S(2)}) %collective-permute-start.5) | collective-permute-done | bytes 6432 | tf_op jit(solution)/shard_map/ppermute | solution.py:134
  77.4 3.8 %collective-permute-done.6 = f32[40,40]{0,1:T(8,128)S(1)} collective-permute-done((f32[40,40]{0,1:T(8,128)S(1)}, f32[40,40]{0,1:T(8,128)S(1)}, u32[]{:S(2)}, u32[]{:S(2)}) %collective-permute-start.6) | collective-permute-done | bytes 6432 | tf_op jit(solution)/shard_map/ppermute | solution.py:134
  81.2 5.0 %collective-permute-done.7 = f32[40,40]{0,1:T(8,128)S(1)} collective-permute-done((f32[40,40]{0,1:T(8,128)S(1)}, f32[40,40]{0,1:T(8,128)S(1)}, u32[]{:S(2)}, u32[]{:S(2)}) %collective-permute-start.7) | collective-permute-done | bytes 6432 | tf_op jit(solution)/shard_map/ppermute | solution.py:134
  86.2 1.2 collective-permute-done.8
  87.4 3.8 %collective-permute-done.9 = f32[40,40]{0,1:T(8,128)S(1)} collective-permute-done((f32[40,40]{0,1:T(8,128)S(1)}, f32[40,40]{0,1:T(8,128)S(1)}, u32[]{:S(2)}, u32[]{:S(2)}) %collective-permute-start.9) | collective-permute-done | bytes 6432 | tf_op jit(solution)/shard_map/ppermute | solution.py:134
  91.7 4.4 %collective-permute-done.10 = f32[40,40]{0,1:T(8,128)S(1)} collective-permute-done((f32[40,40]{0,1:T(8,128)S(1)}, f32[40,40]{0,1:T(8,128)S(1)}, u32[]{:S(2)}, u32[]{:S(2)}) %collective-permute-start.10) | collective-permute-done | bytes 6432 | tf_op jit(solution)/shard_map/ppermute | solution.py:134
  96.9 5.3 %shard_map.60 = (f32[40,40]{1,0:T(8,128)}, f32[40,40]{1,0:T(8,128)}) custom-call(f32[40,40]{1,0:T(8,128)} %fusion.4.gram_ref), custom_call_target="tpu_custom_call" | custom-call | tf_op jit(solution)/shard_map/pallas_call | solution.py:266
  102.1 11.6 %fusion = f32[40,65536]{1,0:T(8,128)S(1)} fusion(f32[40,40]{1,0:T(8,128)} %get-tuple-element.11, f32[5,4096,128]{2,1,0:T(8,128)} %shard_map.59), kind=kOutput, calls=%fused_computation | convolution fusion | flops 1258291200 | bytes 20977920 | tf_op jit(solution)/shard_map/dot_general | solution.py:287
  113.7 4.2 %fusion.8 = f32[40,40]{0,1:T(8,128)S(1)} fusion(f32[40,65536]{1,0:T(8,128)S(1)} %fusion), kind=kOutput, calls=%fused_computation.16 | convolution fusion | flops 629145600 | bytes 10492160 | tf_op jit(solution)/shard_map/dot_general | solution.py:290
  118.0 3.8 %collective-permute-done.11 = f32[40,40]{0,1:T(8,128)S(1)} collective-permute-done((f32[40,40]{0,1:T(8,128)S(1)}, f32[40,40]{0,1:T(8,128)S(1)}, u32[]{:S(2)}, u32[]{:S(2)}) %collective-permute-start.11) | collective-permute-done | bytes 6432 | tf_op jit(solution)/shard_map/ppermute | solution.py:134
  121.8 5.0 %collective-permute-done.12 = f32[40,40]{0,1:T(8,128)S(1)} collective-permute-done((f32[40,40]{0,1:T(8,128)S(1)}, f32[40,40]{0,1:T(8,128)S(1)}, u32[]{:S(2)}, u32[]{:S(2)}) %collective-permute-start.12) | collective-permute-done | bytes 6432 | tf_op jit(solution)/shard_map/ppermute | solution.py:134
  126.8 3.8 %collective-permute-done.13 = f32[40,40]{0,1:T(8,128)S(1)} collective-permute-done((f32[40,40]{0,1:T(8,128)S(1)}, f32[40,40]{0,1:T(8,128)S(1)}, u32[]{:S(2)}, u32[]{:S(2)}) %collective-permute-start.13) | collective-permute-done | bytes 6432 | tf_op jit(solution)/shard_map/ppermute | solution.py:134
  130.6 5.0 %collective-permute-done.14 = f32[40,40]{0,1:T(8,128)S(1)} collective-permute-done((f32[40,40]{0,1:T(8,128)S(1)}, f32[40,40]{0,1:T(8,128)S(1)}, u32[]{:S(2)}, u32[]{:S(2)}) %collective-permute-start.14) | collective-permute-done | bytes 6432 | tf_op jit(solution)/shard_map/ppermute | solution.py:134
  135.6 1.2 collective-permute-done.15
  136.8 3.8 %collective-permute-done.16 = f32[40,40]{0,1:T(8,128)S(1)} collective-permute-done((f32[40,40]{0,1:T(8,128)S(1)}, f32[40,40]{0,1:T(8,128)S(1)}, u32[]{:S(2)}, u32[]{:S(2)}) %collective-permute-start.16) | collective-permute-done | bytes 6432 | tf_op jit(solution)/shard_map/ppermute | solution.py:134
  141.1 4.5 %collective-permute-done.17 = f32[40,40]{0,1:T(8,128)S(1)} collective-permute-done((f32[40,40]{0,1:T(8,128)S(1)}, f32[40,40]{0,1:T(8,128)S(1)}, u32[]{:S(2)}, u32[]{:S(2)}) %collective-permute-start.17) | collective-permute-done | bytes 6432 | tf_op jit(solution)/shard_map/ppermute | solution.py:134
  146.4 5.3 %shard_map.61 = (f32[40,40]{1,0:T(8,128)}, f32[40,40]{1,0:T(8,128)}) custom-call(f32[40,40]{1,0:T(8,128)} %broadcast_multiply_fusion.gram_ref), custom_call_target="tpu_custom_call" | custom-call | tf_op jit(solution)/shard_map/pallas_call | solution.py:266
  151.7 7.1 %convolution_bitcast_fusion = f32[5,8,512,128]{3,1,2,0:T(8,128)S(1)} fusion(f32[40,40]{1,0:T(8,128)} %get-tuple-element.12, f32[40,65536]{1,0:T(8,128)} %copy-done), kind=kOutput, calls=%fused_computation.4 | convolution fusion | flops 629145600 | bytes 20977920 | tf_op jit(solution)/shard_map/dot_general | solution.py:294
  158.8 6.0 %copy.15 = f32[5,8,512,128]{3,2,1,0:T(8,128)} copy(f32[5,8,512,128]{3,1,2,0:T(8,128)S(1)} %convolution_bitcast_fusion) | data formatting | bytes 20971520
  164.8 0.8 fusion.9
  (52 shorter events, 4.3 us)
Async XLA Ops:
  2.6 8.8 %collective-permute-start = (f32[80,4,128]{2,1,0:T(4,128)S(1)}, f32[80,4,128]{2,1,0:T(4,128)S(1)}, u32[]{:S(2)}, u32[]{:S(2)}) collective-permute-start(f32[80,4,128]{2,1,0:T(4,128)S(1)} %pad_maximum_fusion), channel_id=1, source_target_pairs={{8,0},{16,8},{24,16},{32,24},{40,32},{48,40},{56,48},{64,56},{72,6... | collective-permute-start | bytes 491528 | tf_op jit(solution)/shard_map/ppermute | solution.py:91
  8.0 9.0 %collective-permute-start.1 = (f32[80,4,128]{2,1,0:T(4,128)S(1)}, f32[80,4,128]{2,1,0:T(4,128)S(1)}, u32[]{:S(2)}, u32[]{:S(2)}) collective-permute-start(f32[80,4,128]{2,1,0:T(4,128)S(1)} %pad_maximum_fusion.1), channel_id=1, source_target_pairs={{0,8},{8,16},{16,24},{24,32},{32,40},{40,48},{48,56},{56,64},{64,7... | collective-permute-start | bytes 491528 | tf_op jit(solution)/shard_map/ppermute | solution.py:92
  11.4 5.6 %copy-start.1 = (f32[80,4,128]{2,1,0:T(4,128)}, f32[80,4,128]{2,1,0:T(4,128)S(1)}, u32[]{:S(2)}) copy-start(f32[80,4,128]{2,1,0:T(4,128)S(1)} %collective-permute-done.xn_ref.refs_3_.refs_5_.refs_7_) | copy-start | bytes 491524
  17.1 0.7 copy-start.2
  21.8 4.9 %collective-permute-start.2 = (f32[3,72,128]{2,1,0:T(8,128)}, f32[3,72,128]{2,1,0:T(8,128)S(1)}, u32[]{:S(2)}, u32[]{:S(2)}) collective-permute-start(f32[3,72,128]{2,1,0:T(8,128)} %get-tuple-element.9), channel_id=1, source_target_pairs={{1,0},{2,1},{3,2},{4,3},{5,4},{6,5},{7,6},{0,7},{9,8},{10,9},{11,1... | collective-permute-start | bytes 331784 | tf_op jit(solution)/shard_map/ppermute | solution.py:95
  24.1 5.6 %collective-permute-start.3 = (f32[3,72,128]{2,1,0:T(8,128)}, f32[3,72,128]{2,1,0:T(8,128)S(1)}, u32[]{:S(2)}, u32[]{:S(2)}) collective-permute-start(f32[3,72,128]{2,1,0:T(8,128)} %get-tuple-element.10), channel_id=1, source_target_pairs={{0,1},{1,2},{2,3},{3,4},{4,5},{5,6},{6,7},{7,0},{8,9},{9,10},{10,1... | collective-permute-start | bytes 331784 | tf_op jit(solution)/shard_map/ppermute | solution.py:96
  26.7 3.0 %copy-start.3 = (f32[3,72,128]{2,1,0:T(8,128)}, f32[3,72,128]{2,1,0:T(8,128)S(1)}, u32[]{:S(2)}) copy-start(f32[3,72,128]{2,1,0:T(8,128)S(1)} %collective-permute-done.2.refs_9_) | copy-start | bytes 331780
  29.7 0.7 copy-start.4
  68.5 3.9 %collective-permute-start.4 = (f32[40,40]{0,1:T(8,128)S(1)}, f32[40,40]{0,1:T(8,128)S(1)}, u32[]{:S(2)}, u32[]{:S(2)}) collective-permute-start(f32[40,40]{0,1:T(8,128)S(1)} %fusion.2), channel_id=1, source_target_pairs={{0,32},{8,40},{16,48},{24,56},{32,0},{40,8},{48,16},{56,24},{64,96... | collective-permute-start | bytes 19208 | tf_op jit(solution)/shard_map/ppermute | solution.py:134
  72.4 5.0 %collective-permute-start.5 = (f32[40,40]{0,1:T(8,128)S(1)}, f32[40,40]{0,1:T(8,128)S(1)}, u32[]{:S(2)}, u32[]{:S(2)}) collective-permute-start(f32[40,40]{0,1:T(8,128)S(1)} %add.48), channel_id=1, source_target_pairs={{0,96},{8,104},{16,112},{24,120},{32,64},{40,72},{48,80},{56,88},{... | collective-permute-start | bytes 19208 | tf_op jit(solution)/shard_map/ppermute | solution.py:134
  77.4 3.8 %collective-permute-start.6 = (f32[40,40]{0,1:T(8,128)S(1)}, f32[40,40]{0,1:T(8,128)S(1)}, u32[]{:S(2)}, u32[]{:S(2)}) collective-permute-start(f32[40,40]{0,1:T(8,128)S(1)} %add.49), channel_id=1, source_target_pairs={{0,8},{8,0},{16,24},{24,16},{32,40},{40,32},{48,56},{56,48},{64,72... | collective-permute-start | bytes 19208 | tf_op jit(solution)/shard_map/ppermute | solution.py:134
  81.2 5.0 %collective-permute-start.7 = (f32[40,40]{0,1:T(8,128)S(1)}, f32[40,40]{0,1:T(8,128)S(1)}, u32[]{:S(2)}, u32[]{:S(2)}) collective-permute-start(f32[40,40]{0,1:T(8,128)S(1)} %add.50), channel_id=1, source_target_pairs={{0,24},{8,16},{16,8},{24,0},{32,56},{40,48},{48,40},{56,32},{64,88... | collective-permute-start | bytes 19208 | tf_op jit(solution)/shard_map/ppermute | solution.py:134
  86.2 1.2 collective-permute-start.8
  87.4 3.8 %collective-permute-start.9 = (f32[40,40]{0,1:T(8,128)S(1)}, f32[40,40]{0,1:T(8,128)S(1)}, u32[]{:S(2)}, u32[]{:S(2)}) collective-permute-start(f32[40,40]{0,1:T(8,128)S(1)} %add.52), channel_id=1, source_target_pairs={{0,2},{1,3},{2,0},{3,1},{4,6},{5,7},{6,4},{7,5},{8,10},{9,11},{10,... | collective-permute-start | bytes 19208 | tf_op jit(solution)/shard_map/ppermute | solution.py:134
  91.2 5.0 %collective-permute-start.10 = (f32[40,40]{0,1:T(8,128)S(1)}, f32[40,40]{0,1:T(8,128)S(1)}, u32[]{:S(2)}, u32[]{:S(2)}) collective-permute-start(f32[40,40]{0,1:T(8,128)S(1)} %add.53), channel_id=1, source_target_pairs={{0,6},{1,7},{2,4},{3,5},{4,2},{5,3},{6,0},{7,1},{8,14},{9,15},{10,... | collective-permute-start | bytes 19208 | tf_op jit(solution)/shard_map/ppermute | solution.py:134
  113.7 4.2 %copy-start = (f32[40,65536]{1,0:T(8,128)}, f32[40,65536]{1,0:T(8,128)S(1)}, u32[]{:S(2)}) copy-start(f32[40,65536]{1,0:T(8,128)S(1)} %fusion) | copy-start | bytes 31457284
  117.9 3.9 %collective-permute-start.11 = (f32[40,40]{0,1:T(8,128)S(1)}, f32[40,40]{0,1:T(8,128)S(1)}, u32[]{:S(2)}, u32[]{:S(2)}) collective-permute-start(f32[40,40]{0,1:T(8,128)S(1)} %fusion.8), channel_id=1, source_target_pairs={{0,32},{8,40},{16,48},{24,56},{32,0},{40,8},{48,16},{56,24},{64,96... | collective-permute-start | bytes 19208 | tf_op jit(solution)/shard_map/ppermute | solution.py:134
  121.8 5.0 %collective-permute-start.12 = (f32[40,40]{0,1:T(8,128)S(1)}, f32[40,40]{0,1:T(8,128)S(1)}, u32[]{:S(2)}, u32[]{:S(2)}) collective-permute-start(f32[40,40]{0,1:T(8,128)S(1)} %add.56), channel_id=1, source_target_pairs={{0,96},{8,104},{16,112},{24,120},{32,64},{40,72},{48,80},{56,88},{... | collective-permute-start | bytes 19208 | tf_op jit(solution)/shard_map/ppermute | solution.py:134
  126.8 3.8 %collective-permute-start.13 = (f32[40,40]{0,1:T(8,128)S(1)}, f32[40,40]{0,1:T(8,128)S(1)}, u32[]{:S(2)}, u32[]{:S(2)}) collective-permute-start(f32[40,40]{0,1:T(8,128)S(1)} %add.57), channel_id=1, source_target_pairs={{0,8},{8,0},{16,24},{24,16},{32,40},{40,32},{48,56},{56,48},{64,72... | collective-permute-start | bytes 19208 | tf_op jit(solution)/shard_map/ppermute | solution.py:134
  130.6 5.0 %collective-permute-start.14 = (f32[40,40]{0,1:T(8,128)S(1)}, f32[40,40]{0,1:T(8,128)S(1)}, u32[]{:S(2)}, u32[]{:S(2)}) collective-permute-start(f32[40,40]{0,1:T(8,128)S(1)} %add.58), channel_id=1, source_target_pairs={{0,24},{8,16},{16,8},{24,0},{32,56},{40,48},{48,40},{56,32},{64,88... | collective-permute-start | bytes 19208 | tf_op jit(solution)/shard_map/ppermute | solution.py:134
  135.6 1.2 collective-permute-start.15
  136.8 3.8 %collective-permute-start.16 = (f32[40,40]{0,1:T(8,128)S(1)}, f32[40,40]{0,1:T(8,128)S(1)}, u32[]{:S(2)}, u32[]{:S(2)}) collective-permute-start(f32[40,40]{0,1:T(8,128)S(1)} %add.60), channel_id=1, source_target_pairs={{0,2},{1,3},{2,0},{3,1},{4,6},{5,7},{6,4},{7,5},{8,10},{9,11},{10,... | collective-permute-start | bytes 19208 | tf_op jit(solution)/shard_map/ppermute | solution.py:134
  140.6 5.0 %collective-permute-start.17 = (f32[40,40]{0,1:T(8,128)S(1)}, f32[40,40]{0,1:T(8,128)S(1)}, u32[]{:S(2)}, u32[]{:S(2)}) collective-permute-start(f32[40,40]{0,1:T(8,128)S(1)} %add.61), channel_id=1, source_target_pairs={{0,6},{1,7},{2,4},{3,5},{4,2},{5,3},{6,0},{7,1},{8,14},{9,15},{10,... | collective-permute-start | bytes 19208 | tf_op jit(solution)/shard_map/ppermute | solution.py:134
  158.8 6.0 %copy-start.5 = (f32[40,40]{1,0:T(8,128)S(1)}, f32[40,40]{1,0:T(8,128)}, u32[]{:S(2)}) copy-start(f32[40,40]{1,0:T(8,128)} %get-tuple-element.8) | copy-start | bytes 19204
  158.8 6.0 %copy-start.6 = (f32[40,40]{1,0:T(8,128)S(1)}, f32[40,40]{1,0:T(8,128)}, u32[]{:S(2)}) copy-start(f32[40,40]{1,0:T(8,128)} %get-tuple-element.13) | copy-start | bytes 19204

commit v7 on v6

--- a/solution.py
+++ b/solution.py
@@ -187,16 +187,18 @@
     buffers[0][...] = planes(lambda z: block_ref[0, z], 0, r * depth)
     for power in range(1, STEPS + 1):
         source, target = (buffers[(power - 1) % 2], buffers[power % 2])
+        keep = (slice(None), slice(None)) if power < STEPS else (slice(0, rows), slice(0, cols))
         for z in range(depth):
-            current = source[z]
+            whole = source[z]
+            current = whole[keep]
             running = jnp.zeros_like(current)
             for d, (axis, offset) in enumerate(DIRECTIONS):
                 if axis == 0:
-                    beside = source[(z + offset) % depth]
+                    beside = source[(z + offset) % depth][keep]
                 else:
-                    beside = pltpu.roll(current, (-offset) % current.shape[axis - 1], axis - 1)
-                running = running + weight_ref[d, z] * (current - beside)
-            current = (react_pad_ref[z] * current + running - center_shift * current) * step_scale
+                    beside = pltpu.roll(whole, (-offset) % whole.shape[axis - 1], axis - 1)[keep]
+                running = running + weight_ref[d, z][keep] * (current - beside)
+            current = (react_pad_ref[z][keep] * current + running - center_shift * current) * step_scale
             if power < STEPS:
                 target[z] = current
             store_plane(out_ref, power, r, z, current[:rows, :cols])
@@ -241,16 +243,16 @@
     lower = jnp.zeros((size, size), jnp.float32)
     upper = jnp.zeros((size, size), jnp.float32)
     for j in range(size):
-        pivot = jnp.sqrt(work[j : j + 1, j : j + 1])
-        column = jnp.where(rows[:, j : j + 1] >= j, work[:, j : j + 1] / pivot, 0.0)
-        row = jnp.where(cols[j : j + 1, :] >= j, work[j : j + 1, :] / pivot, 0.0)
+        scale = 1.0 / jnp.sqrt(work[j : j + 1, j : j + 1])
+        column = jnp.where(rows[:, j : j + 1] >= j, work[:, j : j + 1] * scale, 0.0)
+        row = jnp.where(cols[j : j + 1, :] >= j, work[j : j + 1, :] * scale, 0.0)
         lower = jnp.where(cols == j, column, lower)
         upper = jnp.where(rows == j, row, upper)
         work = work - column * row
     pending = jnp.where(rows == cols, 1.0, 0.0).astype(jnp.float32)
     inverse = jnp.zeros((size, size), jnp.float32)
     for k in range(size):
-        solved = pending[k : k + 1, :] / lower[k : k + 1, k : k + 1]
+        solved = pending[k : k + 1, :] * (1.0 / lower[k : k + 1, k : k + 1])
         inverse = jnp.where(rows == k, solved, inverse)
         below = jnp.where(rows[:, k : k + 1] > k, lower[:, k : k + 1], 0.0)
         pending = pending - below * solved

time: 166 us -> 166 us (level)
  no operation moved by 1% of the time
where the time goes in v7:
time: 166 us
  waiting for transfers between devices  68.4 us (41%)
  Pallas kernels  41 us (25%)
  matrix products  35.5 us (21%)
  local copies, waits for them, and re-layouts  9.47 us (6%)
  starting transfers between devices  9.01 us (5%)
    ppermute x14, waiting for transfers between devices, tree_sum(): lax.ppermute(value, axis, fold_pairs(count, stride, span, fold))  53.9 us
    pallas_call x1, Pallas kernels, krylov_powers(): pl.pallas_call(powers_kernel, grid=(rhs,), in_specs=[pl.BlockSpec((1, dep...  26.4 us
    dot_general x1, matrix products, body(): jnp.dot(krylov, krylov.T, precision=lax.Precision.HIGHEST, preferred_elem...  11.8 us
    dot_general x1, matrix products, body(): jnp.dot(inverse_first, krylov, precision=lax.Precision.HIGHEST, preferred...  11.6 us
    pallas_call x2, Pallas kernels, cholesky_factors(): return pl.pallas_call(factor_kernel, out_shape=[square, square])(symmetric)  10.5 us
    unnamed x15, local copies, waits for them, and re-layouts  7.31 us
    dot_general x1, matrix products, body(): jnp.dot(inverse_second, first_q, precision=lax.Precision.HIGH, preferred_...  7.14 us
    ppermute x1, waiting for transfers between devices, halo_strips(): x_prev = lax.ppermute(last, 'gx', x_next_pairs)  5.63 us
  transfers between devices with their start and end apart: 18, of which 18 were waited for; matrix products, arithmetic and copies ran while one was open for 0% of the time, Pallas kernels for 0%

profile of v7, /device:TPU:0, one launch (start us, length us, event | category | flops | bytes accessed | tf_op | source)
XLA Modules:
  0.0 165.5 jit_solution(12239962886035468671)
XLA Ops:
  0.6 1.1 fusion.5
  1.7 0.9 fusion.6
  2.6 5.4 %collective-permute-start = (f32[80,4,128]{2,1,0:T(4,128)S(1)}, f32[80,4,128]{2,1,0:T(4,128)S(1)}, u32[]{:S(2)}, u32[]{:S(2)}) collective-permute-start(f32[80,4,128]{2,1,0:T(4,128)S(1)} %pad_maximum_fusion), channel_id=1, source_target_pairs={{8,0},{16,8},{24,16},{32,24},{40,32},{48,40},{56,48},{64,56},{72,6... | collective-permute-start | bytes 491528 | tf_op jit(solution)/shard_map/ppermute | solution.py:91
  8.1 3.3 %collective-permute-done.xn_ref.refs_3_.refs_5_.refs_7_ = f32[80,4,128]{2,1,0:T(4,128)S(1)} collective-permute-done((f32[80,4,128]{2,1,0:T(4,128)S(1)}, f32[80,4,128]{2,1,0:T(4,128)S(1)}, u32[]{:S(2)}, u32[]{:S(2)}) %collective-permute-start) | collective-permute-done | bytes 163872 | tf_op jit(solution)/shard_map/ppermute | solution.py:91
  11.4 5.6 %collective-permute-done.1.xp_ref.refs_4_.refs_6_.refs_8_ = f32[80,4,128]{2,1,0:T(4,128)S(1)} collective-permute-done((f32[80,4,128]{2,1,0:T(4,128)S(1)}, f32[80,4,128]{2,1,0:T(4,128)S(1)}, u32[]{:S(2)}, u32[]{:S(2)}) %collective-permute-start.1) | collective-permute-done | bytes 163872 | tf_op jit(solution)/shard_map/ppermute | solution.py:92
  17.7 4.0 %shard_map.58 = (f32[3,72,128]{2,1,0:T(8,128)}, f32[3,72,128]{2,1,0:T(8,128)}) custom-call(f32[8,8,64,128]{3,2,1,0:T(8,128)} %refs_0_.1, f32[8,64,128]{2,1,0:T(8,128)} %refs_1_.1, f32[8,64,128]{2,1,0:T(8,128)} %refs_2_.1, f32[80,4,128]{2,1,0:T(4,128)} %copy-done.1, f32[80,4,128]{2,1,0:T(4,128)} %copy-done.2), custom_call_target="tpu_custom_call" | custom-call | tf_op jit(solution)/shard_map/pallas_call | solution.py:72
  21.8 2.3 %collective-permute-start.2 = (f32[3,72,128]{2,1,0:T(8,128)}, f32[3,72,128]{2,1,0:T(8,128)S(1)}, u32[]{:S(2)}, u32[]{:S(2)}) collective-permute-start(f32[3,72,128]{2,1,0:T(8,128)} %get-tuple-element.9), channel_id=1, source_target_pairs={{1,0},{2,1},{3,2},{4,3},{5,4},{6,5},{7,6},{0,7},{9,8},{10,9},{11,1... | collective-permute-start | bytes 331784 | tf_op jit(solution)/shard_map/ppermute | solution.py:95
  24.1 2.6 %collective-permute-done.2.refs_9_ = f32[3,72,128]{2,1,0:T(8,128)S(1)} collective-permute-done((f32[3,72,128]{2,1,0:T(8,128)}, f32[3,72,128]{2,1,0:T(8,128)S(1)}, u32[]{:S(2)}, u32[]{:S(2)}) %collective-permute-start.2) | collective-permute-done | bytes 110624 | tf_op jit(solution)/shard_map/ppermute | solution.py:95
  26.7 2.9 %collective-permute-done.3.refs_10_ = f32[3,72,128]{2,1,0:T(8,128)S(1)} collective-permute-done((f32[3,72,128]{2,1,0:T(8,128)}, f32[3,72,128]{2,1,0:T(8,128)S(1)}, u32[]{:S(2)}, u32[]{:S(2)}) %collective-permute-start.3) | collective-permute-done | bytes 110624 | tf_op jit(solution)/shard_map/ppermute | solution.py:96
  30.3 26.4 %shard_map.59 = f32[5,4096,128]{2,1,0:T(8,128)} custom-call(f32[8,8,64,128]{3,2,1,0:T(8,128)} %refs_0_.1, f32[8,64,128]{2,1,0:T(8,128)} %refs_1_.1, f32[8,64,128]{2,1,0:T(8,128)} %refs_2_.1, f32[80,4,128]{2,1,0:T(4,128)} %copy-done.1, f32[80,4,128]{2,1,0:T(4,128)} %copy-done.2, f32[80,4,128]{2,1,0:T(4,128)} %copy-done.1, f32[80,4,128]{2,1,0:T(4,128)} %copy-done.2, ...), custom_call_target="tpu_custom_call" | custom-call | tf_op jit(solution)/shard_map/pallas_call | solution.py:216
  56.7 11.8 %fusion.2 = f32[40,40]{0,1:T(8,128)S(1)} fusion(f32[5,4096,128]{2,1,0:T(8,128)} %shard_map.59), kind=kOutput, calls=%fused_computation.2 | convolution fusion | flops 1258291200 | bytes 10492160 | tf_op jit(solution)/shard_map/dot_general | solution.py:285
  68.6 3.8 %collective-permute-done.4 = f32[40,40]{0,1:T(8,128)S(1)} collective-permute-done((f32[40,40]{0,1:T(8,128)S(1)}, f32[40,40]{0,1:T(8,128)S(1)}, u32[]{:S(2)}, u32[]{:S(2)}) %collective-permute-start.4) | collective-permute-done | bytes 6432 | tf_op jit(solution)/shard_map/ppermute | solution.py:134
  72.4 5.0 %collective-permute-done.5 = f32[40,40]{0,1:T(8,128)S(1)} collective-permute-done((f32[40,40]{0,1:T(8,128)S(1)}, f32[40,40]{0,1:T(8,128)S(1)}, u32[]{:S(2)}, u32[]{:S(2)}) %collective-permute-start.5) | collective-permute-done | bytes 6432 | tf_op jit(solution)/shard_map/ppermute | solution.py:134
  77.4 3.8 %collective-permute-done.6 = f32[40,40]{0,1:T(8,128)S(1)} collective-permute-done((f32[40,40]{0,1:T(8,128)S(1)}, f32[40,40]{0,1:T(8,128)S(1)}, u32[]{:S(2)}, u32[]{:S(2)}) %collective-permute-start.6) | collective-permute-done | bytes 6432 | tf_op jit(solution)/shard_map/ppermute | solution.py:134
  81.2 5.0 %collective-permute-done.7 = f32[40,40]{0,1:T(8,128)S(1)} collective-permute-done((f32[40,40]{0,1:T(8,128)S(1)}, f32[40,40]{0,1:T(8,128)S(1)}, u32[]{:S(2)}, u32[]{:S(2)}) %collective-permute-start.7) | collective-permute-done | bytes 6432 | tf_op jit(solution)/shard_map/ppermute | solution.py:134
  86.2 1.2 collective-permute-done.8
  87.4 3.8 %collective-permute-done.9 = f32[40,40]{0,1:T(8,128)S(1)} collective-permute-done((f32[40,40]{0,1:T(8,128)S(1)}, f32[40,40]{0,1:T(8,128)S(1)}, u32[]{:S(2)}, u32[]{:S(2)}) %collective-permute-start.9) | collective-permute-done | bytes 6432 | tf_op jit(solution)/shard_map/ppermute | solution.py:134
  91.7 4.4 %collective-permute-done.10 = f32[40,40]{0,1:T(8,128)S(1)} collective-permute-done((f32[40,40]{0,1:T(8,128)S(1)}, f32[40,40]{0,1:T(8,128)S(1)}, u32[]{:S(2)}, u32[]{:S(2)}) %collective-permute-start.10) | collective-permute-done | bytes 6432 | tf_op jit(solution)/shard_map/ppermute | solution.py:134
  96.9 5.3 %shard_map.60 = (f32[40,40]{1,0:T(8,128)}, f32[40,40]{1,0:T(8,128)}) custom-call(f32[40,40]{1,0:T(8,128)} %fusion.4.gram_ref), custom_call_target="tpu_custom_call" | custom-call | tf_op jit(solution)/shard_map/pallas_call | solution.py:268
  102.1 11.6 %fusion = f32[40,65536]{1,0:T(8,128)S(1)} fusion(f32[40,40]{1,0:T(8,128)} %get-tuple-element.11, f32[5,4096,128]{2,1,0:T(8,128)} %shard_map.59), kind=kOutput, calls=%fused_computation | convolution fusion | flops 1258291200 | bytes 20977920 | tf_op jit(solution)/shard_map/dot_general | solution.py:289
  113.7 4.2 %fusion.8 = f32[40,40]{0,1:T(8,128)S(1)} fusion(f32[40,65536]{1,0:T(8,128)S(1)} %fusion), kind=kOutput, calls=%fused_computation.16 | convolution fusion | flops 629145600 | bytes 10492160 | tf_op jit(solution)/shard_map/dot_general | solution.py:292
  118.0 3.8 %collective-permute-done.11 = f32[40,40]{0,1:T(8,128)S(1)} collective-permute-done((f32[40,40]{0,1:T(8,128)S(1)}, f32[40,40]{0,1:T(8,128)S(1)}, u32[]{:S(2)}, u32[]{:S(2)}) %collective-permute-start.11) | collective-permute-done | bytes 6432 | tf_op jit(solution)/shard_map/ppermute | solution.py:134
  121.8 5.0 %collective-permute-done.12 = f32[40,40]{0,1:T(8,128)S(1)} collective-permute-done((f32[40,40]{0,1:T(8,128)S(1)}, f32[40,40]{0,1:T(8,128)S(1)}, u32[]{:S(2)}, u32[]{:S(2)}) %collective-permute-start.12) | collective-permute-done | bytes 6432 | tf_op jit(solution)/shard_map/ppermute | solution.py:134
  126.8 3.8 %collective-permute-done.13 = f32[40,40]{0,1:T(8,128)S(1)} collective-permute-done((f32[40,40]{0,1:T(8,128)S(1)}, f32[40,40]{0,1:T(8,128)S(1)}, u32[]{:S(2)}, u32[]{:S(2)}) %collective-permute-start.13) | collective-permute-done | bytes 6432 | tf_op jit(solution)/shard_map/ppermute | solution.py:134
  130.6 5.0 %collective-permute-done.14 = f32[40,40]{0,1:T(8,128)S(1)} collective-permute-done((f32[40,40]{0,1:T(8,128)S(1)}, f32[40,40]{0,1:T(8,128)S(1)}, u32[]{:S(2)}, u32[]{:S(2)}) %collective-permute-start.14) | collective-permute-done | bytes 6432 | tf_op jit(solution)/shard_map/ppermute | solution.py:134
  135.6 1.2 collective-permute-done.15
  136.8 3.8 %collective-permute-done.16 = f32[40,40]{0,1:T(8,128)S(1)} collective-permute-done((f32[40,40]{0,1:T(8,128)S(1)}, f32[40,40]{0,1:T(8,128)S(1)}, u32[]{:S(2)}, u32[]{:S(2)}) %collective-permute-start.16) | collective-permute-done | bytes 6432 | tf_op jit(solution)/shard_map/ppermute | solution.py:134
  141.1 4.5 %collective-permute-done.17 = f32[40,40]{0,1:T(8,128)S(1)} collective-permute-done((f32[40,40]{0,1:T(8,128)S(1)}, f32[40,40]{0,1:T(8,128)S(1)}, u32[]{:S(2)}, u32[]{:S(2)}) %collective-permute-start.17) | collective-permute-done | bytes 6432 | tf_op jit(solution)/shard_map/ppermute | solution.py:134
  146.3 5.3 %shard_map.61 = (f32[40,40]{1,0:T(8,128)}, f32[40,40]{1,0:T(8,128)}) custom-call(f32[40,40]{1,0:T(8,128)} %broadcast_multiply_fusion.gram_ref), custom_call_target="tpu_custom_call" | custom-call | tf_op jit(solution)/shard_map/pallas_call | solution.py:268
  151.6 7.1 %convolution_bitcast_fusion = f32[5,8,512,128]{3,1,2,0:T(8,128)S(1)} fusion(f32[40,40]{1,0:T(8,128)} %get-tuple-element.12, f32[40,65536]{1,0:T(8,128)} %copy-done), kind=kOutput, calls=%fused_computation.4 | convolution fusion | flops 629145600 | bytes 20977920 | tf_op jit(solution)/shard_map/dot_general | solution.py:296
  158.8 6.0 %copy.15 = f32[5,8,512,128]{3,2,1,0:T(8,128)} copy(f32[5,8,512,128]{3,1,2,0:T(8,128)S(1)} %convolution_bitcast_fusion) | data formatting | bytes 20971520
  164.8 0.8 fusion.9
  (52 shorter events, 4.3 us)
Async XLA Ops:
  2.6 8.8 %collective-permute-start = (f32[80,4,128]{2,1,0:T(4,128)S(1)}, f32[80,4,128]{2,1,0:T(4,128)S(1)}, u32[]{:S(2)}, u32[]{:S(2)}) collective-permute-start(f32[80,4,128]{2,1,0:T(4,128)S(1)} %pad_maximum_fusion), channel_id=1, source_target_pairs={{8,0},{16,8},{24,16},{32,24},{40,32},{48,40},{56,48},{64,56},{72,6... | collective-permute-start | bytes 491528 | tf_op jit(solution)/shard_map/ppermute | solution.py:91
  8.0 9.0 %collective-permute-start.1 = (f32[80,4,128]{2,1,0:T(4,128)S(1)}, f32[80,4,128]{2,1,0:T(4,128)S(1)}, u32[]{:S(2)}, u32[]{:S(2)}) collective-permute-start(f32[80,4,128]{2,1,0:T(4,128)S(1)} %pad_maximum_fusion.1), channel_id=1, source_target_pairs={{0,8},{8,16},{16,24},{24,32},{32,40},{40,48},{48,56},{56,64},{64,7... | collective-permute-start | bytes 491528 | tf_op jit(solution)/shard_map/ppermute | solution.py:92
  11.4 5.6 %copy-start.1 = (f32[80,4,128]{2,1,0:T(4,128)}, f32[80,4,128]{2,1,0:T(4,128)S(1)}, u32[]{:S(2)}) copy-start(f32[80,4,128]{2,1,0:T(4,128)S(1)} %collective-permute-done.xn_ref.refs_3_.refs_5_.refs_7_) | copy-start | bytes 491524
  17.1 0.7 copy-start.2
  21.8 4.9 %collective-permute-start.2 = (f32[3,72,128]{2,1,0:T(8,128)}, f32[3,72,128]{2,1,0:T(8,128)S(1)}, u32[]{:S(2)}, u32[]{:S(2)}) collective-permute-start(f32[3,72,128]{2,1,0:T(8,128)} %get-tuple-element.9), channel_id=1, source_target_pairs={{1,0},{2,1},{3,2},{4,3},{5,4},{6,5},{7,6},{0,7},{9,8},{10,9},{11,1... | collective-permute-start | bytes 331784 | tf_op jit(solution)/shard_map/ppermute | solution.py:95
  24.1 5.6 %collective-permute-start.3 = (f32[3,72,128]{2,1,0:T(8,128)}, f32[3,72,128]{2,1,0:T(8,128)S(1)}, u32[]{:S(2)}, u32[]{:S(2)}) collective-permute-start(f32[3,72,128]{2,1,0:T(8,128)} %get-tuple-element.10), channel_id=1, source_target_pairs={{0,1},{1,2},{2,3},{3,4},{4,5},{5,6},{6,7},{7,0},{8,9},{9,10},{10,1... | collective-permute-start | bytes 331784 | tf_op jit(solution)/shard_map/ppermute | solution.py:96
  26.7 3.0 %copy-start.3 = (f32[3,72,128]{2,1,0:T(8,128)}, f32[3,72,128]{2,1,0:T(8,128)S(1)}, u32[]{:S(2)}) copy-start(f32[3,72,128]{2,1,0:T(8,128)S(1)} %collective-permute-done.2.refs_9_) | copy-start | bytes 331780
  29.7 0.7 copy-start.4
  68.5 3.9 %collective-permute-start.4 = (f32[40,40]{0,1:T(8,128)S(1)}, f32[40,40]{0,1:T(8,128)S(1)}, u32[]{:S(2)}, u32[]{:S(2)}) collective-permute-start(f32[40,40]{0,1:T(8,128)S(1)} %fusion.2), channel_id=1, source_target_pairs={{0,32},{8,40},{16,48},{24,56},{32,0},{40,8},{48,16},{56,24},{64,96... | collective-permute-start | bytes 19208 | tf_op jit(solution)/shard_map/ppermute | solution.py:134
  72.4 5.0 %collective-permute-start.5 = (f32[40,40]{0,1:T(8,128)S(1)}, f32[40,40]{0,1:T(8,128)S(1)}, u32[]{:S(2)}, u32[]{:S(2)}) collective-permute-start(f32[40,40]{0,1:T(8,128)S(1)} %add.48), channel_id=1, source_target_pairs={{0,96},{8,104},{16,112},{24,120},{32,64},{40,72},{48,80},{56,88},{... | collective-permute-start | bytes 19208 | tf_op jit(solution)/shard_map/ppermute | solution.py:134
  77.4 3.8 %collective-permute-start.6 = (f32[40,40]{0,1:T(8,128)S(1)}, f32[40,40]{0,1:T(8,128)S(1)}, u32[]{:S(2)}, u32[]{:S(2)}) collective-permute-start(f32[40,40]{0,1:T(8,128)S(1)} %add.49), channel_id=1, source_target_pairs={{0,8},{8,0},{16,24},{24,16},{32,40},{40,32},{48,56},{56,48},{64,72... | collective-permute-start | bytes 19208 | tf_op jit(solution)/shard_map/ppermute | solution.py:134
  81.2 5.0 %collective-permute-start.7 = (f32[40,40]{0,1:T(8,128)S(1)}, f32[40,40]{0,1:T(8,128)S(1)}, u32[]{:S(2)}, u32[]{:S(2)}) collective-permute-start(f32[40,40]{0,1:T(8,128)S(1)} %add.50), channel_id=1, source_target_pairs={{0,24},{8,16},{16,8},{24,0},{32,56},{40,48},{48,40},{56,32},{64,88... | collective-permute-start | bytes 19208 | tf_op jit(solution)/shard_map/ppermute | solution.py:134
  86.2 1.2 collective-permute-start.8
  87.4 3.8 %collective-permute-start.9 = (f32[40,40]{0,1:T(8,128)S(1)}, f32[40,40]{0,1:T(8,128)S(1)}, u32[]{:S(2)}, u32[]{:S(2)}) collective-permute-start(f32[40,40]{0,1:T(8,128)S(1)} %add.52), channel_id=1, source_target_pairs={{0,2},{1,3},{2,0},{3,1},{4,6},{5,7},{6,4},{7,5},{8,10},{9,11},{10,... | collective-permute-start | bytes 19208 | tf_op jit(solution)/shard_map/ppermute | solution.py:134
  91.2 5.0 %collective-permute-start.10 = (f32[40,40]{0,1:T(8,128)S(1)}, f32[40,40]{0,1:T(8,128)S(1)}, u32[]{:S(2)}, u32[]{:S(2)}) collective-permute-start(f32[40,40]{0,1:T(8,128)S(1)} %add.53), channel_id=1, source_target_pairs={{0,6},{1,7},{2,4},{3,5},{4,2},{5,3},{6,0},{7,1},{8,14},{9,15},{10,... | collective-permute-start | bytes 19208 | tf_op jit(solution)/shard_map/ppermute | solution.py:134
  113.7 4.2 %copy-start = (f32[40,65536]{1,0:T(8,128)}, f32[40,65536]{1,0:T(8,128)S(1)}, u32[]{:S(2)}) copy-start(f32[40,65536]{1,0:T(8,128)S(1)} %fusion) | copy-start | bytes 31457284
  117.9 3.9 %collective-permute-start.11 = (f32[40,40]{0,1:T(8,128)S(1)}, f32[40,40]{0,1:T(8,128)S(1)}, u32[]{:S(2)}, u32[]{:S(2)}) collective-permute-start(f32[40,40]{0,1:T(8,128)S(1)} %fusion.8), channel_id=1, source_target_pairs={{0,32},{8,40},{16,48},{24,56},{32,0},{40,8},{48,16},{56,24},{64,96... | collective-permute-start | bytes 19208 | tf_op jit(solution)/shard_map/ppermute | solution.py:134
  121.8 5.0 %collective-permute-start.12 = (f32[40,40]{0,1:T(8,128)S(1)}, f32[40,40]{0,1:T(8,128)S(1)}, u32[]{:S(2)}, u32[]{:S(2)}) collective-permute-start(f32[40,40]{0,1:T(8,128)S(1)} %add.56), channel_id=1, source_target_pairs={{0,96},{8,104},{16,112},{24,120},{32,64},{40,72},{48,80},{56,88},{... | collective-permute-start | bytes 19208 | tf_op jit(solution)/shard_map/ppermute | solution.py:134
  126.8 3.8 %collective-permute-start.13 = (f32[40,40]{0,1:T(8,128)S(1)}, f32[40,40]{0,1:T(8,128)S(1)}, u32[]{:S(2)}, u32[]{:S(2)}) collective-permute-start(f32[40,40]{0,1:T(8,128)S(1)} %add.57), channel_id=1, source_target_pairs={{0,8},{8,0},{16,24},{24,16},{32,40},{40,32},{48,56},{56,48},{64,72... | collective-permute-start | bytes 19208 | tf_op jit(solution)/shard_map/ppermute | solution.py:134
  130.6 5.0 %collective-permute-start.14 = (f32[40,40]{0,1:T(8,128)S(1)}, f32[40,40]{0,1:T(8,128)S(1)}, u32[]{:S(2)}, u32[]{:S(2)}) collective-permute-start(f32[40,40]{0,1:T(8,128)S(1)} %add.58), channel_id=1, source_target_pairs={{0,24},{8,16},{16,8},{24,0},{32,56},{40,48},{48,40},{56,32},{64,88... | collective-permute-start | bytes 19208 | tf_op jit(solution)/shard_map/ppermute | solution.py:134
  135.6 1.2 collective-permute-start.15
  136.8 3.8 %collective-permute-start.16 = (f32[40,40]{0,1:T(8,128)S(1)}, f32[40,40]{0,1:T(8,128)S(1)}, u32[]{:S(2)}, u32[]{:S(2)}) collective-permute-start(f32[40,40]{0,1:T(8,128)S(1)} %add.60), channel_id=1, source_target_pairs={{0,2},{1,3},{2,0},{3,1},{4,6},{5,7},{6,4},{7,5},{8,10},{9,11},{10,... | collective-permute-start | bytes 19208 | tf_op jit(solution)/shard_map/ppermute | solution.py:134
  140.6 5.0 %collective-permute-start.17 = (f32[40,40]{0,1:T(8,128)S(1)}, f32[40,40]{0,1:T(8,128)S(1)}, u32[]{:S(2)}, u32[]{:S(2)}) collective-permute-start(f32[40,40]{0,1:T(8,128)S(1)} %add.61), channel_id=1, source_target_pairs={{0,6},{1,7},{2,4},{3,5},{4,2},{5,3},{6,0},{7,1},{8,14},{9,15},{10,... | collective-permute-start | bytes 19208 | tf_op jit(solution)/shard_map/ppermute | solution.py:134
  158.8 6.0 %copy-start.5 = (f32[40,40]{1,0:T(8,128)S(1)}, f32[40,40]{1,0:T(8,128)}, u32[]{:S(2)}) copy-start(f32[40,40]{1,0:T(8,128)} %get-tuple-element.8) | copy-start | bytes 19204
  158.8 6.0 %copy-start.6 = (f32[40,40]{1,0:T(8,128)S(1)}, f32[40,40]{1,0:T(8,128)}, u32[]{:S(2)}) copy-start(f32[40,40]{1,0:T(8,128)} %get-tuple-element.13) | copy-start | bytes 19204

commit v8 on v7

--- a/solution.py
+++ b/solution.py
@@ -36,10 +36,12 @@
 
 
 def tall_plane(core, from_next, from_prev):
-    return jnp.concatenate([core, from_next, from_prev], axis=0)
+    spare = jnp.zeros_like(from_next)
+    return jnp.concatenate([spare, from_prev, core, from_next, spare], axis=0)
 
 
 PACK = 32
+SKIRT = 8
 
 
 def columns_kernel(block_ref, coef_ref, react_ref, xn_ref, xp_ref, first_ref, last_ref):
@@ -66,7 +68,7 @@
 
 def edge_columns(start_block, conductivity, reaction, x_next, x_prev):
     planes, width, cols = x_next.shape
-    rows = start_block.shape[2] + 2 * width
+    rows = start_block.shape[2] + 4 * width
     whole = lambda shape: pl.BlockSpec(shape, lambda: (0,) * len(shape))
     strip = jax.ShapeDtypeStruct((-(-planes // PACK), rows, cols), jnp.float32)
     return pl.pallas_call(
@@ -161,6 +163,8 @@
     buffers = refs[14:]
     depth, rows, cols = block_ref.shape[1:]
     r = pl.program_id(0)
+    tall = weight_ref.shape[2]
+    lead = (tall - rows) // 2
 
     def planes(core_of, group, first_plane):
         xn, xp = (x_strips[2 * group], x_strips[2 * group + 1])
@@ -181,27 +185,40 @@
         for d, direction in enumerate(DIRECTIONS):
             weight_ref[d] = 0.5 * (coef + neighbour(coef, direction))
         react_pad_ref[...] = planes(lambda z: react_ref[z], 2, rhs * depth + depth)
+        for buffer in buffers:
+            buffer[:, :SKIRT] = jnp.zeros((depth, SKIRT, LANES), jnp.float32)
+            buffer[:, SKIRT + tall :] = jnp.zeros((depth, SKIRT, LANES), jnp.float32)
 
     for z in range(depth):
         store_plane(out_ref, 0, r, z, block_ref[0, z])
-    buffers[0][...] = planes(lambda z: block_ref[0, z], 0, r * depth)
+    buffers[0][:, SKIRT : SKIRT + tall] = planes(lambda z: block_ref[0, z], 0, r * depth)
     for power in range(1, STEPS + 1):
         source, target = (buffers[(power - 1) % 2], buffers[power % 2])
-        keep = (slice(None), slice(None)) if power < STEPS else (slice(0, rows), slice(0, cols))
+        first, count = (0, tall) if power < STEPS else (lead, rows)
+        top = SKIRT + first
         for z in range(depth):
-            whole = source[z]
-            current = whole[keep]
+            current = source[z, top : top + count]
+            sides = {
+                (1, 1): source[z, top + 1 : top + 1 + count],
+                (1, -1): source[z, top - 1 : top - 1 + count],
+                (0, 1): source[(z + 1) % depth, top : top + count],
+                (0, -1): source[(z - 1) % depth, top : top + count],
+            }
             running = jnp.zeros_like(current)
             for d, (axis, offset) in enumerate(DIRECTIONS):
-                if axis == 0:
-                    beside = source[(z + offset) % depth][keep]
+                if axis == 2:
+                    beside = pltpu.roll(current, (-offset) % LANES, 1)
                 else:
-                    beside = pltpu.roll(whole, (-offset) % whole.shape[axis - 1], axis - 1)[keep]
-                running = running + weight_ref[d, z][keep] * (current - beside)
-            current = (react_pad_ref[z][keep] * current + running - center_shift * current) * step_scale
+                    beside = sides[(axis, offset)]
+                running = running + weight_ref[d, z, first : first + count] * (current - beside)
+            current = (
+                react_pad_ref[z, first : first + count] * current + running - center_shift * current
+            ) * step_scale
             if power < STEPS:
-                target[z] = current
-            store_plane(out_ref, power, r, z, current[:rows, :cols])
+                target[z, SKIRT : SKIRT + tall] = current
+                store_plane(out_ref, power, r, z, current[lead : lead + rows, :cols])
+            else:
+                store_plane(out_ref, power, r, z, current[:, :cols])
 
 
 def krylov_powers(start_block, conductivity, reaction, strips):
@@ -226,10 +243,10 @@
         out_specs=pl.BlockSpec((STEPS + 1, depth * rows * rhs, cols), lambda r: (0, 0, 0)),
         out_shape=jax.ShapeDtypeStruct((STEPS + 1, depth * rows * rhs, cols), jnp.float32),
         scratch_shapes=[
-            pltpu.VMEM((len(DIRECTIONS), depth, rows + 2 * width, LANES), jnp.float32),
-            pltpu.VMEM((depth, rows + 2 * width, LANES), jnp.float32),
-            pltpu.VMEM((depth, rows + 2 * width, LANES), jnp.float32),
-            pltpu.VMEM((depth, rows + 2 * width, LANES), jnp.float32),
+            pltpu.VMEM((len(DIRECTIONS), depth, rows + 4 * width, LANES), jnp.float32),
+            pltpu.VMEM((depth, rows + 4 * width, LANES), jnp.float32),
+            pltpu.VMEM((depth, rows + 4 * width + 2 * SKIRT, LANES), jnp.float32),
+            pltpu.VMEM((depth, rows + 4 * width + 2 * SKIRT, LANES), jnp.float32),
         ],
         compiler_params=pltpu.CompilerParams(dimension_semantics=("arbitrary",)),
     )(start_block, conductivity, reaction, *([x_next, x_prev] * 3), y_next, y_prev)

time: 166 us -> 166 us (level)
  no operation moved by 1% of the time
where the time goes in v8:
time: 166 us
  waiting for transfers between devices  68.5 us (41%)
  Pallas kernels  41.1 us (25%)
  matrix products  35.5 us (21%)
  local copies, waits for them, and re-layouts  9.46 us (6%)
  starting transfers between devices  9.01 us (5%)
    ppermute x14, waiting for transfers between devices, tree_sum(): lax.ppermute(value, axis, fold_pairs(count, stride, span, fold))  53.9 us
    pallas_call x1, Pallas kernels, krylov_powers(): pl.pallas_call(powers_kernel, grid=(rhs,), in_specs=[pl.BlockSpec((1, dep...  26.4 us
    dot_general x1, matrix products, body(): jnp.dot(krylov, krylov.T, precision=lax.Precision.HIGHEST, preferred_elem...  11.8 us
    dot_general x1, matrix products, body(): jnp.dot(inverse_first, krylov, precision=lax.Precision.HIGHEST, preferred...  11.6 us
    pallas_call x2, Pallas kernels, cholesky_factors(): return pl.pallas_call(factor_kernel, out_shape=[square, square])(symmetric)  10.5 us
    unnamed x15, local copies, waits for them, and re-layouts  7.31 us
    dot_general x1, matrix products, body(): jnp.dot(inverse_second, first_q, precision=lax.Precision.HIGH, preferred_...  7.14 us
    ppermute x1, waiting for transfers between devices, halo_strips(): x_prev = lax.ppermute(last, 'gx', x_next_pairs)  5.63 us
  transfers between devices with their start and end apart: 18, of which 18 were waited for; matrix products, arithmetic and copies ran while one was open for 0% of the time, Pallas kernels for 0%

profile of v8, /device:TPU:0, one launch (start us, length us, event | category | flops | bytes accessed | tf_op | source)
XLA Modules:
  0.0 165.8 jit_solution(8359647964648535824)
XLA Ops:
  0.6 1.1 fusion.5
  1.7 0.9 fusion.6
  2.6 5.4 %collective-permute-start = (f32[80,4,128]{2,1,0:T(4,128)S(1)}, f32[80,4,128]{2,1,0:T(4,128)S(1)}, u32[]{:S(2)}, u32[]{:S(2)}) collective-permute-start(f32[80,4,128]{2,1,0:T(4,128)S(1)} %pad_maximum_fusion), channel_id=1, source_target_pairs={{8,0},{16,8},{24,16},{32,24},{40,32},{48,40},{56,48},{64,56},{72,6... | collective-permute-start | bytes 491528 | tf_op jit(solution)/shard_map/ppermute | solution.py:93
  8.1 3.3 %collective-permute-done.xn_ref.refs_3_.refs_5_.refs_7_ = f32[80,4,128]{2,1,0:T(4,128)S(1)} collective-permute-done((f32[80,4,128]{2,1,0:T(4,128)S(1)}, f32[80,4,128]{2,1,0:T(4,128)S(1)}, u32[]{:S(2)}, u32[]{:S(2)}) %collective-permute-start) | collective-permute-done | bytes 163872 | tf_op jit(solution)/shard_map/ppermute | solution.py:93
  11.4 5.6 %collective-permute-done.1.xp_ref.refs_4_.refs_6_.refs_8_ = f32[80,4,128]{2,1,0:T(4,128)S(1)} collective-permute-done((f32[80,4,128]{2,1,0:T(4,128)S(1)}, f32[80,4,128]{2,1,0:T(4,128)S(1)}, u32[]{:S(2)}, u32[]{:S(2)}) %collective-permute-start.1) | collective-permute-done | bytes 163872 | tf_op jit(solution)/shard_map/ppermute | solution.py:94
  17.7 4.2 %shard_map.58 = (f32[3,80,128]{2,1,0:T(8,128)}, f32[3,80,128]{2,1,0:T(8,128)}) custom-call(f32[8,8,64,128]{3,2,1,0:T(8,128)} %refs_0_.1, f32[8,64,128]{2,1,0:T(8,128)} %refs_1_.1, f32[8,64,128]{2,1,0:T(8,128)} %refs_2_.1, f32[80,4,128]{2,1,0:T(4,128)} %copy-done.1, f32[80,4,128]{2,1,0:T(4,128)} %copy-done.2), custom_call_target="tpu_custom_call" | custom-call | tf_op jit(solution)/shard_map/pallas_call | solution.py:74
  21.9 2.3 %collective-permute-start.2 = (f32[3,80,128]{2,1,0:T(8,128)}, f32[3,80,128]{2,1,0:T(8,128)S(1)}, u32[]{:S(2)}, u32[]{:S(2)}) collective-permute-start(f32[3,80,128]{2,1,0:T(8,128)} %get-tuple-element.9), channel_id=1, source_target_pairs={{1,0},{2,1},{3,2},{4,3},{5,4},{6,5},{7,6},{0,7},{9,8},{10,9},{11,1... | collective-permute-start | bytes 368648 | tf_op jit(solution)/shard_map/ppermute | solution.py:97
  24.2 2.8 %collective-permute-done.2.refs_9_ = f32[3,80,128]{2,1,0:T(8,128)S(1)} collective-permute-done((f32[3,80,128]{2,1,0:T(8,128)}, f32[3,80,128]{2,1,0:T(8,128)S(1)}, u32[]{:S(2)}, u32[]{:S(2)}) %collective-permute-start.2) | collective-permute-done | bytes 122912 | tf_op jit(solution)/shard_map/ppermute | solution.py:97
  27.0 3.0 %collective-permute-done.3.refs_10_ = f32[3,80,128]{2,1,0:T(8,128)S(1)} collective-permute-done((f32[3,80,128]{2,1,0:T(8,128)}, f32[3,80,128]{2,1,0:T(8,128)S(1)}, u32[]{:S(2)}, u32[]{:S(2)}) %collective-permute-start.3) | collective-permute-done | bytes 122912 | tf_op jit(solution)/shard_map/ppermute | solution.py:98
  30.6 26.4 %shard_map.59 = f32[5,4096,128]{2,1,0:T(8,128)} custom-call(f32[8,8,64,128]{3,2,1,0:T(8,128)} %refs_0_.1, f32[8,64,128]{2,1,0:T(8,128)} %refs_1_.1, f32[8,64,128]{2,1,0:T(8,128)} %refs_2_.1, f32[80,4,128]{2,1,0:T(4,128)} %copy-done.1, f32[80,4,128]{2,1,0:T(4,128)} %copy-done.2, f32[80,4,128]{2,1,0:T(4,128)} %copy-done.1, f32[80,4,128]{2,1,0:T(4,128)} %copy-done.2, ...), custom_call_target="tpu_custom_call" | custom-call | tf_op jit(solution)/shard_map/pallas_call | solution.py:233
  57.0 11.8 %fusion.2 = f32[40,40]{0,1:T(8,128)S(1)} fusion(f32[5,4096,128]{2,1,0:T(8,128)} %shard_map.59), kind=kOutput, calls=%fused_computation.2 | convolution fusion | flops 1258291200 | bytes 10492160 | tf_op jit(solution)/shard_map/dot_general | solution.py:302
  68.9 3.8 %collective-permute-done.4 = f32[40,40]{0,1:T(8,128)S(1)} collective-permute-done((f32[40,40]{0,1:T(8,128)S(1)}, f32[40,40]{0,1:T(8,128)S(1)}, u32[]{:S(2)}, u32[]{:S(2)}) %collective-permute-start.4) | collective-permute-done | bytes 6432 | tf_op jit(solution)/shard_map/ppermute | solution.py:136
  72.7 5.0 %collective-permute-done.5 = f32[40,40]{0,1:T(8,128)S(1)} collective-permute-done((f32[40,40]{0,1:T(8,128)S(1)}, f32[40,40]{0,1:T(8,128)S(1)}, u32[]{:S(2)}, u32[]{:S(2)}) %collective-permute-start.5) | collective-permute-done | bytes 6432 | tf_op jit(solution)/shard_map/ppermute | solution.py:136
  77.7 3.8 %collective-permute-done.6 = f32[40,40]{0,1:T(8,128)S(1)} collective-permute-done((f32[40,40]{0,1:T(8,128)S(1)}, f32[40,40]{0,1:T(8,128)S(1)}, u32[]{:S(2)}, u32[]{:S(2)}) %collective-permute-start.6) | collective-permute-done | bytes 6432 | tf_op jit(solution)/shard_map/ppermute | solution.py:136
  81.5 5.0 %collective-permute-done.7 = f32[40,40]{0,1:T(8,128)S(1)} collective-permute-done((f32[40,40]{0,1:T(8,128)S(1)}, f32[40,40]{0,1:T(8,128)S(1)}, u32[]{:S(2)}, u32[]{:S(2)}) %collective-permute-start.7) | collective-permute-done | bytes 6432 | tf_op jit(solution)/shard_map/ppermute | solution.py:136
  86.5 1.2 collective-permute-done.8
  87.7 3.8 %collective-permute-done.9 = f32[40,40]{0,1:T(8,128)S(1)} collective-permute-done((f32[40,40]{0,1:T(8,128)S(1)}, f32[40,40]{0,1:T(8,128)S(1)}, u32[]{:S(2)}, u32[]{:S(2)}) %collective-permute-start.9) | collective-permute-done | bytes 6432 | tf_op jit(solution)/shard_map/ppermute | solution.py:136
  92.0 4.5 %collective-permute-done.10 = f32[40,40]{0,1:T(8,128)S(1)} collective-permute-done((f32[40,40]{0,1:T(8,128)S(1)}, f32[40,40]{0,1:T(8,128)S(1)}, u32[]{:S(2)}, u32[]{:S(2)}) %collective-permute-start.10) | collective-permute-done | bytes 6432 | tf_op jit(solution)/shard_map/ppermute | solution.py:136
  97.1 5.3 %shard_map.60 = (f32[40,40]{1,0:T(8,128)}, f32[40,40]{1,0:T(8,128)}) custom-call(f32[40,40]{1,0:T(8,128)} %fusion.4.gram_ref), custom_call_target="tpu_custom_call" | custom-call | tf_op jit(solution)/shard_map/pallas_call | solution.py:285
  102.4 11.6 %fusion = f32[40,65536]{1,0:T(8,128)S(1)} fusion(f32[40,40]{1,0:T(8,128)} %get-tuple-element.11, f32[5,4096,128]{2,1,0:T(8,128)} %shard_map.59), kind=kOutput, calls=%fused_computation | convolution fusion | flops 1258291200 | bytes 20977920 | tf_op jit(solution)/shard_map/dot_general | solution.py:306
  114.0 4.2 %fusion.8 = f32[40,40]{0,1:T(8,128)S(1)} fusion(f32[40,65536]{1,0:T(8,128)S(1)} %fusion), kind=kOutput, calls=%fused_computation.16 | convolution fusion | flops 629145600 | bytes 10492160 | tf_op jit(solution)/shard_map/dot_general | solution.py:309
  118.3 3.8 %collective-permute-done.11 = f32[40,40]{0,1:T(8,128)S(1)} collective-permute-done((f32[40,40]{0,1:T(8,128)S(1)}, f32[40,40]{0,1:T(8,128)S(1)}, u32[]{:S(2)}, u32[]{:S(2)}) %collective-permute-start.11) | collective-permute-done | bytes 6432 | tf_op jit(solution)/shard_map/ppermute | solution.py:136
  122.1 5.0 %collective-permute-done.12 = f32[40,40]{0,1:T(8,128)S(1)} collective-permute-done((f32[40,40]{0,1:T(8,128)S(1)}, f32[40,40]{0,1:T(8,128)S(1)}, u32[]{:S(2)}, u32[]{:S(2)}) %collective-permute-start.12) | collective-permute-done | bytes 6432 | tf_op jit(solution)/shard_map/ppermute | solution.py:136
  127.1 3.8 %collective-permute-done.13 = f32[40,40]{0,1:T(8,128)S(1)} collective-permute-done((f32[40,40]{0,1:T(8,128)S(1)}, f32[40,40]{0,1:T(8,128)S(1)}, u32[]{:S(2)}, u32[]{:S(2)}) %collective-permute-start.13) | collective-permute-done | bytes 6432 | tf_op jit(solution)/shard_map/ppermute | solution.py:136
  130.9 5.0 %collective-permute-done.14 = f32[40,40]{0,1:T(8,128)S(1)} collective-permute-done((f32[40,40]{0,1:T(8,128)S(1)}, f32[40,40]{0,1:T(8,128)S(1)}, u32[]{:S(2)}, u32[]{:S(2)}) %collective-permute-start.14) | collective-permute-done | bytes 6432 | tf_op jit(solution)/shard_map/ppermute | solution.py:136
  135.9 1.2 collective-permute-done.15
  137.1 3.8 %collective-permute-done.16 = f32[40,40]{0,1:T(8,128)S(1)} collective-permute-done((f32[40,40]{0,1:T(8,128)S(1)}, f32[40,40]{0,1:T(8,128)S(1)}, u32[]{:S(2)}, u32[]{:S(2)}) %collective-permute-start.16) | collective-permute-done | bytes 6432 | tf_op jit(solution)/shard_map/ppermute | solution.py:136
  141.4 4.5 %collective-permute-done.17 = f32[40,40]{0,1:T(8,128)S(1)} collective-permute-done((f32[40,40]{0,1:T(8,128)S(1)}, f32[40,40]{0,1:T(8,128)S(1)}, u32[]{:S(2)}, u32[]{:S(2)}) %collective-permute-start.17) | collective-permute-done | bytes 6432 | tf_op jit(solution)/shard_map/ppermute | solution.py:136
  146.6 5.3 %shard_map.61 = (f32[40,40]{1,0:T(8,128)}, f32[40,40]{1,0:T(8,128)}) custom-call(f32[40,40]{1,0:T(8,128)} %broadcast_multiply_fusion.gram_ref), custom_call_target="tpu_custom_call" | custom-call | tf_op jit(solution)/shard_map/pallas_call | solution.py:285
  151.9 7.1 %convolution_bitcast_fusion = f32[5,8,512,128]{3,1,2,0:T(8,128)S(1)} fusion(f32[40,40]{1,0:T(8,128)} %get-tuple-element.12, f32[40,65536]{1,0:T(8,128)} %copy-done), kind=kOutput, calls=%fused_computation.4 | convolution fusion | flops 629145600 | bytes 20977920 | tf_op jit(solution)/shard_map/dot_general | solution.py:313
  159.1 6.0 %copy.15 = f32[5,8,512,128]{3,2,1,0:T(8,128)} copy(f32[5,8,512,128]{3,1,2,0:T(8,128)S(1)} %convolution_bitcast_fusion) | data formatting | bytes 20971520
  165.0 0.8 fusion.9
  (52 shorter events, 4.3 us)
Async XLA Ops:
  2.6 8.8 %collective-permute-start = (f32[80,4,128]{2,1,0:T(4,128)S(1)}, f32[80,4,128]{2,1,0:T(4,128)S(1)}, u32[]{:S(2)}, u32[]{:S(2)}) collective-permute-start(f32[80,4,128]{2,1,0:T(4,128)S(1)} %pad_maximum_fusion), channel_id=1, source_target_pairs={{8,0},{16,8},{24,16},{32,24},{40,32},{48,40},{56,48},{64,56},{72,6... | collective-permute-start | bytes 491528 | tf_op jit(solution)/shard_map/ppermute | solution.py:93
  8.0 9.0 %collective-permute-start.1 = (f32[80,4,128]{2,1,0:T(4,128)S(1)}, f32[80,4,128]{2,1,0:T(4,128)S(1)}, u32[]{:S(2)}, u32[]{:S(2)}) collective-permute-start(f32[80,4,128]{2,1,0:T(4,128)S(1)} %pad_maximum_fusion.1), channel_id=1, source_target_pairs={{0,8},{8,16},{16,24},{24,32},{32,40},{40,48},{48,56},{56,64},{64,7... | collective-permute-start | bytes 491528 | tf_op jit(solution)/shard_map/ppermute | solution.py:94
  11.4 5.6 %copy-start.1 = (f32[80,4,128]{2,1,0:T(4,128)}, f32[80,4,128]{2,1,0:T(4,128)S(1)}, u32[]{:S(2)}) copy-start(f32[80,4,128]{2,1,0:T(4,128)S(1)} %collective-permute-done.xn_ref.refs_3_.refs_5_.refs_7_) | copy-start | bytes 491524
  17.1 0.7 copy-start.2
  21.9 5.0 %collective-permute-start.2 = (f32[3,80,128]{2,1,0:T(8,128)}, f32[3,80,128]{2,1,0:T(8,128)S(1)}, u32[]{:S(2)}, u32[]{:S(2)}) collective-permute-start(f32[3,80,128]{2,1,0:T(8,128)} %get-tuple-element.9), channel_id=1, source_target_pairs={{1,0},{2,1},{3,2},{4,3},{5,4},{6,5},{7,6},{0,7},{9,8},{10,9},{11,1... | collective-permute-start | bytes 368648 | tf_op jit(solution)/shard_map/ppermute | solution.py:97
  24.2 5.7 %collective-permute-start.3 = (f32[3,80,128]{2,1,0:T(8,128)}, f32[3,80,128]{2,1,0:T(8,128)S(1)}, u32[]{:S(2)}, u32[]{:S(2)}) collective-permute-start(f32[3,80,128]{2,1,0:T(8,128)} %get-tuple-element.10), channel_id=1, source_target_pairs={{0,1},{1,2},{2,3},{3,4},{4,5},{5,6},{6,7},{7,0},{8,9},{9,10},{10,1... | collective-permute-start | bytes 368648 | tf_op jit(solution)/shard_map/ppermute | solution.py:98
  27.0 3.0 %copy-start.3 = (f32[3,80,128]{2,1,0:T(8,128)}, f32[3,80,128]{2,1,0:T(8,128)S(1)}, u32[]{:S(2)}) copy-start(f32[3,80,128]{2,1,0:T(8,128)S(1)} %collective-permute-done.2.refs_9_) | copy-start | bytes 368644
  30.0 0.7 copy-start.4
  68.8 3.9 %collective-permute-start.4 = (f32[40,40]{0,1:T(8,128)S(1)}, f32[40,40]{0,1:T(8,128)S(1)}, u32[]{:S(2)}, u32[]{:S(2)}) collective-permute-start(f32[40,40]{0,1:T(8,128)S(1)} %fusion.2), channel_id=1, source_target_pairs={{0,32},{8,40},{16,48},{24,56},{32,0},{40,8},{48,16},{56,24},{64,96... | collective-permute-start | bytes 19208 | tf_op jit(solution)/shard_map/ppermute | solution.py:136
  72.7 5.0 %collective-permute-start.5 = (f32[40,40]{0,1:T(8,128)S(1)}, f32[40,40]{0,1:T(8,128)S(1)}, u32[]{:S(2)}, u32[]{:S(2)}) collective-permute-start(f32[40,40]{0,1:T(8,128)S(1)} %add.48), channel_id=1, source_target_pairs={{0,96},{8,104},{16,112},{24,120},{32,64},{40,72},{48,80},{56,88},{... | collective-permute-start | bytes 19208 | tf_op jit(solution)/shard_map/ppermute | solution.py:136
  77.7 3.8 %collective-permute-start.6 = (f32[40,40]{0,1:T(8,128)S(1)}, f32[40,40]{0,1:T(8,128)S(1)}, u32[]{:S(2)}, u32[]{:S(2)}) collective-permute-start(f32[40,40]{0,1:T(8,128)S(1)} %add.49), channel_id=1, source_target_pairs={{0,8},{8,0},{16,24},{24,16},{32,40},{40,32},{48,56},{56,48},{64,72... | collective-permute-start | bytes 19208 | tf_op jit(solution)/shard_map/ppermute | solution.py:136
  81.5 5.0 %collective-permute-start.7 = (f32[40,40]{0,1:T(8,128)S(1)}, f32[40,40]{0,1:T(8,128)S(1)}, u32[]{:S(2)}, u32[]{:S(2)}) collective-permute-start(f32[40,40]{0,1:T(8,128)S(1)} %add.50), channel_id=1, source_target_pairs={{0,24},{8,16},{16,8},{24,0},{32,56},{40,48},{48,40},{56,32},{64,88... | collective-permute-start | bytes 19208 | tf_op jit(solution)/shard_map/ppermute | solution.py:136
  86.5 1.2 collective-permute-start.8
  87.7 3.8 %collective-permute-start.9 = (f32[40,40]{0,1:T(8,128)S(1)}, f32[40,40]{0,1:T(8,128)S(1)}, u32[]{:S(2)}, u32[]{:S(2)}) collective-permute-start(f32[40,40]{0,1:T(8,128)S(1)} %add.52), channel_id=1, source_target_pairs={{0,2},{1,3},{2,0},{3,1},{4,6},{5,7},{6,4},{7,5},{8,10},{9,11},{10,... | collective-permute-start | bytes 19208 | tf_op jit(solution)/shard_map/ppermute | solution.py:136
  91.4 5.0 %collective-permute-start.10 = (f32[40,40]{0,1:T(8,128)S(1)}, f32[40,40]{0,1:T(8,128)S(1)}, u32[]{:S(2)}, u32[]{:S(2)}) collective-permute-start(f32[40,40]{0,1:T(8,128)S(1)} %add.53), channel_id=1, source_target_pairs={{0,6},{1,7},{2,4},{3,5},{4,2},{5,3},{6,0},{7,1},{8,14},{9,15},{10,... | collective-permute-start | bytes 19208 | tf_op jit(solution)/shard_map/ppermute | solution.py:136
  114.0 4.2 %copy-start = (f32[40,65536]{1,0:T(8,128)}, f32[40,65536]{1,0:T(8,128)S(1)}, u32[]{:S(2)}) copy-start(f32[40,65536]{1,0:T(8,128)S(1)} %fusion) | copy-start | bytes 31457284
  118.2 3.9 %collective-permute-start.11 = (f32[40,40]{0,1:T(8,128)S(1)}, f32[40,40]{0,1:T(8,128)S(1)}, u32[]{:S(2)}, u32[]{:S(2)}) collective-permute-start(f32[40,40]{0,1:T(8,128)S(1)} %fusion.8), channel_id=1, source_target_pairs={{0,32},{8,40},{16,48},{24,56},{32,0},{40,8},{48,16},{56,24},{64,96... | collective-permute-start | bytes 19208 | tf_op jit(solution)/shard_map/ppermute | solution.py:136
  122.1 5.0 %collective-permute-start.12 = (f32[40,40]{0,1:T(8,128)S(1)}, f32[40,40]{0,1:T(8,128)S(1)}, u32[]{:S(2)}, u32[]{:S(2)}) collective-permute-start(f32[40,40]{0,1:T(8,128)S(1)} %add.56), channel_id=1, source_target_pairs={{0,96},{8,104},{16,112},{24,120},{32,64},{40,72},{48,80},{56,88},{... | collective-permute-start | bytes 19208 | tf_op jit(solution)/shard_map/ppermute | solution.py:136
  127.1 3.8 %collective-permute-start.13 = (f32[40,40]{0,1:T(8,128)S(1)}, f32[40,40]{0,1:T(8,128)S(1)}, u32[]{:S(2)}, u32[]{:S(2)}) collective-permute-start(f32[40,40]{0,1:T(8,128)S(1)} %add.57), channel_id=1, source_target_pairs={{0,8},{8,0},{16,24},{24,16},{32,40},{40,32},{48,56},{56,48},{64,72... | collective-permute-start | bytes 19208 | tf_op jit(solution)/shard_map/ppermute | solution.py:136
  130.9 5.0 %collective-permute-start.14 = (f32[40,40]{0,1:T(8,128)S(1)}, f32[40,40]{0,1:T(8,128)S(1)}, u32[]{:S(2)}, u32[]{:S(2)}) collective-permute-start(f32[40,40]{0,1:T(8,128)S(1)} %add.58), channel_id=1, source_target_pairs={{0,24},{8,16},{16,8},{24,0},{32,56},{40,48},{48,40},{56,32},{64,88... | collective-permute-start | bytes 19208 | tf_op jit(solution)/shard_map/ppermute | solution.py:136
  135.9 1.2 collective-permute-start.15
  137.1 3.8 %collective-permute-start.16 = (f32[40,40]{0,1:T(8,128)S(1)}, f32[40,40]{0,1:T(8,128)S(1)}, u32[]{:S(2)}, u32[]{:S(2)}) collective-permute-start(f32[40,40]{0,1:T(8,128)S(1)} %add.60), channel_id=1, source_target_pairs={{0,2},{1,3},{2,0},{3,1},{4,6},{5,7},{6,4},{7,5},{8,10},{9,11},{10,... | collective-permute-start | bytes 19208 | tf_op jit(solution)/shard_map/ppermute | solution.py:136
  140.8 5.0 %collective-permute-start.17 = (f32[40,40]{0,1:T(8,128)S(1)}, f32[40,40]{0,1:T(8,128)S(1)}, u32[]{:S(2)}, u32[]{:S(2)}) collective-permute-start(f32[40,40]{0,1:T(8,128)S(1)} %add.61), channel_id=1, source_target_pairs={{0,6},{1,7},{2,4},{3,5},{4,2},{5,3},{6,0},{7,1},{8,14},{9,15},{10,... | collective-permute-start | bytes 19208 | tf_op jit(solution)/shard_map/ppermute | solution.py:136
  159.0 6.0 %copy-start.5 = (f32[40,40]{1,0:T(8,128)S(1)}, f32[40,40]{1,0:T(8,128)}, u32[]{:S(2)}) copy-start(f32[40,40]{1,0:T(8,128)} %get-tuple-element.8) | copy-start | bytes 19204
  159.1 6.0 %copy-start.6 = (f32[40,40]{1,0:T(8,128)S(1)}, f32[40,40]{1,0:T(8,128)}, u32[]{:S(2)}) copy-start(f32[40,40]{1,0:T(8,128)} %get-tuple-element.13) | copy-start | bytes 19204

commit v9 on v7

--- a/solution.py
+++ b/solution.py
@@ -242,6 +242,8 @@
     work = gram_ref[...]
     lower = jnp.zeros((size, size), jnp.float32)
     upper = jnp.zeros((size, size), jnp.float32)
+    pending = jnp.where(rows == cols, 1.0, 0.0).astype(jnp.float32)
+    inverse = jnp.zeros((size, size), jnp.float32)
     for j in range(size):
         scale = 1.0 / jnp.sqrt(work[j : j + 1, j : j + 1])
         column = jnp.where(rows[:, j : j + 1] >= j, work[:, j : j + 1] * scale, 0.0)
@@ -249,12 +251,9 @@
         lower = jnp.where(cols == j, column, lower)
         upper = jnp.where(rows == j, row, upper)
         work = work - column * row
-    pending = jnp.where(rows == cols, 1.0, 0.0).astype(jnp.float32)
-    inverse = jnp.zeros((size, size), jnp.float32)
-    for k in range(size):
-        solved = pending[k : k + 1, :] * (1.0 / lower[k : k + 1, k : k + 1])
-        inverse = jnp.where(rows == k, solved, inverse)
-        below = jnp.where(rows[:, k : k + 1] > k, lower[:, k : k + 1], 0.0)
+        solved = pending[j : j + 1, :] * (1.0 / column[j : j + 1, :])
+        inverse = jnp.where(rows == j, solved, inverse)
+        below = jnp.where(rows[:, j : j + 1] > j, column, 0.0)
         pending = pending - below * solved
     upper_ref[...] = upper
     inverse_ref[...] = inverse

time: 166 us -> 166 us (level)
  no operation moved by 1% of the time
where the time goes in v9:
time: 166 us; the launch traced here: 165 us
  waiting for transfers between devices  68.4 us (41%)
  Pallas kernels  40.7 us (25%)
  matrix products  35.5 us (21%)
  local copies, waits for them, and re-layouts  9.47 us (6%)
  starting transfers between devices  9.02 us (5%)
    ppermute x14, waiting for transfers between devices, tree_sum(): lax.ppermute(value, axis, fold_pairs(count, stride, span, fold))  53.9 us
    pallas_call x1, Pallas kernels, krylov_powers(): pl.pallas_call(powers_kernel, grid=(rhs,), in_specs=[pl.BlockSpec((1, dep...  26.4 us
    dot_general x1, matrix products, body(): jnp.dot(krylov, krylov.T, precision=lax.Precision.HIGHEST, preferred_elem...  11.8 us
    dot_general x1, matrix products, body(): jnp.dot(inverse_first, krylov, precision=lax.Precision.HIGHEST, preferred...  11.6 us
    pallas_call x2, Pallas kernels, cholesky_factors(): return pl.pallas_call(factor_kernel, out_shape=[square, square])(symmetric)  10.2 us
    unnamed x15, local copies, waits for them, and re-layouts  7.31 us
    dot_general x1, matrix products, body(): jnp.dot(inverse_second, first_q, precision=lax.Precision.HIGH, preferred_...  7.14 us
    ppermute x1, waiting for transfers between devices, halo_strips(): x_prev = lax.ppermute(last, 'gx', x_next_pairs)  5.63 us
  transfers between devices with their start and end apart: 18, of which 18 were waited for; matrix products, arithmetic and copies ran while one was open for 0% of the time, Pallas kernels for 0%

profile of v9, /device:TPU:0, one launch (start us, length us, event | category | flops | bytes accessed | tf_op | source)
XLA Modules:
  0.0 165.2 jit_solution(13598181185683142242)
XLA Ops:
  0.6 1.1 fusion.5
  1.7 0.9 fusion.6
  2.6 5.4 %collective-permute-start = (f32[80,4,128]{2,1,0:T(4,128)S(1)}, f32[80,4,128]{2,1,0:T(4,128)S(1)}, u32[]{:S(2)}, u32[]{:S(2)}) collective-permute-start(f32[80,4,128]{2,1,0:T(4,128)S(1)} %pad_maximum_fusion), channel_id=1, source_target_pairs={{8,0},{16,8},{24,16},{32,24},{40,32},{48,40},{56,48},{64,56},{72,6... | collective-permute-start | bytes 491528 | tf_op jit(solution)/shard_map/ppermute | solution.py:91
  8.1 3.3 %collective-permute-done.xn_ref.refs_3_.refs_5_.refs_7_ = f32[80,4,128]{2,1,0:T(4,128)S(1)} collective-permute-done((f32[80,4,128]{2,1,0:T(4,128)S(1)}, f32[80,4,128]{2,1,0:T(4,128)S(1)}, u32[]{:S(2)}, u32[]{:S(2)}) %collective-permute-start) | collective-permute-done | bytes 163872 | tf_op jit(solution)/shard_map/ppermute | solution.py:91
  11.4 5.6 %collective-permute-done.1.xp_ref.refs_4_.refs_6_.refs_8_ = f32[80,4,128]{2,1,0:T(4,128)S(1)} collective-permute-done((f32[80,4,128]{2,1,0:T(4,128)S(1)}, f32[80,4,128]{2,1,0:T(4,128)S(1)}, u32[]{:S(2)}, u32[]{:S(2)}) %collective-permute-start.1) | collective-permute-done | bytes 163872 | tf_op jit(solution)/shard_map/ppermute | solution.py:92
  17.7 4.0 %shard_map.58 = (f32[3,72,128]{2,1,0:T(8,128)}, f32[3,72,128]{2,1,0:T(8,128)}) custom-call(f32[8,8,64,128]{3,2,1,0:T(8,128)} %refs_0_.1, f32[8,64,128]{2,1,0:T(8,128)} %refs_1_.1, f32[8,64,128]{2,1,0:T(8,128)} %refs_2_.1, f32[80,4,128]{2,1,0:T(4,128)} %copy-done.1, f32[80,4,128]{2,1,0:T(4,128)} %copy-done.2), custom_call_target="tpu_custom_call" | custom-call | tf_op jit(solution)/shard_map/pallas_call | solution.py:72
  21.8 2.3 %collective-permute-start.2 = (f32[3,72,128]{2,1,0:T(8,128)}, f32[3,72,128]{2,1,0:T(8,128)S(1)}, u32[]{:S(2)}, u32[]{:S(2)}) collective-permute-start(f32[3,72,128]{2,1,0:T(8,128)} %get-tuple-element.9), channel_id=1, source_target_pairs={{1,0},{2,1},{3,2},{4,3},{5,4},{6,5},{7,6},{0,7},{9,8},{10,9},{11,1... | collective-permute-start | bytes 331784 | tf_op jit(solution)/shard_map/ppermute | solution.py:95
  24.1 2.6 %collective-permute-done.2.refs_9_ = f32[3,72,128]{2,1,0:T(8,128)S(1)} collective-permute-done((f32[3,72,128]{2,1,0:T(8,128)}, f32[3,72,128]{2,1,0:T(8,128)S(1)}, u32[]{:S(2)}, u32[]{:S(2)}) %collective-permute-start.2) | collective-permute-done | bytes 110624 | tf_op jit(solution)/shard_map/ppermute | solution.py:95
  26.7 2.9 %collective-permute-done.3.refs_10_ = f32[3,72,128]{2,1,0:T(8,128)S(1)} collective-permute-done((f32[3,72,128]{2,1,0:T(8,128)}, f32[3,72,128]{2,1,0:T(8,128)S(1)}, u32[]{:S(2)}, u32[]{:S(2)}) %collective-permute-start.3) | collective-permute-done | bytes 110624 | tf_op jit(solution)/shard_map/ppermute | solution.py:96
  30.3 26.4 %shard_map.59 = f32[5,4096,128]{2,1,0:T(8,128)} custom-call(f32[8,8,64,128]{3,2,1,0:T(8,128)} %refs_0_.1, f32[8,64,128]{2,1,0:T(8,128)} %refs_1_.1, f32[8,64,128]{2,1,0:T(8,128)} %refs_2_.1, f32[80,4,128]{2,1,0:T(4,128)} %copy-done.1, f32[80,4,128]{2,1,0:T(4,128)} %copy-done.2, f32[80,4,128]{2,1,0:T(4,128)} %copy-done.1, f32[80,4,128]{2,1,0:T(4,128)} %copy-done.2, ...), custom_call_target="tpu_custom_call" | custom-call | tf_op jit(solution)/shard_map/pallas_call | solution.py:216
  56.7 11.8 %fusion.2 = f32[40,40]{0,1:T(8,128)S(1)} fusion(f32[5,4096,128]{2,1,0:T(8,128)} %shard_map.59), kind=kOutput, calls=%fused_computation.2 | convolution fusion | flops 1258291200 | bytes 10492160 | tf_op jit(solution)/shard_map/dot_general | solution.py:284
  68.6 3.8 %collective-permute-done.4 = f32[40,40]{0,1:T(8,128)S(1)} collective-permute-done((f32[40,40]{0,1:T(8,128)S(1)}, f32[40,40]{0,1:T(8,128)S(1)}, u32[]{:S(2)}, u32[]{:S(2)}) %collective-permute-start.4) | collective-permute-done | bytes 6432 | tf_op jit(solution)/shard_map/ppermute | solution.py:134
  72.4 5.0 %collective-permute-done.5 = f32[40,40]{0,1:T(8,128)S(1)} collective-permute-done((f32[40,40]{0,1:T(8,128)S(1)}, f32[40,40]{0,1:T(8,128)S(1)}, u32[]{:S(2)}, u32[]{:S(2)}) %collective-permute-start.5) | collective-permute-done | bytes 6432 | tf_op jit(solution)/shard_map/ppermute | solution.py:134
  77.4 3.8 %collective-permute-done.6 = f32[40,40]{0,1:T(8,128)S(1)} collective-permute-done((f32[40,40]{0,1:T(8,128)S(1)}, f32[40,40]{0,1:T(8,128)S(1)}, u32[]{:S(2)}, u32[]{:S(2)}) %collective-permute-start.6) | collective-permute-done | bytes 6432 | tf_op jit(solution)/shard_map/ppermute | solution.py:134
  81.2 5.0 %collective-permute-done.7 = f32[40,40]{0,1:T(8,128)S(1)} collective-permute-done((f32[40,40]{0,1:T(8,128)S(1)}, f32[40,40]{0,1:T(8,128)S(1)}, u32[]{:S(2)}, u32[]{:S(2)}) %collective-permute-start.7) | collective-permute-done | bytes 6432 | tf_op jit(solution)/shard_map/ppermute | solution.py:134
  86.2 1.2 collective-permute-done.8
  87.4 3.8 %collective-permute-done.9 = f32[40,40]{0,1:T(8,128)S(1)} collective-permute-done((f32[40,40]{0,1:T(8,128)S(1)}, f32[40,40]{0,1:T(8,128)S(1)}, u32[]{:S(2)}, u32[]{:S(2)}) %collective-permute-start.9) | collective-permute-done | bytes 6432 | tf_op jit(solution)/shard_map/ppermute | solution.py:134
  91.7 4.4 %collective-permute-done.10 = f32[40,40]{0,1:T(8,128)S(1)} collective-permute-done((f32[40,40]{0,1:T(8,128)S(1)}, f32[40,40]{0,1:T(8,128)S(1)}, u32[]{:S(2)}, u32[]{:S(2)}) %collective-permute-start.10) | collective-permute-done | bytes 6432 | tf_op jit(solution)/shard_map/ppermute | solution.py:134
  96.9 5.1 %shard_map.60 = (f32[40,40]{1,0:T(8,128)}, f32[40,40]{1,0:T(8,128)}) custom-call(f32[40,40]{1,0:T(8,128)} %fusion.4.gram_ref), custom_call_target="tpu_custom_call" | custom-call | tf_op jit(solution)/shard_map/pallas_call | solution.py:267
  102.0 11.6 %fusion = f32[40,65536]{1,0:T(8,128)S(1)} fusion(f32[40,40]{1,0:T(8,128)} %get-tuple-element.11, f32[5,4096,128]{2,1,0:T(8,128)} %shard_map.59), kind=kOutput, calls=%fused_computation | convolution fusion | flops 1258291200 | bytes 20977920 | tf_op jit(solution)/shard_map/dot_general | solution.py:288
  113.6 4.2 %fusion.8 = f32[40,40]{0,1:T(8,128)S(1)} fusion(f32[40,65536]{1,0:T(8,128)S(1)} %fusion), kind=kOutput, calls=%fused_computation.16 | convolution fusion | flops 629145600 | bytes 10492160 | tf_op jit(solution)/shard_map/dot_general | solution.py:291
  117.9 3.8 %collective-permute-done.11 = f32[40,40]{0,1:T(8,128)S(1)} collective-permute-done((f32[40,40]{0,1:T(8,128)S(1)}, f32[40,40]{0,1:T(8,128)S(1)}, u32[]{:S(2)}, u32[]{:S(2)}) %collective-permute-start.11) | collective-permute-done | bytes 6432 | tf_op jit(solution)/shard_map/ppermute | solution.py:134
  121.7 5.0 %collective-permute-done.12 = f32[40,40]{0,1:T(8,128)S(1)} collective-permute-done((f32[40,40]{0,1:T(8,128)S(1)}, f32[40,40]{0,1:T(8,128)S(1)}, u32[]{:S(2)}, u32[]{:S(2)}) %collective-permute-start.12) | collective-permute-done | bytes 6432 | tf_op jit(solution)/shard_map/ppermute | solution.py:134
  126.7 3.8 %collective-permute-done.13 = f32[40,40]{0,1:T(8,128)S(1)} collective-permute-done((f32[40,40]{0,1:T(8,128)S(1)}, f32[40,40]{0,1:T(8,128)S(1)}, u32[]{:S(2)}, u32[]{:S(2)}) %collective-permute-start.13) | collective-permute-done | bytes 6432 | tf_op jit(solution)/shard_map/ppermute | solution.py:134
  130.4 5.0 %collective-permute-done.14 = f32[40,40]{0,1:T(8,128)S(1)} collective-permute-done((f32[40,40]{0,1:T(8,128)S(1)}, f32[40,40]{0,1:T(8,128)S(1)}, u32[]{:S(2)}, u32[]{:S(2)}) %collective-permute-start.14) | collective-permute-done | bytes 6432 | tf_op jit(solution)/shard_map/ppermute | solution.py:134
  135.4 1.2 collective-permute-done.15
  136.6 3.8 %collective-permute-done.16 = f32[40,40]{0,1:T(8,128)S(1)} collective-permute-done((f32[40,40]{0,1:T(8,128)S(1)}, f32[40,40]{0,1:T(8,128)S(1)}, u32[]{:S(2)}, u32[]{:S(2)}) %collective-permute-start.16) | collective-permute-done | bytes 6432 | tf_op jit(solution)/shard_map/ppermute | solution.py:134
  141.0 4.4 %collective-permute-done.17 = f32[40,40]{0,1:T(8,128)S(1)} collective-permute-done((f32[40,40]{0,1:T(8,128)S(1)}, f32[40,40]{0,1:T(8,128)S(1)}, u32[]{:S(2)}, u32[]{:S(2)}) %collective-permute-start.17) | collective-permute-done | bytes 6432 | tf_op jit(solution)/shard_map/ppermute | solution.py:134
  146.2 5.1 %shard_map.61 = (f32[40,40]{1,0:T(8,128)}, f32[40,40]{1,0:T(8,128)}) custom-call(f32[40,40]{1,0:T(8,128)} %broadcast_multiply_fusion.gram_ref), custom_call_target="tpu_custom_call" | custom-call | tf_op jit(solution)/shard_map/pallas_call | solution.py:267
  151.3 7.1 %convolution_bitcast_fusion = f32[5,8,512,128]{3,1,2,0:T(8,128)S(1)} fusion(f32[40,40]{1,0:T(8,128)} %get-tuple-element.12, f32[40,65536]{1,0:T(8,128)} %copy-done), kind=kOutput, calls=%fused_computation.4 | convolution fusion | flops 629145600 | bytes 20977920 | tf_op jit(solution)/shard_map/dot_general | solution.py:295
  158.5 6.0 %copy.15 = f32[5,8,512,128]{3,2,1,0:T(8,128)} copy(f32[5,8,512,128]{3,1,2,0:T(8,128)S(1)} %convolution_bitcast_fusion) | data formatting | bytes 20971520
  164.5 0.8 fusion.9
  (52 shorter events, 4.3 us)
Async XLA Ops:
  2.6 8.8 %collective-permute-start = (f32[80,4,128]{2,1,0:T(4,128)S(1)}, f32[80,4,128]{2,1,0:T(4,128)S(1)}, u32[]{:S(2)}, u32[]{:S(2)}) collective-permute-start(f32[80,4,128]{2,1,0:T(4,128)S(1)} %pad_maximum_fusion), channel_id=1, source_target_pairs={{8,0},{16,8},{24,16},{32,24},{40,32},{48,40},{56,48},{64,56},{72,6... | collective-permute-start | bytes 491528 | tf_op jit(solution)/shard_map/ppermute | solution.py:91
  8.0 9.0 %collective-permute-start.1 = (f32[80,4,128]{2,1,0:T(4,128)S(1)}, f32[80,4,128]{2,1,0:T(4,128)S(1)}, u32[]{:S(2)}, u32[]{:S(2)}) collective-permute-start(f32[80,4,128]{2,1,0:T(4,128)S(1)} %pad_maximum_fusion.1), channel_id=1, source_target_pairs={{0,8},{8,16},{16,24},{24,32},{32,40},{40,48},{48,56},{56,64},{64,7... | collective-permute-start | bytes 491528 | tf_op jit(solution)/shard_map/ppermute | solution.py:92
  11.4 5.6 %copy-start.1 = (f32[80,4,128]{2,1,0:T(4,128)}, f32[80,4,128]{2,1,0:T(4,128)S(1)}, u32[]{:S(2)}) copy-start(f32[80,4,128]{2,1,0:T(4,128)S(1)} %collective-permute-done.xn_ref.refs_3_.refs_5_.refs_7_) | copy-start | bytes 491524
  17.1 0.7 copy-start.2
  21.8 4.9 %collective-permute-start.2 = (f32[3,72,128]{2,1,0:T(8,128)}, f32[3,72,128]{2,1,0:T(8,128)S(1)}, u32[]{:S(2)}, u32[]{:S(2)}) collective-permute-start(f32[3,72,128]{2,1,0:T(8,128)} %get-tuple-element.9), channel_id=1, source_target_pairs={{1,0},{2,1},{3,2},{4,3},{5,4},{6,5},{7,6},{0,7},{9,8},{10,9},{11,1... | collective-permute-start | bytes 331784 | tf_op jit(solution)/shard_map/ppermute | solution.py:95
  24.1 5.6 %collective-permute-start.3 = (f32[3,72,128]{2,1,0:T(8,128)}, f32[3,72,128]{2,1,0:T(8,128)S(1)}, u32[]{:S(2)}, u32[]{:S(2)}) collective-permute-start(f32[3,72,128]{2,1,0:T(8,128)} %get-tuple-element.10), channel_id=1, source_target_pairs={{0,1},{1,2},{2,3},{3,4},{4,5},{5,6},{6,7},{7,0},{8,9},{9,10},{10,1... | collective-permute-start | bytes 331784 | tf_op jit(solution)/shard_map/ppermute | solution.py:96
  26.7 3.0 %copy-start.3 = (f32[3,72,128]{2,1,0:T(8,128)}, f32[3,72,128]{2,1,0:T(8,128)S(1)}, u32[]{:S(2)}) copy-start(f32[3,72,128]{2,1,0:T(8,128)S(1)} %collective-permute-done.2.refs_9_) | copy-start | bytes 331780
  29.7 0.7 copy-start.4
  68.5 3.9 %collective-permute-start.4 = (f32[40,40]{0,1:T(8,128)S(1)}, f32[40,40]{0,1:T(8,128)S(1)}, u32[]{:S(2)}, u32[]{:S(2)}) collective-permute-start(f32[40,40]{0,1:T(8,128)S(1)} %fusion.2), channel_id=1, source_target_pairs={{0,32},{8,40},{16,48},{24,56},{32,0},{40,8},{48,16},{56,24},{64,96... | collective-permute-start | bytes 19208 | tf_op jit(solution)/shard_map/ppermute | solution.py:134
  72.4 5.0 %collective-permute-start.5 = (f32[40,40]{0,1:T(8,128)S(1)}, f32[40,40]{0,1:T(8,128)S(1)}, u32[]{:S(2)}, u32[]{:S(2)}) collective-permute-start(f32[40,40]{0,1:T(8,128)S(1)} %add.48), channel_id=1, source_target_pairs={{0,96},{8,104},{16,112},{24,120},{32,64},{40,72},{48,80},{56,88},{... | collective-permute-start | bytes 19208 | tf_op jit(solution)/shard_map/ppermute | solution.py:134
  77.4 3.8 %collective-permute-start.6 = (f32[40,40]{0,1:T(8,128)S(1)}, f32[40,40]{0,1:T(8,128)S(1)}, u32[]{:S(2)}, u32[]{:S(2)}) collective-permute-start(f32[40,40]{0,1:T(8,128)S(1)} %add.49), channel_id=1, source_target_pairs={{0,8},{8,0},{16,24},{24,16},{32,40},{40,32},{48,56},{56,48},{64,72... | collective-permute-start | bytes 19208 | tf_op jit(solution)/shard_map/ppermute | solution.py:134
  81.2 5.0 %collective-permute-start.7 = (f32[40,40]{0,1:T(8,128)S(1)}, f32[40,40]{0,1:T(8,128)S(1)}, u32[]{:S(2)}, u32[]{:S(2)}) collective-permute-start(f32[40,40]{0,1:T(8,128)S(1)} %add.50), channel_id=1, source_target_pairs={{0,24},{8,16},{16,8},{24,0},{32,56},{40,48},{48,40},{56,32},{64,88... | collective-permute-start | bytes 19208 | tf_op jit(solution)/shard_map/ppermute | solution.py:134
  86.2 1.2 collective-permute-start.8
  87.4 3.8 %collective-permute-start.9 = (f32[40,40]{0,1:T(8,128)S(1)}, f32[40,40]{0,1:T(8,128)S(1)}, u32[]{:S(2)}, u32[]{:S(2)}) collective-permute-start(f32[40,40]{0,1:T(8,128)S(1)} %add.52), channel_id=1, source_target_pairs={{0,2},{1,3},{2,0},{3,1},{4,6},{5,7},{6,4},{7,5},{8,10},{9,11},{10,... | collective-permute-start | bytes 19208 | tf_op jit(solution)/shard_map/ppermute | solution.py:134
  91.2 5.0 %collective-permute-start.10 = (f32[40,40]{0,1:T(8,128)S(1)}, f32[40,40]{0,1:T(8,128)S(1)}, u32[]{:S(2)}, u32[]{:S(2)}) collective-permute-start(f32[40,40]{0,1:T(8,128)S(1)} %add.53), channel_id=1, source_target_pairs={{0,6},{1,7},{2,4},{3,5},{4,2},{5,3},{6,0},{7,1},{8,14},{9,15},{10,... | collective-permute-start | bytes 19208 | tf_op jit(solution)/shard_map/ppermute | solution.py:134
  113.6 4.2 %copy-start = (f32[40,65536]{1,0:T(8,128)}, f32[40,65536]{1,0:T(8,128)S(1)}, u32[]{:S(2)}) copy-start(f32[40,65536]{1,0:T(8,128)S(1)} %fusion) | copy-start | bytes 31457284
  117.8 3.9 %collective-permute-start.11 = (f32[40,40]{0,1:T(8,128)S(1)}, f32[40,40]{0,1:T(8,128)S(1)}, u32[]{:S(2)}, u32[]{:S(2)}) collective-permute-start(f32[40,40]{0,1:T(8,128)S(1)} %fusion.8), channel_id=1, source_target_pairs={{0,32},{8,40},{16,48},{24,56},{32,0},{40,8},{48,16},{56,24},{64,96... | collective-permute-start | bytes 19208 | tf_op jit(solution)/shard_map/ppermute | solution.py:134
  121.6 5.0 %collective-permute-start.12 = (f32[40,40]{0,1:T(8,128)S(1)}, f32[40,40]{0,1:T(8,128)S(1)}, u32[]{:S(2)}, u32[]{:S(2)}) collective-permute-start(f32[40,40]{0,1:T(8,128)S(1)} %add.56), channel_id=1, source_target_pairs={{0,96},{8,104},{16,112},{24,120},{32,64},{40,72},{48,80},{56,88},{... | collective-permute-start | bytes 19208 | tf_op jit(solution)/shard_map/ppermute | solution.py:134
  126.6 3.8 %collective-permute-start.13 = (f32[40,40]{0,1:T(8,128)S(1)}, f32[40,40]{0,1:T(8,128)S(1)}, u32[]{:S(2)}, u32[]{:S(2)}) collective-permute-start(f32[40,40]{0,1:T(8,128)S(1)} %add.57), channel_id=1, source_target_pairs={{0,8},{8,0},{16,24},{24,16},{32,40},{40,32},{48,56},{56,48},{64,72... | collective-permute-start | bytes 19208 | tf_op jit(solution)/shard_map/ppermute | solution.py:134
  130.4 5.0 %collective-permute-start.14 = (f32[40,40]{0,1:T(8,128)S(1)}, f32[40,40]{0,1:T(8,128)S(1)}, u32[]{:S(2)}, u32[]{:S(2)}) collective-permute-start(f32[40,40]{0,1:T(8,128)S(1)} %add.58), channel_id=1, source_target_pairs={{0,24},{8,16},{16,8},{24,0},{32,56},{40,48},{48,40},{56,32},{64,88... | collective-permute-start | bytes 19208 | tf_op jit(solution)/shard_map/ppermute | solution.py:134
  135.4 1.2 collective-permute-start.15
  136.6 3.8 %collective-permute-start.16 = (f32[40,40]{0,1:T(8,128)S(1)}, f32[40,40]{0,1:T(8,128)S(1)}, u32[]{:S(2)}, u32[]{:S(2)}) collective-permute-start(f32[40,40]{0,1:T(8,128)S(1)} %add.60), channel_id=1, source_target_pairs={{0,2},{1,3},{2,0},{3,1},{4,6},{5,7},{6,4},{7,5},{8,10},{9,11},{10,... | collective-permute-start | bytes 19208 | tf_op jit(solution)/shard_map/ppermute | solution.py:134
  140.4 5.0 %collective-permute-start.17 = (f32[40,40]{0,1:T(8,128)S(1)}, f32[40,40]{0,1:T(8,128)S(1)}, u32[]{:S(2)}, u32[]{:S(2)}) collective-permute-start(f32[40,40]{0,1:T(8,128)S(1)} %add.61), channel_id=1, source_target_pairs={{0,6},{1,7},{2,4},{3,5},{4,2},{5,3},{6,0},{7,1},{8,14},{9,15},{10,... | collective-permute-start | bytes 19208 | tf_op jit(solution)/shard_map/ppermute | solution.py:134
  158.5 6.0 %copy-start.5 = (f32[40,40]{1,0:T(8,128)S(1)}, f32[40,40]{1,0:T(8,128)}, u32[]{:S(2)}) copy-start(f32[40,40]{1,0:T(8,128)} %get-tuple-element.8) | copy-start | bytes 19204
  158.5 6.0 %copy-start.6 = (f32[40,40]{1,0:T(8,128)S(1)}, f32[40,40]{1,0:T(8,128)}, u32[]{:S(2)}) copy-start(f32[40,40]{1,0:T(8,128)} %get-tuple-element.13) | copy-start | bytes 19204

commit v10 on v7

--- a/solution.py
+++ b/solution.py
@@ -1,3 +1,5 @@
+import functools
+
 import jax
 import jax.numpy as jnp
 from jax import lax
@@ -235,11 +237,17 @@
     )(start_block, conductivity, reaction, *([x_next, x_prev] * 3), y_next, y_prev)
 
 
-def factor_kernel(gram_ref, upper_ref, inverse_ref):
+def factor_kernel(gram_ref, upper_ref, inverse_ref, *, cells_total):
     size = gram_ref.shape[0]
     rows = lax.broadcasted_iota(jnp.int32, (size, size), 0)
     cols = lax.broadcasted_iota(jnp.int32, (size, size), 1)
-    work = gram_ref[...]
+    scaled = gram_ref[...] / cells_total
+    wide = LANES // 2
+    tile = jnp.zeros((wide, wide), jnp.float32)
+    tile = jnp.concatenate(
+        [jnp.concatenate([scaled, jnp.zeros((size, wide - size), jnp.float32)], axis=1), tile[size:]], axis=0
+    )
+    work = (scaled + tile.T[:size, :size]) / 2
     lower = jnp.zeros((size, size), jnp.float32)
     upper = jnp.zeros((size, size), jnp.float32)
     for j in range(size):
@@ -263,9 +271,8 @@
 def cholesky_factors(gram, cells_total):
     size = gram.shape[0]
     square = jax.ShapeDtypeStruct((size, size), jnp.float32)
-    scaled = gram / cells_total
-    symmetric = (scaled + scaled.T) / 2
-    return pl.pallas_call(factor_kernel, out_shape=[square, square])(symmetric)
+    kernel = functools.partial(factor_kernel, cells_total=float(cells_total))
+    return pl.pallas_call(kernel, out_shape=[square, square])(gram)
 
 
 def body(start_block, conductivity, reaction):

time: 166 us -> 167 us (level)
  no operation moved by 1% of the time
where the time goes in v10:
time: 167 us; the launch traced here: 166 us
  waiting for transfers between devices  68.4 us (41%)
  Pallas kernels  41.1 us (25%)
  matrix products  36.3 us (22%)
  local copies, waits for them, and re-layouts  9.25 us (6%)
  starting transfers between devices  9 us (5%)
    ppermute x14, waiting for transfers between devices, tree_sum(): lax.ppermute(value, axis, fold_pairs(count, stride, span, fold))  53.9 us
    pallas_call x1, Pallas kernels, krylov_powers(): pl.pallas_call(powers_kernel, grid=(rhs,), in_specs=[pl.BlockSpec((1, dep...  26.4 us
    dot_general x1, matrix products, body(): jnp.dot(krylov, krylov.T, precision=lax.Precision.HIGHEST, preferred_elem...  12.6 us
    dot_general x1, matrix products, body(): jnp.dot(inverse_first, krylov, precision=lax.Precision.HIGHEST, preferred...  11.6 us
    pallas_call x2, Pallas kernels, cholesky_factors(): return pl.pallas_call(kernel, out_shape=[square, square])(gram)  10.7 us
    unnamed x15, local copies, waits for them, and re-layouts  7.31 us
    dot_general x1, matrix products, body(): jnp.dot(inverse_second, first_q, precision=lax.Precision.HIGH, preferred_...  7.14 us
    ppermute x1, waiting for transfers between devices, halo_strips(): x_prev = lax.ppermute(last, 'gx', x_next_pairs)  5.63 us
  transfers between devices with their start and end apart: 18, of which 18 were waited for; matrix products, arithmetic and copies ran while one was open for 0% of the time, Pallas kernels for 0%

profile of v10, /device:TPU:0, one launch (start us, length us, event | category | flops | bytes accessed | tf_op | source)
XLA Modules:
  0.0 166.2 jit_solution(8287831814236910416)
XLA Ops:
  0.6 1.1 fusion.4
  1.7 0.9 fusion.5
  2.6 5.4 %collective-permute-start = (f32[80,4,128]{2,1,0:T(4,128)S(1)}, f32[80,4,128]{2,1,0:T(4,128)S(1)}, u32[]{:S(2)}, u32[]{:S(2)}) collective-permute-start(f32[80,4,128]{2,1,0:T(4,128)S(1)} %pad_maximum_fusion), channel_id=1, source_target_pairs={{8,0},{16,8},{24,16},{32,24},{40,32},{48,40},{56,48},{64,56},{72,6... | collective-permute-start | bytes 491528 | tf_op jit(solution)/shard_map/ppermute | solution.py:93
  8.1 3.3 %collective-permute-done.xn_ref.refs_3_.refs_5_.refs_7_ = f32[80,4,128]{2,1,0:T(4,128)S(1)} collective-permute-done((f32[80,4,128]{2,1,0:T(4,128)S(1)}, f32[80,4,128]{2,1,0:T(4,128)S(1)}, u32[]{:S(2)}, u32[]{:S(2)}) %collective-permute-start) | collective-permute-done | bytes 163872 | tf_op jit(solution)/shard_map/ppermute | solution.py:93
  11.4 5.6 %collective-permute-done.1.xp_ref.refs_4_.refs_6_.refs_8_ = f32[80,4,128]{2,1,0:T(4,128)S(1)} collective-permute-done((f32[80,4,128]{2,1,0:T(4,128)S(1)}, f32[80,4,128]{2,1,0:T(4,128)S(1)}, u32[]{:S(2)}, u32[]{:S(2)}) %collective-permute-start.1) | collective-permute-done | bytes 163872 | tf_op jit(solution)/shard_map/ppermute | solution.py:94
  17.7 4.0 %shard_map.58 = (f32[3,72,128]{2,1,0:T(8,128)}, f32[3,72,128]{2,1,0:T(8,128)}) custom-call(f32[8,8,64,128]{3,2,1,0:T(8,128)} %refs_0_.1, f32[8,64,128]{2,1,0:T(8,128)} %refs_1_.1, f32[8,64,128]{2,1,0:T(8,128)} %refs_2_.1, f32[80,4,128]{2,1,0:T(4,128)} %copy-done.1, f32[80,4,128]{2,1,0:T(4,128)} %copy-done.2), custom_call_target="tpu_custom_call" | custom-call | tf_op jit(solution)/shard_map/pallas_call | solution.py:74
  21.8 2.3 %collective-permute-start.2 = (f32[3,72,128]{2,1,0:T(8,128)}, f32[3,72,128]{2,1,0:T(8,128)S(1)}, u32[]{:S(2)}, u32[]{:S(2)}) collective-permute-start(f32[3,72,128]{2,1,0:T(8,128)} %get-tuple-element.9), channel_id=1, source_target_pairs={{1,0},{2,1},{3,2},{4,3},{5,4},{6,5},{7,6},{0,7},{9,8},{10,9},{11,1... | collective-permute-start | bytes 331784 | tf_op jit(solution)/shard_map/ppermute | solution.py:97
  24.1 2.6 %collective-permute-done.2.refs_9_ = f32[3,72,128]{2,1,0:T(8,128)S(1)} collective-permute-done((f32[3,72,128]{2,1,0:T(8,128)}, f32[3,72,128]{2,1,0:T(8,128)S(1)}, u32[]{:S(2)}, u32[]{:S(2)}) %collective-permute-start.2) | collective-permute-done | bytes 110624 | tf_op jit(solution)/shard_map/ppermute | solution.py:97
  26.7 2.9 %collective-permute-done.3.refs_10_ = f32[3,72,128]{2,1,0:T(8,128)S(1)} collective-permute-done((f32[3,72,128]{2,1,0:T(8,128)}, f32[3,72,128]{2,1,0:T(8,128)S(1)}, u32[]{:S(2)}, u32[]{:S(2)}) %collective-permute-start.3) | collective-permute-done | bytes 110624 | tf_op jit(solution)/shard_map/ppermute | solution.py:98
  30.3 26.4 %shard_map.59 = f32[5,4096,128]{2,1,0:T(8,128)} custom-call(f32[8,8,64,128]{3,2,1,0:T(8,128)} %refs_0_.1, f32[8,64,128]{2,1,0:T(8,128)} %refs_1_.1, f32[8,64,128]{2,1,0:T(8,128)} %refs_2_.1, f32[80,4,128]{2,1,0:T(4,128)} %copy-done.1, f32[80,4,128]{2,1,0:T(4,128)} %copy-done.2, f32[80,4,128]{2,1,0:T(4,128)} %copy-done.1, f32[80,4,128]{2,1,0:T(4,128)} %copy-done.2, ...), custom_call_target="tpu_custom_call" | custom-call | tf_op jit(solution)/shard_map/pallas_call | solution.py:218
  56.7 12.6 %fusion.2 = f32[40,40]{1,0:T(8,128)S(1)} fusion(f32[5,4096,128]{2,1,0:T(8,128)} %shard_map.59), kind=kOutput, calls=%fused_computation.2 | convolution fusion | flops 1258291200 | bytes 10492160 | tf_op jit(solution)/shard_map/dot_general | solution.py:292
  69.4 3.8 %collective-permute-done.4 = f32[40,40]{1,0:T(8,128)S(1)} collective-permute-done((f32[40,40]{1,0:T(8,128)S(1)}, f32[40,40]{1,0:T(8,128)S(1)}, u32[]{:S(2)}, u32[]{:S(2)}) %collective-permute-start.4) | collective-permute-done | bytes 6432 | tf_op jit(solution)/shard_map/ppermute | solution.py:136
  73.2 5.0 %collective-permute-done.5 = f32[40,40]{1,0:T(8,128)S(1)} collective-permute-done((f32[40,40]{1,0:T(8,128)S(1)}, f32[40,40]{1,0:T(8,128)S(1)}, u32[]{:S(2)}, u32[]{:S(2)}) %collective-permute-start.5) | collective-permute-done | bytes 6432 | tf_op jit(solution)/shard_map/ppermute | solution.py:136
  78.2 3.8 %collective-permute-done.6 = f32[40,40]{1,0:T(8,128)S(1)} collective-permute-done((f32[40,40]{1,0:T(8,128)S(1)}, f32[40,40]{1,0:T(8,128)S(1)}, u32[]{:S(2)}, u32[]{:S(2)}) %collective-permute-start.6) | collective-permute-done | bytes 6432 | tf_op jit(solution)/shard_map/ppermute | solution.py:136
  82.0 5.0 %collective-permute-done.7 = f32[40,40]{1,0:T(8,128)S(1)} collective-permute-done((f32[40,40]{1,0:T(8,128)S(1)}, f32[40,40]{1,0:T(8,128)S(1)}, u32[]{:S(2)}, u32[]{:S(2)}) %collective-permute-start.7) | collective-permute-done | bytes 6432 | tf_op jit(solution)/shard_map/ppermute | solution.py:136
  87.0 1.2 collective-permute-done.8
  88.2 3.8 %collective-permute-done.9 = f32[40,40]{1,0:T(8,128)S(1)} collective-permute-done((f32[40,40]{1,0:T(8,128)S(1)}, f32[40,40]{1,0:T(8,128)S(1)}, u32[]{:S(2)}, u32[]{:S(2)}) %collective-permute-start.9) | collective-permute-done | bytes 6432 | tf_op jit(solution)/shard_map/ppermute | solution.py:136
  92.5 4.5 %collective-permute-done.10 = f32[40,40]{1,0:T(8,128)S(1)} collective-permute-done((f32[40,40]{1,0:T(8,128)S(1)}, f32[40,40]{1,0:T(8,128)S(1)}, u32[]{:S(2)}, u32[]{:S(2)}) %collective-permute-start.10) | collective-permute-done | bytes 6432 | tf_op jit(solution)/shard_map/ppermute | solution.py:136
  97.6 5.3 %shard_map.60 = (f32[40,40]{1,0:T(8,128)}, f32[40,40]{1,0:T(8,128)}) custom-call(f32[40,40]{1,0:T(8,128)} %add.48.gram_ref), custom_call_target="tpu_custom_call" | custom-call | tf_op jit(solution)/shard_map/pallas_call | solution.py:275
  102.9 11.6 %fusion = f32[40,65536]{1,0:T(8,128)S(1)} fusion(f32[40,40]{1,0:T(8,128)} %get-tuple-element.11, f32[5,4096,128]{2,1,0:T(8,128)} %shard_map.59), kind=kOutput, calls=%fused_computation | convolution fusion | flops 1258291200 | bytes 20977920 | tf_op jit(solution)/shard_map/dot_general | solution.py:296
  114.5 4.2 %fusion.7 = f32[40,40]{1,0:T(8,128)S(1)} fusion(f32[40,65536]{1,0:T(8,128)S(1)} %fusion), kind=kOutput, calls=%fused_computation.10 | convolution fusion | flops 629145600 | bytes 10492160 | tf_op jit(solution)/shard_map/dot_general | solution.py:299
  118.8 3.8 %collective-permute-done.11 = f32[40,40]{1,0:T(8,128)S(1)} collective-permute-done((f32[40,40]{1,0:T(8,128)S(1)}, f32[40,40]{1,0:T(8,128)S(1)}, u32[]{:S(2)}, u32[]{:S(2)}) %collective-permute-start.11) | collective-permute-done | bytes 6432 | tf_op jit(solution)/shard_map/ppermute | solution.py:136
  122.6 5.0 %collective-permute-done.12 = f32[40,40]{1,0:T(8,128)S(1)} collective-permute-done((f32[40,40]{1,0:T(8,128)S(1)}, f32[40,40]{1,0:T(8,128)S(1)}, u32[]{:S(2)}, u32[]{:S(2)}) %collective-permute-start.12) | collective-permute-done | bytes 6432 | tf_op jit(solution)/shard_map/ppermute | solution.py:136
  127.6 3.8 %collective-permute-done.13 = f32[40,40]{1,0:T(8,128)S(1)} collective-permute-done((f32[40,40]{1,0:T(8,128)S(1)}, f32[40,40]{1,0:T(8,128)S(1)}, u32[]{:S(2)}, u32[]{:S(2)}) %collective-permute-start.13) | collective-permute-done | bytes 6432 | tf_op jit(solution)/shard_map/ppermute | solution.py:136
  131.4 5.0 %collective-permute-done.14 = f32[40,40]{1,0:T(8,128)S(1)} collective-permute-done((f32[40,40]{1,0:T(8,128)S(1)}, f32[40,40]{1,0:T(8,128)S(1)}, u32[]{:S(2)}, u32[]{:S(2)}) %collective-permute-start.14) | collective-permute-done | bytes 6432 | tf_op jit(solution)/shard_map/ppermute | solution.py:136
  136.4 1.2 collective-permute-done.15
  137.6 3.8 %collective-permute-done.16 = f32[40,40]{1,0:T(8,128)S(1)} collective-permute-done((f32[40,40]{1,0:T(8,128)S(1)}, f32[40,40]{1,0:T(8,128)S(1)}, u32[]{:S(2)}, u32[]{:S(2)}) %collective-permute-start.16) | collective-permute-done | bytes 6432 | tf_op jit(solution)/shard_map/ppermute | solution.py:136
  141.9 4.5 %collective-permute-done.17 = f32[40,40]{1,0:T(8,128)S(1)} collective-permute-done((f32[40,40]{1,0:T(8,128)S(1)}, f32[40,40]{1,0:T(8,128)S(1)}, u32[]{:S(2)}, u32[]{:S(2)}) %collective-permute-start.17) | collective-permute-done | bytes 6432 | tf_op jit(solution)/shard_map/ppermute | solution.py:136
  147.0 5.3 %shard_map.61 = (f32[40,40]{1,0:T(8,128)}, f32[40,40]{1,0:T(8,128)}) custom-call(f32[40,40]{1,0:T(8,128)} %add.55.gram_ref), custom_call_target="tpu_custom_call" | custom-call | tf_op jit(solution)/shard_map/pallas_call | solution.py:275
  152.3 7.1 %convolution_bitcast_fusion = f32[5,8,512,128]{3,1,2,0:T(8,128)S(1)} fusion(f32[40,40]{1,0:T(8,128)} %get-tuple-element.12, f32[40,65536]{1,0:T(8,128)} %copy-done), kind=kOutput, calls=%fused_computation.4 | convolution fusion | flops 629145600 | bytes 20977920 | tf_op jit(solution)/shard_map/dot_general | solution.py:303
  159.5 6.0 %copy.6 = f32[5,8,512,128]{3,2,1,0:T(8,128)} copy(f32[5,8,512,128]{3,1,2,0:T(8,128)S(1)} %convolution_bitcast_fusion) | data formatting | bytes 20971520
  165.5 0.8 fusion.8
  (46 shorter events, 4.0 us)
Async XLA Ops:
  2.6 8.8 %collective-permute-start = (f32[80,4,128]{2,1,0:T(4,128)S(1)}, f32[80,4,128]{2,1,0:T(4,128)S(1)}, u32[]{:S(2)}, u32[]{:S(2)}) collective-permute-start(f32[80,4,128]{2,1,0:T(4,128)S(1)} %pad_maximum_fusion), channel_id=1, source_target_pairs={{8,0},{16,8},{24,16},{32,24},{40,32},{48,40},{56,48},{64,56},{72,6... | collective-permute-start | bytes 491528 | tf_op jit(solution)/shard_map/ppermute | solution.py:93
  8.0 9.0 %collective-permute-start.1 = (f32[80,4,128]{2,1,0:T(4,128)S(1)}, f32[80,4,128]{2,1,0:T(4,128)S(1)}, u32[]{:S(2)}, u32[]{:S(2)}) collective-permute-start(f32[80,4,128]{2,1,0:T(4,128)S(1)} %pad_maximum_fusion.1), channel_id=1, source_target_pairs={{0,8},{8,16},{16,24},{24,32},{32,40},{40,48},{48,56},{56,64},{64,7... | collective-permute-start | bytes 491528 | tf_op jit(solution)/shard_map/ppermute | solution.py:94
  11.4 5.6 %copy-start.1 = (f32[80,4,128]{2,1,0:T(4,128)}, f32[80,4,128]{2,1,0:T(4,128)S(1)}, u32[]{:S(2)}) copy-start(f32[80,4,128]{2,1,0:T(4,128)S(1)} %collective-permute-done.xn_ref.refs_3_.refs_5_.refs_7_) | copy-start | bytes 491524
  17.1 0.7 copy-start.2
  21.8 4.9 %collective-permute-start.2 = (f32[3,72,128]{2,1,0:T(8,128)}, f32[3,72,128]{2,1,0:T(8,128)S(1)}, u32[]{:S(2)}, u32[]{:S(2)}) collective-permute-start(f32[3,72,128]{2,1,0:T(8,128)} %get-tuple-element.9), channel_id=1, source_target_pairs={{1,0},{2,1},{3,2},{4,3},{5,4},{6,5},{7,6},{0,7},{9,8},{10,9},{11,1... | collective-permute-start | bytes 331784 | tf_op jit(solution)/shard_map/ppermute | solution.py:97
  24.1 5.6 %collective-permute-start.3 = (f32[3,72,128]{2,1,0:T(8,128)}, f32[3,72,128]{2,1,0:T(8,128)S(1)}, u32[]{:S(2)}, u32[]{:S(2)}) collective-permute-start(f32[3,72,128]{2,1,0:T(8,128)} %get-tuple-element.10), channel_id=1, source_target_pairs={{0,1},{1,2},{2,3},{3,4},{4,5},{5,6},{6,7},{7,0},{8,9},{9,10},{10,1... | collective-permute-start | bytes 331784 | tf_op jit(solution)/shard_map/ppermute | solution.py:98
  26.7 3.0 %copy-start.3 = (f32[3,72,128]{2,1,0:T(8,128)}, f32[3,72,128]{2,1,0:T(8,128)S(1)}, u32[]{:S(2)}) copy-start(f32[3,72,128]{2,1,0:T(8,128)S(1)} %collective-permute-done.2.refs_9_) | copy-start | bytes 331780
  29.7 0.7 copy-start.4
  69.3 3.9 %collective-permute-start.4 = (f32[40,40]{1,0:T(8,128)S(1)}, f32[40,40]{1,0:T(8,128)S(1)}, u32[]{:S(2)}, u32[]{:S(2)}) collective-permute-start(f32[40,40]{1,0:T(8,128)S(1)} %fusion.2), channel_id=1, source_target_pairs={{0,32},{8,40},{16,48},{24,56},{32,0},{40,8},{48,16},{56,24},{64,96... | collective-permute-start | bytes 19208 | tf_op jit(solution)/shard_map/ppermute | solution.py:136
  73.2 5.0 %collective-permute-start.5 = (f32[40,40]{1,0:T(8,128)S(1)}, f32[40,40]{1,0:T(8,128)S(1)}, u32[]{:S(2)}, u32[]{:S(2)}) collective-permute-start(f32[40,40]{1,0:T(8,128)S(1)} %add.42), channel_id=1, source_target_pairs={{0,96},{8,104},{16,112},{24,120},{32,64},{40,72},{48,80},{56,88},{... | collective-permute-start | bytes 19208 | tf_op jit(solution)/shard_map/ppermute | solution.py:136
  78.2 3.8 %collective-permute-start.6 = (f32[40,40]{1,0:T(8,128)S(1)}, f32[40,40]{1,0:T(8,128)S(1)}, u32[]{:S(2)}, u32[]{:S(2)}) collective-permute-start(f32[40,40]{1,0:T(8,128)S(1)} %add.43), channel_id=1, source_target_pairs={{0,8},{8,0},{16,24},{24,16},{32,40},{40,32},{48,56},{56,48},{64,72... | collective-permute-start | bytes 19208 | tf_op jit(solution)/shard_map/ppermute | solution.py:136
  82.0 5.0 %collective-permute-start.7 = (f32[40,40]{1,0:T(8,128)S(1)}, f32[40,40]{1,0:T(8,128)S(1)}, u32[]{:S(2)}, u32[]{:S(2)}) collective-permute-start(f32[40,40]{1,0:T(8,128)S(1)} %add.44), channel_id=1, source_target_pairs={{0,24},{8,16},{16,8},{24,0},{32,56},{40,48},{48,40},{56,32},{64,88... | collective-permute-start | bytes 19208 | tf_op jit(solution)/shard_map/ppermute | solution.py:136
  87.0 1.2 collective-permute-start.8
  88.2 3.8 %collective-permute-start.9 = (f32[40,40]{1,0:T(8,128)S(1)}, f32[40,40]{1,0:T(8,128)S(1)}, u32[]{:S(2)}, u32[]{:S(2)}) collective-permute-start(f32[40,40]{1,0:T(8,128)S(1)} %add.46), channel_id=1, source_target_pairs={{0,2},{1,3},{2,0},{3,1},{4,6},{5,7},{6,4},{7,5},{8,10},{9,11},{10,... | collective-permute-start | bytes 19208 | tf_op jit(solution)/shard_map/ppermute | solution.py:136
  92.0 5.0 %collective-permute-start.10 = (f32[40,40]{1,0:T(8,128)S(1)}, f32[40,40]{1,0:T(8,128)S(1)}, u32[]{:S(2)}, u32[]{:S(2)}) collective-permute-start(f32[40,40]{1,0:T(8,128)S(1)} %add.47), channel_id=1, source_target_pairs={{0,6},{1,7},{2,4},{3,5},{4,2},{5,3},{6,0},{7,1},{8,14},{9,15},{10,... | collective-permute-start | bytes 19208 | tf_op jit(solution)/shard_map/ppermute | solution.py:136
  114.5 4.2 %copy-start = (f32[40,65536]{1,0:T(8,128)}, f32[40,65536]{1,0:T(8,128)S(1)}, u32[]{:S(2)}) copy-start(f32[40,65536]{1,0:T(8,128)S(1)} %fusion) | copy-start | bytes 31457284
  118.7 3.9 %collective-permute-start.11 = (f32[40,40]{1,0:T(8,128)S(1)}, f32[40,40]{1,0:T(8,128)S(1)}, u32[]{:S(2)}, u32[]{:S(2)}) collective-permute-start(f32[40,40]{1,0:T(8,128)S(1)} %fusion.7), channel_id=1, source_target_pairs={{0,32},{8,40},{16,48},{24,56},{32,0},{40,8},{48,16},{56,24},{64,96... | collective-permute-start | bytes 19208 | tf_op jit(solution)/shard_map/ppermute | solution.py:136
  122.6 5.0 %collective-permute-start.12 = (f32[40,40]{1,0:T(8,128)S(1)}, f32[40,40]{1,0:T(8,128)S(1)}, u32[]{:S(2)}, u32[]{:S(2)}) collective-permute-start(f32[40,40]{1,0:T(8,128)S(1)} %add.49), channel_id=1, source_target_pairs={{0,96},{8,104},{16,112},{24,120},{32,64},{40,72},{48,80},{56,88},{... | collective-permute-start | bytes 19208 | tf_op jit(solution)/shard_map/ppermute | solution.py:136
  127.6 3.8 %collective-permute-start.13 = (f32[40,40]{1,0:T(8,128)S(1)}, f32[40,40]{1,0:T(8,128)S(1)}, u32[]{:S(2)}, u32[]{:S(2)}) collective-permute-start(f32[40,40]{1,0:T(8,128)S(1)} %add.50), channel_id=1, source_target_pairs={{0,8},{8,0},{16,24},{24,16},{32,40},{40,32},{48,56},{56,48},{64,72... | collective-permute-start | bytes 19208 | tf_op jit(solution)/shard_map/ppermute | solution.py:136
  131.4 5.0 %collective-permute-start.14 = (f32[40,40]{1,0:T(8,128)S(1)}, f32[40,40]{1,0:T(8,128)S(1)}, u32[]{:S(2)}, u32[]{:S(2)}) collective-permute-start(f32[40,40]{1,0:T(8,128)S(1)} %add.51), channel_id=1, source_target_pairs={{0,24},{8,16},{16,8},{24,0},{32,56},{40,48},{48,40},{56,32},{64,88... | collective-permute-start | bytes 19208 | tf_op jit(solution)/shard_map/ppermute | solution.py:136
  136.4 1.2 collective-permute-start.15
  137.6 3.8 %collective-permute-start.16 = (f32[40,40]{1,0:T(8,128)S(1)}, f32[40,40]{1,0:T(8,128)S(1)}, u32[]{:S(2)}, u32[]{:S(2)}) collective-permute-start(f32[40,40]{1,0:T(8,128)S(1)} %add.53), channel_id=1, source_target_pairs={{0,2},{1,3},{2,0},{3,1},{4,6},{5,7},{6,4},{7,5},{8,10},{9,11},{10,... | collective-permute-start | bytes 19208 | tf_op jit(solution)/shard_map/ppermute | solution.py:136
  141.4 5.0 %collective-permute-start.17 = (f32[40,40]{1,0:T(8,128)S(1)}, f32[40,40]{1,0:T(8,128)S(1)}, u32[]{:S(2)}, u32[]{:S(2)}) collective-permute-start(f32[40,40]{1,0:T(8,128)S(1)} %add.54), channel_id=1, source_target_pairs={{0,6},{1,7},{2,4},{3,5},{4,2},{5,3},{6,0},{7,1},{8,14},{9,15},{10,... | collective-permute-start | bytes 19208 | tf_op jit(solution)/shard_map/ppermute | solution.py:136
  159.5 6.0 %copy-start.5 = (f32[40,40]{1,0:T(8,128)S(1)}, f32[40,40]{1,0:T(8,128)}, u32[]{:S(2)}) copy-start(f32[40,40]{1,0:T(8,128)} %get-tuple-element.8) | copy-start | bytes 19204
  159.5 6.0 %copy-start.6 = (f32[40,40]{1,0:T(8,128)S(1)}, f32[40,40]{1,0:T(8,128)}, u32[]{:S(2)}) copy-start(f32[40,40]{1,0:T(8,128)} %get-tuple-element.13) | copy-start | bytes 19204
